TPU v7x, 256 devices: a whole 4x4x8 slice. The times are simulated.
256 devices in a mesh: dp: 16 (over y, x), ctx: 16 (over z, core).
Axes of the slice: x: 4, y: 4, z: 8, core: 2. Of those that a mesh axis runs over, the one named last changes fastest.
Arguments:
- query_heads: bfloat16 [65536, 16, 128], P(('dp', 'ctx')), parts along dimension 0, may hold values from -64 to 64
- key_heads: bfloat16 [65536, 8, 128], P(('dp', 'ctx')), parts along dimension 0, may hold values from -64 to 64
- value_heads: bfloat16 [65536, 8, 128], P(('dp', 'ctx')), parts along dimension 0, may hold values from -6 to 6
- grad_out: bfloat16 [65536, 16, 128], P(('dp', 'ctx')), parts along dimension 0, may hold values from -6 to 6
- doc_ids: int32 [65536], P('dp'), parts along dimension 0, may hold values from 0 to 4, as said below
Outputs:
- attended: bfloat16 [65536, 16, 128], P(('dp', 'ctx')), parts along dimension 0
- grad_query: bfloat16 [65536, 16, 128], P(('dp', 'ctx')), parts along dimension 0
- grad_key: bfloat16 [65536, 8, 128], P(('dp', 'ctx')), parts along dimension 0
- grad_value: bfloat16 [65536, 8, 128], P(('dp', 'ctx')), parts along dimension 0
There are 16 independent parts, one for each index of `dp`. A program takes and returns all parts, laid end to end along the dimension named above; each array names one. Nothing has to cross between parts.
Inputs may be any that keep to these rules, and one draw needn't show every extreme that they name: doc_ids starts at 0 and never falls; within each aligned block of 1024 tokens it rises by one exactly once, never at the block's first token.
All inputs are finite; a program needn't handle non-finite values.
Results may differ from a plain program's by a relative error of at most 0.012.
Values may be sent and summed in bfloat16 or wider, within the bound.
No kernel may reach another device: no remote copies, remote signals or barrier semaphores. Data moves between devices by JAX's collectives and lax.ppermute only.
A program may use at most 64 MiB of HBM per device.

v0:
```python
import jax
import jax.numpy as jnp
from jax import lax
from jax.sharding import PartitionSpec as P

WINDOW = 1024


QUERY_SCALE = 168.0 ** (-0.5)


def from_behind(block, axis, distance):
    devices = range(lax.axis_size(axis))
    route = [(i - distance, i) for i in devices if i - distance in devices]
    return lax.ppermute(block, axis, route)


def group_grads(q_group, k_group, v_group, g_group, allowed):
    scores = QUERY_SCALE * jnp.einsum(
        "rad,cd->arc", q_group, k_group, preferred_element_type=jnp.float32
    )
    masked = jnp.where(allowed[None], scores, -jnp.inf)
    row_max = jnp.max(masked, axis=-1, keepdims=True)
    unnorm = jnp.exp(masked - row_max)
    weights = unnorm / jnp.sum(unnorm, axis=-1, keepdims=True)
    weights_b = weights.astype(jnp.bfloat16)
    attended = jnp.einsum(
        "arc,cd->rad", weights_b, v_group, preferred_element_type=jnp.float32
    ).astype(jnp.bfloat16)
    row_dot = jnp.sum(g_group.astype(jnp.float32) * attended.astype(jnp.float32), axis=-1)
    dprob = jnp.einsum("rad,cd->arc", g_group, v_group, preferred_element_type=jnp.float32)
    dscore = (weights * (dprob - jnp.transpose(row_dot)[..., None])).astype(jnp.bfloat16)
    grad_q = (
        QUERY_SCALE * jnp.einsum("arc,cd->rad", dscore, k_group, preferred_element_type=jnp.float32)
    ).astype(jnp.bfloat16)
    grad_k = (
        QUERY_SCALE * jnp.einsum("arc,rad->cd", dscore, q_group, preferred_element_type=jnp.float32)
    ).astype(jnp.bfloat16)
    grad_v = jnp.einsum(
        "arc,rad->cd", weights_b, g_group, preferred_element_type=jnp.float32
    ).astype(jnp.bfloat16)
    return (attended, grad_q, grad_k, grad_v)


def body(query_heads, key_heads, value_heads, grad_out, doc_ids):
    row_count = query_heads.shape[0]
    groups = key_heads.shape[1]
    head_size = key_heads.shape[2]
    reach = WINDOW // row_count
    piece_pos = lax.axis_index("ctx")
    earlier = []
    for offset in range(reach, 0, -1):
        earlier.append(from_behind((key_heads, value_heads), "ctx", offset))
    k_window = jnp.concatenate([pair[0] for pair in earlier] + [key_heads], 0)
    v_window = jnp.concatenate([pair[1] for pair in earlier] + [value_heads], 0)
    pad_docs = jnp.concatenate([jnp.full((WINDOW,), -1, jnp.int32), doc_ids], 0)
    first_row = piece_pos * row_count
    q_docs = lax.dynamic_slice_in_dim(doc_ids, first_row, row_count, 0)
    k_docs = lax.dynamic_slice_in_dim(pad_docs, first_row, WINDOW + row_count, 0)
    q_index = jnp.arange(row_count)[:, None]
    k_index = jnp.arange(WINDOW + row_count)[None, :]
    allowed = (
        (q_docs[:, None] == k_docs[None, :]) & (k_index > q_index) & (k_index <= q_index + WINDOW)
    )
    q_major = jnp.transpose(query_heads.reshape(row_count, groups, 2, head_size), (1, 0, 2, 3))
    g_major = jnp.transpose(grad_out.reshape(row_count, groups, 2, head_size), (1, 0, 2, 3))
    k_major = jnp.transpose(k_window, (1, 0, 2))
    v_major = jnp.transpose(v_window, (1, 0, 2))

    def per_group(operands):
        return group_grads(operands[0], operands[1], operands[2], operands[3], allowed)

    attended, grad_q, key_terms, value_terms = lax.map(
        per_group, (q_major, k_major, v_major, g_major)
    )
    attended = jnp.transpose(attended, (1, 0, 2, 3)).reshape(query_heads.shape)
    grad_q = jnp.transpose(grad_q, (1, 0, 2, 3)).reshape(query_heads.shape)
    key_terms = jnp.transpose(key_terms, (1, 0, 2))
    value_terms = jnp.transpose(value_terms, (1, 0, 2))
    key_terms, value_terms = lax.optimization_barrier((key_terms, value_terms))

    def term_for(offset):
        lower = (reach - offset) * row_count
        return (key_terms[lower : lower + row_count], value_terms[lower : lower + row_count])

    own_k, own_v = term_for(0)
    total_k = own_k.astype(jnp.float32)
    total_v = own_v.astype(jnp.float32)
    for offset in range(1, reach + 1):
        send_k, send_v = term_for(offset)
        back_k, back_v = from_behind((send_k, send_v), "ctx", -offset)
        total_k = total_k + back_k.astype(jnp.float32)
        total_v = total_v + back_v.astype(jnp.float32)
    return (attended, grad_q, total_k.astype(jnp.bfloat16), total_v.astype(jnp.bfloat16))


def solution(mesh):
    placed = (
        P(("dp", "ctx"), None, None),
        P(("dp", "ctx"), None, None),
        P(("dp", "ctx"), None, None),
        P(("dp", "ctx"), None, None),
        P("dp"),
    )
    return jax.shard_map(
        body,
        mesh=mesh,
        in_specs=placed,
        out_specs=(
            P(("dp", "ctx"), None, None),
            P(("dp", "ctx"), None, None),
            P(("dp", "ctx"), None, None),
            P(("dp", "ctx"), None, None),
        ),
        check_vma=False,
    )
```

profile of v0, /device:TPU:100, one launch (start us, length us, event | category | flops | bytes accessed | tf_op | source)
XLA Modules:
  0.0 366.0 jit_solution(3155375957293777799)
XLA Ops:
  2.1 5.5 %collective-permute-start = (bf16[256,8,128]{0,2,1:T(8,128)(2,1)S(1)}, bf16[256,8,128]{0,2,1:T(8,128)(2,1)}, u32[]{:S(2)}, u32[]{:S(2)}) collective-permute-start(bf16[256,8,128]{0,2,1:T(8,128)(2,1)S(1)} %copy.15), channel_id=1, source_target_pairs={{0,4},{1,5},{2,6},{3,7},{4,8},{5,9},{6,10},{7,11},{8,12},{9,13},{1... | collective-permute-start | bytes 1572872 | tf_op jit(solution)/shard_map/ppermute | solution.py:15
  9.7 2.9 collective-permute-start.2
  12.7 2.3 collective-permute-start.3
  16.9 2.5 collective-permute-start.7
  22.4 12.9 %collective-permute-done = bf16[256,8,128]{0,2,1:T(8,128)(2,1)} collective-permute-done((bf16[256,8,128]{0,2,1:T(8,128)(2,1)S(1)}, bf16[256,8,128]{0,2,1:T(8,128)(2,1)}, u32[]{:S(2)}, u32[]{:S(2)}) %collective-permute-start) | collective-permute-done | bytes 524320 | tf_op jit(solution)/shard_map/ppermute | solution.py:15
  35.3 4.2 %collective-permute-start.4 = (bf16[256,8,128]{2,0,1:T(8,128)(2,1)}, bf16[256,8,128]{2,0,1:T(8,128)(2,1)S(1)}, u32[]{:S(2)}, u32[]{:S(2)}) collective-permute-start(bf16[256,8,128]{2,0,1:T(8,128)(2,1)} %copy.20), channel_id=1, source_target_pairs={{0,4},{1,5},{2,6},{3,7},{4,8},{5,9},{6,10},{7,11},{8,12},{9,13},{1... | collective-permute-start | bytes 1572872 | tf_op jit(solution)/shard_map/ppermute | solution.py:15
  40.6 10.0 %collective-permute-done.1 = bf16[256,8,128]{0,2,1:T(8,128)(2,1)} collective-permute-done((bf16[256,8,128]{0,2,1:T(8,128)(2,1)S(1)}, bf16[256,8,128]{0,2,1:T(8,128)(2,1)}, u32[]{:S(2)}, u32[]{:S(2)}) %collective-permute-start.1) | collective-permute-done | bytes 524320 | tf_op jit(solution)/shard_map/ppermute | solution.py:15
  53.7 7.1 %collective-permute-done.2 = bf16[256,8,128]{0,2,1:T(8,128)(2,1)} collective-permute-done((bf16[256,8,128]{0,2,1:T(8,128)(2,1)S(1)}, bf16[256,8,128]{0,2,1:T(8,128)(2,1)}, u32[]{:S(2)}, u32[]{:S(2)}) %collective-permute-start.2) | collective-permute-done | bytes 524320 | tf_op jit(solution)/shard_map/ppermute | solution.py:15
  60.7 3.6 collective-permute-start.6
  65.4 4.3 %collective-permute-done.3 = bf16[256,8,128]{0,2,1:T(8,128)(2,1)} collective-permute-done((bf16[256,8,128]{0,2,1:T(8,128)(2,1)S(1)}, bf16[256,8,128]{0,2,1:T(8,128)(2,1)}, u32[]{:S(2)}, u32[]{:S(2)}) %collective-permute-start.3) | collective-permute-done | bytes 524320 | tf_op jit(solution)/shard_map/ppermute | solution.py:15
  70.9 14.8 %collective-permute-done.4 = bf16[256,8,128]{2,0,1:T(8,128)(2,1)S(1)} collective-permute-done((bf16[256,8,128]{2,0,1:T(8,128)(2,1)}, bf16[256,8,128]{2,0,1:T(8,128)(2,1)S(1)}, u32[]{:S(2)}, u32[]{:S(2)}) %collective-permute-start.4) | collective-permute-done | bytes 524320 | tf_op jit(solution)/shard_map/ppermute | solution.py:15
  85.7 28.1 %collective-permute-done.5 = bf16[256,8,128]{2,0,1:T(8,128)(2,1)S(1)} collective-permute-done((bf16[256,8,128]{2,0,1:T(8,128)(2,1)}, bf16[256,8,128]{2,0,1:T(8,128)(2,1)S(1)}, u32[]{:S(2)}, u32[]{:S(2)}) %collective-permute-start.5) | collective-permute-done | bytes 524320 | tf_op jit(solution)/shard_map/ppermute | solution.py:15
  115.7 107.3 %while.17 = (s32[]{:T(128)}, bf16[8,256,2,128]{1,3,2,0:T(8,128)(2,1)}, bf16[8,256,2,128]{1,3,2,0:T(8,128)(2,1)}, bf16[8,1280,128]{2,1,0:T(8,128)(2,1)}, bf16[8,1...) while((s32[]{:T(128)}, ...), condition=%wide.region_4.5_spmd.clone, body=%wide.region_0.4_spmd.clone.sunk | while | flops 1015776000 | bytes 19553416 | solution.py:73
  127.0 2.2 fusion.106
  140.4 2.2 fusion.106
  153.8 2.2 fusion.106
  194.0 2.2 fusion.106
  220.8 2.2 fusion.106
  223.0 13.2 %copy_bitcast_fusion = (bf16[1280,8,128]{2,1,0:T(8,128)(2,1)S(1)}, bf16[1280,8,128]{2,1,0:T(8,128)(2,1)S(1)}) fusion(bf16[8,1280,128]{2,1,0:T(8,128)(2,1)} %get-tuple-element.64, bf16[8,1280,128]{2,1,0:T(8,128)(2,1)} %get-tuple-element.63), kind=kLoop, calls=%fused_computation.61 | loop fusion | bytes 10485760 | tf_op jit(solution)/shard_map/transpose | solution.py:79
  237.3 8.8 %collective-permute-start.8 = (bf16[256,8,128]{2,1,0:T(8,128)(2,1)S(1)}, bf16[256,8,128]{2,1,0:T(8,128)(2,1)S(1)}, u32[]{:S(2)}, u32[]{:S(2)}) collective-permute-start(bf16[256,8,128]{2,1,0:T(8,128)(2,1)S(1)} %get-tuple-element.128), channel_id=1, source_target_pairs={{1,0},{2,1},{3,2},{4,3},{5,4},{6,5},{7,6},{8,7},{9,8},{10,9},{11,1... | collective-permute-start | bytes 1572872 | tf_op jit(solution)/shard_map/ppermute | solution.py:15
  255.1 4.3 %collective-permute-done.8 = bf16[256,8,128]{2,1,0:T(8,128)(2,1)S(1)} collective-permute-done((bf16[256,8,128]{2,1,0:T(8,128)(2,1)S(1)}, bf16[256,8,128]{2,1,0:T(8,128)(2,1)S(1)}, u32[]{:S(2)}, u32[]{:S(2)}) %collective-permute-start.8) | collective-permute-done | bytes 524320 | tf_op jit(solution)/shard_map/ppermute | solution.py:15
  261.4 19.1 %collective-permute-done.11 = bf16[256,8,128]{2,1,0:T(8,128)(2,1)} collective-permute-done((bf16[256,8,128]{2,1,0:T(8,128)(2,1)S(1)}, bf16[256,8,128]{2,1,0:T(8,128)(2,1)}, u32[]{:S(2)}, u32[]{:S(2)}) %collective-permute-start.11) | collective-permute-done | bytes 524320 | tf_op jit(solution)/shard_map/ppermute | solution.py:15
  282.4 10.4 %collective-permute-done.10 = bf16[256,8,128]{2,1,0:T(8,128)(2,1)} collective-permute-done((bf16[256,8,128]{2,1,0:T(8,128)(2,1)S(1)}, bf16[256,8,128]{2,1,0:T(8,128)(2,1)}, u32[]{:S(2)}, u32[]{:S(2)}) %collective-permute-start.10) | collective-permute-done | bytes 524320 | tf_op jit(solution)/shard_map/ppermute | solution.py:15
  294.7 3.7 %copy.27 = bf16[256,8,2,128]{3,2,1,0:T(2,128)(2,1)} copy(bf16[256,8,2,128]{0,3,2,1:T(8,128)(2,1)} %bitcast.169) | data formatting | bytes 2097152 | tf_op jit(solution)/shard_map/transpose | solution.py:76
  298.4 3.7 copy.28
  302.0 15.7 %collective-permute-done.9 = bf16[256,8,128]{2,1,0:T(8,128)(2,1)} collective-permute-done((bf16[256,8,128]{2,1,0:T(8,128)(2,1)}, bf16[256,8,128]{2,1,0:T(8,128)(2,1)}, u32[]{:S(2)}, u32[]{:S(2)}) %collective-permute-start.9) | collective-permute-done | bytes 524320 | tf_op jit(solution)/shard_map/ppermute | solution.py:15
  317.7 2.6 add_convert_fusion.1
  320.3 3.8 %collective-permute-done.12 = bf16[256,8,128]{2,1,0:T(8,128)(2,1)} collective-permute-done((bf16[256,8,128]{2,1,0:T(8,128)(2,1)}, bf16[256,8,128]{2,1,0:T(8,128)(2,1)}, u32[]{:S(2)}, u32[]{:S(2)}) %collective-permute-start.12) | collective-permute-done | bytes 524320 | tf_op jit(solution)/shard_map/ppermute | solution.py:15
  324.1 16.9 %collective-permute-done.15 = bf16[256,8,128]{2,1,0:T(8,128)(2,1)} collective-permute-done((bf16[256,8,128]{2,1,0:T(8,128)(2,1)}, bf16[256,8,128]{2,1,0:T(8,128)(2,1)}, u32[]{:S(2)}, u32[]{:S(2)}) %collective-permute-start.15) | collective-permute-done | bytes 524320 | tf_op jit(solution)/shard_map/ppermute | solution.py:15
  341.0 8.2 %collective-permute-done.14 = bf16[256,8,128]{2,1,0:T(8,128)(2,1)} collective-permute-done((bf16[256,8,128]{2,1,0:T(8,128)(2,1)}, bf16[256,8,128]{2,1,0:T(8,128)(2,1)}, u32[]{:S(2)}, u32[]{:S(2)}) %collective-permute-start.14) | collective-permute-done | bytes 524320 | tf_op jit(solution)/shard_map/ppermute | solution.py:15
  349.2 14.1 %collective-permute-done.13 = bf16[256,8,128]{2,1,0:T(8,128)(2,1)} collective-permute-done((bf16[256,8,128]{2,1,0:T(8,128)(2,1)}, bf16[256,8,128]{2,1,0:T(8,128)(2,1)}, u32[]{:S(2)}, u32[]{:S(2)}) %collective-permute-start.13) | collective-permute-done | bytes 524320 | tf_op jit(solution)/shard_map/ppermute | solution.py:15
  363.3 2.6 add_convert_fusion
  (115 shorter events, 128.6 us)
Async XLA Ops:
  0.6 18.8 %copy-start.4 = (bf16[256,16,128]{2,1,0:T(8,128)(2,1)S(1)}, bf16[256,16,128]{2,1,0:T(8,128)(2,1)}, u32[]{:S(2)}) copy-start(bf16[256,16,128]{2,1,0:T(8,128)(2,1)} %param.7) | copy-start | bytes 3145732
  0.6 20.0 %copy-start.5 = (bf16[256,16,128]{2,1,0:T(8,128)(2,1)S(1)}, bf16[256,16,128]{2,1,0:T(8,128)(2,1)}, u32[]{:S(2)}) copy-start(bf16[256,16,128]{2,1,0:T(8,128)(2,1)} %param.10) | copy-start | bytes 3145732
  2.1 20.1 %copy-start.6 = (s32[4096]{0:T(1024)S(1)}, s32[4096]{0:T(1024)}, u32[]{:S(2)}) copy-start(s32[4096]{0:T(1024)} %param.11) | copy-start | bytes 49156
  2.1 33.2 %collective-permute-start = (bf16[256,8,128]{0,2,1:T(8,128)(2,1)S(1)}, bf16[256,8,128]{0,2,1:T(8,128)(2,1)}, u32[]{:S(2)}, u32[]{:S(2)}) collective-permute-start(bf16[256,8,128]{0,2,1:T(8,128)(2,1)S(1)} %copy.15), channel_id=1, source_target_pairs={{0,4},{1,5},{2,6},{3,7},{4,8},{5,9},{6,10},{7,11},{8,12},{9,13},{1... | collective-permute-start | bytes 1572872 | tf_op jit(solution)/shard_map/ppermute | solution.py:15
  7.6 43.0 %collective-permute-start.1 = (bf16[256,8,128]{0,2,1:T(8,128)(2,1)S(1)}, bf16[256,8,128]{0,2,1:T(8,128)(2,1)}, u32[]{:S(2)}, u32[]{:S(2)}) collective-permute-start(bf16[256,8,128]{0,2,1:T(8,128)(2,1)S(1)} %copy.15), channel_id=1, source_target_pairs={{0,3},{1,4},{2,5},{3,6},{4,7},{5,8},{6,9},{7,10},{8,11},{9,12},{10... | collective-permute-start | bytes 1572872 | tf_op jit(solution)/shard_map/ppermute | solution.py:15
  9.7 51.0 %collective-permute-start.2 = (bf16[256,8,128]{0,2,1:T(8,128)(2,1)S(1)}, bf16[256,8,128]{0,2,1:T(8,128)(2,1)}, u32[]{:S(2)}, u32[]{:S(2)}) collective-permute-start(bf16[256,8,128]{0,2,1:T(8,128)(2,1)S(1)} %copy.15), channel_id=1, source_target_pairs={{0,2},{1,3},{2,4},{3,5},{4,6},{5,7},{6,8},{7,9},{8,10},{9,11},{10,... | collective-permute-start | bytes 1572872 | tf_op jit(solution)/shard_map/ppermute | solution.py:15
  12.7 57.1 %collective-permute-start.3 = (bf16[256,8,128]{0,2,1:T(8,128)(2,1)S(1)}, bf16[256,8,128]{0,2,1:T(8,128)(2,1)}, u32[]{:S(2)}, u32[]{:S(2)}) collective-permute-start(bf16[256,8,128]{0,2,1:T(8,128)(2,1)S(1)} %copy.15), channel_id=1, source_target_pairs={{0,1},{1,2},{2,3},{3,4},{4,5},{5,6},{6,7},{7,8},{8,9},{9,10},{10,1... | collective-permute-start | bytes 1572872 | tf_op jit(solution)/shard_map/ppermute | solution.py:15
  16.9 97.1 %collective-permute-start.7 = (bf16[256,8,128]{2,0,1:T(8,128)(2,1)}, bf16[256,8,128]{2,0,1:T(8,128)(2,1)S(1)}, u32[]{:S(2)}, u32[]{:S(2)}) collective-permute-start(bf16[256,8,128]{2,0,1:T(8,128)(2,1)} %copy.20), channel_id=1, source_target_pairs={{0,1},{1,2},{2,3},{3,4},{4,5},{5,6},{6,7},{7,8},{8,9},{9,10},{10,1... | collective-permute-start | bytes 1572872 | tf_op jit(solution)/shard_map/ppermute | solution.py:15
  35.3 50.4 %collective-permute-start.4 = (bf16[256,8,128]{2,0,1:T(8,128)(2,1)}, bf16[256,8,128]{2,0,1:T(8,128)(2,1)S(1)}, u32[]{:S(2)}, u32[]{:S(2)}) collective-permute-start(bf16[256,8,128]{2,0,1:T(8,128)(2,1)} %copy.20), channel_id=1, source_target_pairs={{0,4},{1,5},{2,6},{3,7},{4,8},{5,9},{6,10},{7,11},{8,12},{9,13},{1... | collective-permute-start | bytes 1572872 | tf_op jit(solution)/shard_map/ppermute | solution.py:15
  50.7 63.1 %collective-permute-start.5 = (bf16[256,8,128]{2,0,1:T(8,128)(2,1)}, bf16[256,8,128]{2,0,1:T(8,128)(2,1)S(1)}, u32[]{:S(2)}, u32[]{:S(2)}) collective-permute-start(bf16[256,8,128]{2,0,1:T(8,128)(2,1)} %copy.20), channel_id=1, source_target_pairs={{0,3},{1,4},{2,5},{3,6},{4,7},{5,8},{6,9},{7,10},{8,11},{9,12},{10... | collective-permute-start | bytes 1572872 | tf_op jit(solution)/shard_map/ppermute | solution.py:15
  60.7 53.1 %collective-permute-start.6 = (bf16[256,8,128]{2,0,1:T(8,128)(2,1)}, bf16[256,8,128]{2,0,1:T(8,128)(2,1)S(1)}, u32[]{:S(2)}, u32[]{:S(2)}) collective-permute-start(bf16[256,8,128]{2,0,1:T(8,128)(2,1)} %copy.20), channel_id=1, source_target_pairs={{0,2},{1,3},{2,4},{3,5},{4,6},{5,7},{6,8},{7,9},{8,10},{9,11},{10,... | collective-permute-start | bytes 1572872 | tf_op jit(solution)/shard_map/ppermute | solution.py:15
  70.8 43.2 %copy-start.1 = (bf16[256,8,128]{2,1,0:T(8,128)(2,1)S(1)}, bf16[256,8,128]{2,1,0:T(8,128)(2,1)}, u32[]{:S(2)}) copy-start(bf16[256,8,128]{2,1,0:T(8,128)(2,1)} %param.8) | copy-start | bytes 1572868
  70.9 43.3 %copy-start.2 = (bf16[1280,8,128]{0,2,1:T(8,128)(2,1)}, bf16[1280,8,128]{0,2,1:T(8,128)(2,1)S(1)}, u32[]{:S(2)}) copy-start(bf16[1280,8,128]{0,2,1:T(8,128)(2,1)S(1)} %constant_dynamic-update-slice_fusion) | copy-start | bytes 7864324
  114.2 1.5 copy-start.3
  236.2 17.0 %copy-start = (bf16[1280,8,128]{2,1,0:T(8,128)(2,1)}, bf16[1280,8,128]{2,1,0:T(8,128)(2,1)S(1)}, u32[]{:S(2)}) copy-start(bf16[1280,8,128]{2,1,0:T(8,128)(2,1)S(1)} %get-tuple-element.65) | copy-start | bytes 7864324
  237.3 22.1 %collective-permute-start.8 = (bf16[256,8,128]{2,1,0:T(8,128)(2,1)S(1)}, bf16[256,8,128]{2,1,0:T(8,128)(2,1)S(1)}, u32[]{:S(2)}, u32[]{:S(2)}) collective-permute-start(bf16[256,8,128]{2,1,0:T(8,128)(2,1)S(1)} %get-tuple-element.128), channel_id=1, source_target_pairs={{1,0},{2,1},{3,2},{4,3},{5,4},{6,5},{7,6},{8,7},{9,8},{10,9},{11,1... | collective-permute-start | bytes 1572872 | tf_op jit(solution)/shard_map/ppermute | solution.py:15
  246.1 34.4 %collective-permute-start.11 = (bf16[256,8,128]{2,1,0:T(8,128)(2,1)S(1)}, bf16[256,8,128]{2,1,0:T(8,128)(2,1)}, u32[]{:S(2)}, u32[]{:S(2)}) collective-permute-start(bf16[256,8,128]{2,1,0:T(8,128)(2,1)S(1)} %get-tuple-element.129), channel_id=1, source_target_pairs={{4,0},{5,1},{6,2},{7,3},{8,4},{9,5},{10,6},{11,7},{12,8},{13,9},{1... | collective-permute-start | bytes 1572872 | tf_op jit(solution)/shard_map/ppermute | solution.py:15
  248.0 44.8 %collective-permute-start.10 = (bf16[256,8,128]{2,1,0:T(8,128)(2,1)S(1)}, bf16[256,8,128]{2,1,0:T(8,128)(2,1)}, u32[]{:S(2)}, u32[]{:S(2)}) collective-permute-start(bf16[256,8,128]{2,1,0:T(8,128)(2,1)S(1)} %get-tuple-element.130), channel_id=1, source_target_pairs={{3,0},{4,1},{5,2},{6,3},{7,4},{8,5},{9,6},{10,7},{11,8},{12,9},{13... | collective-permute-start | bytes 1572872 | tf_op jit(solution)/shard_map/ppermute | solution.py:15
  249.9 67.8 %collective-permute-start.9 = (bf16[256,8,128]{2,1,0:T(8,128)(2,1)}, bf16[256,8,128]{2,1,0:T(8,128)(2,1)}, u32[]{:S(2)}, u32[]{:S(2)}) collective-permute-start(bf16[256,8,128]{2,1,0:T(8,128)(2,1)} %get-tuple-element.131), channel_id=1, source_target_pairs={{2,0},{3,1},{4,2},{5,3},{6,4},{7,5},{8,6},{9,7},{10,8},{11,9},{12,... | collective-permute-start | bytes 1572872 | tf_op jit(solution)/shard_map/ppermute | solution.py:15
  253.2 70.9 %collective-permute-start.12 = (bf16[256,8,128]{2,1,0:T(8,128)(2,1)}, bf16[256,8,128]{2,1,0:T(8,128)(2,1)}, u32[]{:S(2)}, u32[]{:S(2)}) collective-permute-start(bf16[256,8,128]{2,1,0:T(8,128)(2,1)} %get-tuple-element.124), channel_id=1, source_target_pairs={{1,0},{2,1},{3,2},{4,3},{5,4},{6,5},{7,6},{8,7},{9,8},{10,9},{11,1... | collective-permute-start | bytes 1572872 | tf_op jit(solution)/shard_map/ppermute | solution.py:15
  259.4 81.6 %collective-permute-start.15 = (bf16[256,8,128]{2,1,0:T(8,128)(2,1)}, bf16[256,8,128]{2,1,0:T(8,128)(2,1)}, u32[]{:S(2)}, u32[]{:S(2)}) collective-permute-start(bf16[256,8,128]{2,1,0:T(8,128)(2,1)} %get-tuple-element.125), channel_id=1, source_target_pairs={{4,0},{5,1},{6,2},{7,3},{8,4},{9,5},{10,6},{11,7},{12,8},{13,9},{1... | collective-permute-start | bytes 1572872 | tf_op jit(solution)/shard_map/ppermute | solution.py:15
  280.5 68.7 %collective-permute-start.14 = (bf16[256,8,128]{2,1,0:T(8,128)(2,1)}, bf16[256,8,128]{2,1,0:T(8,128)(2,1)}, u32[]{:S(2)}, u32[]{:S(2)}) collective-permute-start(bf16[256,8,128]{2,1,0:T(8,128)(2,1)} %get-tuple-element.126), channel_id=1, source_target_pairs={{3,0},{4,1},{5,2},{6,3},{7,4},{8,5},{9,6},{10,7},{11,8},{12,9},{13... | collective-permute-start | bytes 1572872 | tf_op jit(solution)/shard_map/ppermute | solution.py:15
  292.8 70.6 %collective-permute-start.13 = (bf16[256,8,128]{2,1,0:T(8,128)(2,1)}, bf16[256,8,128]{2,1,0:T(8,128)(2,1)}, u32[]{:S(2)}, u32[]{:S(2)}) collective-permute-start(bf16[256,8,128]{2,1,0:T(8,128)(2,1)} %get-tuple-element.127), channel_id=1, source_target_pairs={{2,0},{3,1},{4,2},{5,3},{6,4},{7,5},{8,6},{9,7},{10,8},{11,9},{12,... | collective-permute-start | bytes 1572872 | tf_op jit(solution)/shard_map/ppermute | solution.py:15
where the time goes:
time: 368 us; the launch traced here: 366 us
  waiting for transfers between devices  170 us (46%)
  matrix products  94.7 us (26%)
  starting transfers between devices  47.2 us (13%)
  local copies, waits for them, and re-layouts  35.6 us (10%)
  other arithmetic  17.7 us (5%)
    ppermute x16, waiting for transfers between devices, from_behind(): return lax.ppermute(block, axis, route)  170 us
    ppermute x16, starting transfers between devices, from_behind(): return lax.ppermute(block, axis, route)  47.2 us
    dot_general x8, matrix products, group_grads(): jnp.einsum('arc,rad->cd', weights_b, g_group, preferred_element_type=jnp....  17.2 us
    dot_general x8, matrix products, group_grads(): jnp.einsum('arc,rad->cd', dscore, q_group, preferred_element_type=jnp.flo...  17.1 us
    dot_general x8, matrix products, group_grads(): jnp.einsum('arc,cd->rad', dscore, k_group, preferred_element_type=jnp.flo...  16.1 us
    sub x8, matrix products, group_grads(): unnorm = jnp.exp(masked - row_max)  16.1 us
    dot_general x8, matrix products, group_grads(): jnp.einsum('arc,cd->rad', weights_b, v_group, preferred_element_type=jnp....  15.8 us
    transpose x1, local copies, waits for them, and re-layouts, body(): value_terms = jnp.transpose(value_terms, (1, 0, 2))  13.2 us
  transfers between devices with their start and end apart: 16, of which 14 were waited for; matrix products, arithmetic and copies ran while one was open for 6% of the time, Pallas kernels for 0%

commit v1 on v0

v1 whole, which is shorter than its diff:
```python
import functools

import jax
import jax.numpy as jnp
from jax import lax
from jax.experimental import pallas as pl
from jax.experimental.pallas import tpu as pltpu
from jax.sharding import PartitionSpec as P

WINDOW = 1024


QUERY_SCALE = 168.0 ** (-0.5)

NT = (((1,), (1,)), ((), ()))
TN = (((0,), (0,)), ((), ()))


def shift(block, axis, distance):
    devices = range(lax.axis_size(axis))
    route = [(i, i + distance) for i in devices if i + distance in devices]
    return lax.ppermute(block, axis, route)


def to_sibling(block, axis, from_parity):
    size = lax.axis_size(axis)
    route = [(i, i ^ 1) for i in range(size) if i % 2 == from_parity]
    return lax.ppermute(block, axis, route)


def attention_kernel(qd_ref, kd_ref, q_ref, k_ref, v_ref, g_ref, o_ref, dq_ref, dk_ref, dv_ref):
    rows = q_ref.shape[0]
    cols = k_ref.shape[0]
    head_size = k_ref.shape[1]
    q_pos = lax.broadcasted_iota(jnp.int32, (rows, cols), 0)
    k_pos = lax.broadcasted_iota(jnp.int32, (rows, cols), 1)
    allowed = (qd_ref[...] == kd_ref[...]) & (k_pos > q_pos) & (k_pos <= q_pos + WINDOW)
    k = k_ref[...]
    v = v_ref[...]
    dk_acc = jnp.zeros((cols, head_size), jnp.float32)
    dv_acc = jnp.zeros((cols, head_size), jnp.float32)
    for a in range(q_ref.shape[1] // head_size):
        lanes = slice(a * head_size, (a + 1) * head_size)
        q = q_ref[:, lanes]
        g = g_ref[:, lanes]
        scores = QUERY_SCALE * lax.dot_general(q, k, NT, preferred_element_type=jnp.float32)
        masked = jnp.where(allowed, scores, -jnp.inf)
        row_max = jnp.max(masked, axis=1, keepdims=True)
        unnorm = jnp.exp(masked - row_max)
        inv = 1.0 / jnp.sum(unnorm, axis=1, keepdims=True)
        weights = unnorm * inv
        weights_b = weights.astype(jnp.bfloat16)
        attended = jnp.dot(weights_b, v, preferred_element_type=jnp.float32).astype(jnp.bfloat16)
        o_ref[:, lanes] = attended
        row_dot = jnp.sum(g.astype(jnp.float32) * attended.astype(jnp.float32), axis=1, keepdims=True)
        dprob = lax.dot_general(g, v, NT, preferred_element_type=jnp.float32)
        dscore = (weights * (dprob - row_dot)).astype(jnp.bfloat16)
        dq = QUERY_SCALE * jnp.dot(dscore, k, preferred_element_type=jnp.float32)
        dq_ref[:, lanes] = dq.astype(jnp.bfloat16)
        dk_acc = dk_acc + lax.dot_general(dscore, q, TN, preferred_element_type=jnp.float32)
        dv_acc = dv_acc + lax.dot_general(weights_b, g, TN, preferred_element_type=jnp.float32)
    dk_ref[...] = (QUERY_SCALE * dk_acc).astype(jnp.bfloat16)
    dv_ref[...] = dv_acc.astype(jnp.bfloat16)


def attention(q2, k_win, v_win, g2, q_docs, k_docs, groups, head_size):
    rows = q2.shape[0]
    cols = k_win.shape[0]
    per_group = q2.shape[1] // groups
    q_spec = pl.BlockSpec((rows, per_group), lambda i: (0, i))
    kv_spec = pl.BlockSpec((cols, head_size), lambda i: (0, i))
    flops = 12 * rows * cols * q2.shape[1]
    bytes_accessed = 2 * (4 * q2.size + 4 * k_win.size)
    return pl.pallas_call(
        attention_kernel,
        grid=(groups,),
        in_specs=[
            pl.BlockSpec((rows, 1), lambda i: (0, 0)),
            pl.BlockSpec((1, cols), lambda i: (0, 0)),
            q_spec,
            kv_spec,
            kv_spec,
            q_spec,
        ],
        out_specs=[q_spec, q_spec, kv_spec, kv_spec],
        out_shape=[
            jax.ShapeDtypeStruct(q2.shape, jnp.bfloat16),
            jax.ShapeDtypeStruct(q2.shape, jnp.bfloat16),
            jax.ShapeDtypeStruct(k_win.shape, jnp.bfloat16),
            jax.ShapeDtypeStruct(k_win.shape, jnp.bfloat16),
        ],
        compiler_params=pltpu.CompilerParams(dimension_semantics=("arbitrary",)),
        cost_estimate=pl.CostEstimate(
            flops=flops, transcendentals=rows * cols * q2.shape[1] // head_size,
            bytes_accessed=bytes_accessed),
    )(q_docs, k_docs, q2, k_win, v_win, g2)


def body(query_heads, key_heads, value_heads, grad_out, doc_ids):
    row_count = query_heads.shape[0]
    groups = key_heads.shape[1]
    head_size = key_heads.shape[2]
    reach = WINDOW // row_count
    assert reach == 4
    piece_pos = lax.axis_index("ctx")
    is_even = piece_pos % 2 == 0

    own = (key_heads, value_heads)
    back2 = shift(own, "ctx", 2)
    back4 = shift(back2, "ctx", 2)
    from_even_1 = to_sibling(own, "ctx", 0)
    from_odd_1 = to_sibling(back2, "ctx", 1)
    from_even_3 = to_sibling(back2, "ctx", 0)
    from_odd_3 = to_sibling(back4, "ctx", 1)
    back1 = jax.tree.map(lambda e, o: jnp.where(is_even, o, e), from_even_1, from_odd_1)
    back3 = jax.tree.map(lambda e, o: jnp.where(is_even, o, e), from_even_3, from_odd_3)
    pieces = [back4, back3, back2, back1, own]
    k_window = jnp.concatenate([p[0] for p in pieces], 0)
    v_window = jnp.concatenate([p[1] for p in pieces], 0)
    cols = k_window.shape[0]

    pad_docs = jnp.concatenate([jnp.full((WINDOW,), -1, jnp.int32), doc_ids], 0)
    first_row = piece_pos * row_count
    q_docs = lax.dynamic_slice_in_dim(doc_ids, first_row, row_count, 0)
    k_docs = lax.dynamic_slice_in_dim(pad_docs, first_row, WINDOW + row_count, 0)

    attended, grad_q, key_terms, value_terms = attention(
        query_heads.reshape(row_count, -1),
        k_window.reshape(cols, -1),
        v_window.reshape(cols, -1),
        grad_out.reshape(row_count, -1),
        q_docs.reshape(row_count, 1),
        k_docs.reshape(1, cols),
        groups,
        head_size,
    )
    key_terms = key_terms.reshape(cols, groups, head_size)
    value_terms = value_terms.reshape(cols, groups, head_size)

    def term_for(offset):
        lower = (reach - offset) * row_count
        return (key_terms[lower : lower + row_count], value_terms[lower : lower + row_count])

    def wide(pair):
        return tuple(x.astype(jnp.float32) for x in pair)

    def add(*pairs):
        total = wide(pairs[0])
        for pair in pairs[1:]:
            total = tuple(t + x.astype(jnp.float32) for t, x in zip(total, wide(pair)))
        return total

    def narrow(pair):
        return tuple(x.astype(jnp.bfloat16) for x in pair)

    terms = [term_for(d) for d in range(reach + 1)]
    sib = to_sibling((terms[1], terms[3]), "ctx", 0), to_sibling((terms[1], terms[3]), "ctx", 1)
    sib_1 = jax.tree.map(lambda e, o: jnp.where(is_even, o, e), sib[0][0], sib[1][0])
    sib_3 = jax.tree.map(lambda e, o: jnp.where(is_even, o, e), sib[0][1], sib[1][1])
    first = narrow(jax.tree.map(
        lambda p4, s3: jnp.where(is_even, p4.astype(jnp.float32), p4.astype(jnp.float32) + s3.astype(jnp.float32)),
        terms[4], sib_3))
    got_first = shift(first, "ctx", -2)
    second = narrow(jax.tree.map(
        lambda g, p2, s1, s3: g.astype(jnp.float32) + p2.astype(jnp.float32)
        + jnp.where(is_even, s3, s1).astype(jnp.float32),
        got_first, terms[2], sib_1, sib_3))
    got_second = shift(second, "ctx", -2)
    total = jax.tree.map(
        lambda g, p0, s1: g.astype(jnp.float32) + p0.astype(jnp.float32)
        + jnp.where(is_even, s1.astype(jnp.float32), 0.0),
        got_second, terms[0], sib_1)
    total_k, total_v = total
    attended = attended.reshape(query_heads.shape)
    grad_q = grad_q.reshape(query_heads.shape)
    return (attended, grad_q, total_k.astype(jnp.bfloat16), total_v.astype(jnp.bfloat16))


def solution(mesh):
    placed = (
        P(("dp", "ctx"), None, None),
        P(("dp", "ctx"), None, None),
        P(("dp", "ctx"), None, None),
        P(("dp", "ctx"), None, None),
        P("dp"),
    )
    return jax.shard_map(
        body,
        mesh=mesh,
        in_specs=placed,
        out_specs=(
            P(("dp", "ctx"), None, None),
            P(("dp", "ctx"), None, None),
            P(("dp", "ctx"), None, None),
            P(("dp", "ctx"), None, None),
        ),
        check_vma=False,
    )
```

time: 368 us -> 164 us (0.45)
  waiting for transfers between devices: 170 us -> 54 us
  matrix products: 94.7 us -> 0 us
  Pallas kernels: 0 us -> 28.2 us
  local copies, waits for them, and re-layouts: 35.6 us -> 13.7 us
  starting transfers between devices: 47.2 us -> 58.2 us
  other arithmetic: 17.7 us -> 8.03 us
    ppermute x16 -> x24, waiting for transfers between devices: 170 us -> 54 us  [the longest x8 53 us: shift(): return lax.ppermute(block, axis, route)]
    dot_general x40 -> x0, matrix products: 78.6 us -> none  [the longest x8 17.2 us: group_grads(): jnp.einsum('arc,rad->cd', weights_b, g_group, preferred_element_type=jnp....]
    pallas_call x0 -> x1, Pallas kernels: none -> 28.2 us  [attention(): pl.pallas_call(attention_kernel, grid=(groups,), in_specs=[pl.BlockSpec((...]
    transpose x3 -> x0, local copies, waits for them, and re-layouts: 20.6 us -> none  [the longest x1 13.2 us: body(): value_terms = jnp.transpose(value_terms, (1, 0, 2))]
    sub x8 -> x0, matrix products: 16.1 us -> none  [group_grads(): unnorm = jnp.exp(masked - row_max)]
    ppermute x16 -> x24, starting transfers between devices: 47.2 us -> 58.2 us  [the longest x16 31.4 us: to_sibling(): return lax.ppermute(block, axis, route)]
    reduce_sum x8 -> x0, other arithmetic: 7.64 us -> none  [group_grads(): jnp.sum(g_group.astype(jnp.float32) * attended.astype(jnp.float32), axis=-1)]
    reshape x0 -> x3, local copies, waits for them, and re-layouts: none -> 4.82 us  [the longest x1 3.42 us: body(): grad_out.reshape(row_count, -1)]
  transfers between devices with their start and end apart: 16 -> 24, of which waited for: 14 -> 9; matrix products, arithmetic and copies ran while one was open for 6% -> 8% of each run, Pallas kernels for 0% -> 0%
where the time goes in v1:
time: 164 us; the launch traced here: 163 us
  starting transfers between devices  58.2 us (35%)
  waiting for transfers between devices  54 us (33%)
  Pallas kernels  28.2 us (17%)
  local copies, waits for them, and re-layouts  13.7 us (8%)
  other arithmetic  8.03 us (5%)
    ppermute x8, waiting for transfers between devices, shift(): return lax.ppermute(block, axis, route)  53 us
    ppermute x16, starting transfers between devices, to_sibling(): return lax.ppermute(block, axis, route)  31.4 us
    pallas_call x1, Pallas kernels, attention(): pl.pallas_call(attention_kernel, grid=(groups,), in_specs=[pl.BlockSpec((...  28.2 us
    ppermute x8, starting transfers between devices, shift(): return lax.ppermute(block, axis, route)  26.8 us
    unnamed x30, local copies, waits for them, and re-layouts  8.55 us
    unnamed x5, other arithmetic  4.66 us
    reshape x1, local copies, waits for them, and re-layouts, body(): grad_out.reshape(row_count, -1)  3.42 us
  transfers between devices with their start and end apart: 24, of which 9 were waited for; matrix products, arithmetic and copies ran while one was open for 8% of the time, Pallas kernels for 0%

profile of v1, /device:TPU:100, one launch (start us, length us, event | category | flops | bytes accessed | tf_op | source)
XLA Modules:
  0.0 163.2 jit_solution(13148551992908450609)
XLA Ops:
  0.6 5.0 %collective-permute-start.6 = (bf16[256,8,128]{2,1,0:T(8,128)(2,1)}, bf16[256,8,128]{2,1,0:T(8,128)(2,1)S(1)}, u32[]{:S(2)}, u32[]{:S(2)}) collective-permute-start(bf16[256,8,128]{2,1,0:T(8,128)(2,1)} %param.7), channel_id=1, source_target_pairs={{0,2},{1,3},{2,4},{3,5},{4,6},{5,7},{6,8},{7,9},{8,10},{9,11},{10,... | collective-permute-start | bytes 1572872 | tf_op jit(solution)/shard_map/ppermute | solution.py:22
  5.7 2.9 %collective-permute-start = (bf16[256,8,128]{2,1,0:T(8,128)(2,1)}, bf16[256,8,128]{2,1,0:T(8,128)(2,1)S(1)}, u32[]{:S(2)}, u32[]{:S(2)}) collective-permute-start(bf16[256,8,128]{2,1,0:T(8,128)(2,1)} %param.6), channel_id=1, source_target_pairs={{0,2},{1,3},{2,4},{3,5},{4,6},{5,7},{6,8},{7,9},{8,10},{9,11},{10,... | collective-permute-start | bytes 1572872 | tf_op jit(solution)/shard_map/ppermute | solution.py:22
  8.6 9.7 %collective-permute-done.6 = bf16[256,8,128]{2,1,0:T(8,128)(2,1)S(1)} collective-permute-done((bf16[256,8,128]{2,1,0:T(8,128)(2,1)}, bf16[256,8,128]{2,1,0:T(8,128)(2,1)S(1)}, u32[]{:S(2)}, u32[]{:S(2)}) %collective-permute-start.6) | collective-permute-done | bytes 524320 | tf_op jit(solution)/shard_map/ppermute | solution.py:22
  18.3 5.5 %collective-permute-start.7 = (bf16[256,8,128]{2,1,0:T(8,128)(2,1)S(1)}, bf16[256,8,128]{2,1,0:T(8,128)(2,1)S(1)}, u32[]{:S(2)}, u32[]{:S(2)}) collective-permute-start(bf16[256,8,128]{2,1,0:T(8,128)(2,1)S(1)} %collective-permute-done.6), channel_id=1, source_target_pairs={{0,2},{1,3},{2,4},{3,5},{4,6},{5,7},{6,8},{7,9},{8,10},{9,11},{10,... | collective-permute-start | bytes 1572872 | tf_op jit(solution)/shard_map/ppermute | solution.py:22
  23.8 2.1 %collective-permute-start.5 = (bf16[256,8,128]{2,1,0:T(8,128)(2,1)}, bf16[256,8,128]{2,1,0:T(8,128)(2,1)}, u32[]{:S(2)}, u32[]{:S(2)}) collective-permute-start(bf16[256,8,128]{2,1,0:T(8,128)(2,1)} %param.6), channel_id=1, source_target_pairs={{0,1},{2,3},{4,5},{6,7},{8,9},{10,11},{12,13},{14,15},{16,17},{18,... | collective-permute-start | bytes 1572872 | tf_op jit(solution)/shard_map/ppermute | solution.py:28
  25.9 3.6 %collective-permute-done = bf16[256,8,128]{2,1,0:T(8,128)(2,1)S(1)} collective-permute-done((bf16[256,8,128]{2,1,0:T(8,128)(2,1)}, bf16[256,8,128]{2,1,0:T(8,128)(2,1)S(1)}, u32[]{:S(2)}, u32[]{:S(2)}) %collective-permute-start) | collective-permute-done | bytes 524320 | tf_op jit(solution)/shard_map/ppermute | solution.py:22
  29.5 1.3 collective-permute-start.3
  30.8 5.5 %collective-permute-start.1 = (bf16[256,8,128]{2,1,0:T(8,128)(2,1)S(1)}, bf16[256,8,128]{2,1,0:T(8,128)(2,1)S(1)}, u32[]{:S(2)}, u32[]{:S(2)}) collective-permute-start(bf16[256,8,128]{2,1,0:T(8,128)(2,1)S(1)} %collective-permute-done), channel_id=1, source_target_pairs={{0,2},{1,3},{2,4},{3,5},{4,6},{5,7},{6,8},{7,9},{8,10},{9,11},{10,... | collective-permute-start | bytes 1572872 | tf_op jit(solution)/shard_map/ppermute | solution.py:22
  36.3 2.1 %collective-permute-start.9 = (bf16[256,8,128]{2,1,0:T(8,128)(2,1)S(1)}, bf16[256,8,128]{2,1,0:T(8,128)(2,1)}, u32[]{:S(2)}, u32[]{:S(2)}) collective-permute-start(bf16[256,8,128]{2,1,0:T(8,128)(2,1)S(1)} %collective-permute-done.6), channel_id=1, source_target_pairs={{0,1},{2,3},{4,5},{6,7},{8,9},{10,11},{12,13},{14,15},{16,17},{18,... | collective-permute-start | bytes 1572872 | tf_op jit(solution)/shard_map/ppermute | solution.py:28
  38.4 2.2 %collective-permute-done.7 = bf16[256,8,128]{2,1,0:T(8,128)(2,1)S(1)} collective-permute-done((bf16[256,8,128]{2,1,0:T(8,128)(2,1)S(1)}, bf16[256,8,128]{2,1,0:T(8,128)(2,1)S(1)}, u32[]{:S(2)}, u32[]{:S(2)}) %collective-permute-start.7) | collective-permute-done | bytes 524320 | tf_op jit(solution)/shard_map/ppermute | solution.py:22
  42.0 3.4 %copy_bitcast_fusion.2 = (bf16[256,2048]{1,0:T(8,128)(2,1)}, bf16[256,2048]{1,0:T(8,128)(2,1)}) fusion(bf16[32,8,16,128]{3,2,1,0:T(8,128)(2,1)} %bitcast.79, bf16[32,8,16,128]{3,2,1,0:T(8,128)(2,1)} %bitcast.80), kind=kLoop, calls=%fused_computation.18 | loop fusion | bytes 4194304 | tf_op jit(solution)/shard_map/reshape | solution.py:131
  46.9 3.8 %collective-permute-done.1 = bf16[256,8,128]{2,1,0:T(8,128)(2,1)S(1)} collective-permute-done((bf16[256,8,128]{2,1,0:T(8,128)(2,1)S(1)}, bf16[256,8,128]{2,1,0:T(8,128)(2,1)S(1)}, u32[]{:S(2)}, u32[]{:S(2)}) %collective-permute-start.1) | collective-permute-done | bytes 524320 | tf_op jit(solution)/shard_map/ppermute | solution.py:22
  52.2 3.1 %collective-permute-start.11 = (bf16[256,8,128]{2,1,0:T(8,128)(2,1)S(1)}, bf16[256,8,128]{2,1,0:T(8,128)(2,1)S(1)}, u32[]{:S(2)}, u32[]{:S(2)}) collective-permute-start(bf16[256,8,128]{2,1,0:T(8,128)(2,1)S(1)} %copy-done.3), channel_id=1, source_target_pairs={{0,1},{2,3},{4,5},{6,7},{8,9},{10,11},{12,13},{14,15},{16,17},{18,... | collective-permute-start | bytes 1572872 | tf_op jit(solution)/shard_map/ppermute | solution.py:28
  55.3 1.3 collective-permute-start.4
  56.6 1.3 collective-permute-start.10
  60.8 2.2 %copy.30 = bf16[160,8,8,128]{3,1,2,0:T(8,128)(2,1)} copy(bf16[160,8,8,128]{3,2,1,0:T(8,128)(2,1)S(1)} %bitcast.72) | data formatting | bytes 5242880
  63.1 2.1 %copy.31 = bf16[160,8,8,128]{3,1,2,0:T(8,128)(2,1)} copy(bf16[160,8,8,128]{3,2,1,0:T(8,128)(2,1)S(1)} %bitcast.71) | data formatting | bytes 5242880
  65.2 28.2 %shard_map.84 = (bf16[256,2048]{1,0:T(8,128)(2,1)}, bf16[256,2048]{1,0:T(8,128)(2,1)}, bf16[1280,1024]{1,0:T(8,128)(2,1)}, bf16[1280,1024]{1,0:T(8,128)(2,1)}) custom-call(s32[256,1]{1,0:T(8,128)} %copy.9.qd_ref, s32[1,1280]{1,0:T(1,128)} %reshape.57.kd_ref, bf16[256,2048]{1,0:T(8,128)(2,1)} %get-tuple-element.25.q_ref, bf16[1280,1024]{1,0:T(8,128)(2,1)} %bitcast.74, ...), custom_call_target="tpu_custom_call" | custom-call | flops 8053063680 | bytes 14680064 | tf_op jit(solution)/shard_map/pallas_call | solution.py:74
  93.4 2.3 %slice_bitcast_fusion.2 = (bf16[32,8,8,128]{3,1,2,0:T(8,128)(2,1)S(1)}, f32[32,8,8,128]{3,1,2,0:T(8,128)S(1)}, f32[32,8,8,128]{3,1,2,0:T(8,128)S(1)}, bf16[32,8,...) fusion(bf16[1280,1024]{1,0:T(8,128)(2,1)} %get-tuple-element.10), kind=kLoop, calls=%fused_computation.28 | loop fusion | flops 786432 | bytes 6815744
  95.8 3.2 %collective-permute-start.13 = (bf16[256,8,128]{2,1,0:T(8,128)(2,1)S(1)}, bf16[256,8,128]{2,1,0:T(8,128)(2,1)S(1)}, u32[]{:S(2)}, u32[]{:S(2)}) collective-permute-start(bf16[256,8,128]{2,1,0:T(8,128)(2,1)S(1)} %bitcast.87), channel_id=1, source_target_pairs={{0,1},{2,3},{4,5},{6,7},{8,9},{10,11},{12,13},{14,15},{16,17},{18,... | collective-permute-start | bytes 1572872 | tf_op jit(solution)/shard_map/ppermute | solution.py:28
  99.1 1.3 collective-permute-start.12
  101.1 3.1 %collective-permute-start.19 = (bf16[256,8,128]{2,1,0:T(8,128)(2,1)S(1)}, bf16[256,8,128]{2,1,0:T(8,128)(2,1)S(1)}, u32[]{:S(2)}, u32[]{:S(2)}) collective-permute-start(bf16[256,8,128]{2,1,0:T(8,128)(2,1)S(1)} %bitcast.85), channel_id=1, source_target_pairs={{0,1},{2,3},{4,5},{6,7},{8,9},{10,11},{12,13},{14,15},{16,17},{18,... | collective-permute-start | bytes 1572872 | tf_op jit(solution)/shard_map/ppermute | solution.py:28
  105.6 3.1 %collective-permute-start.16 = (bf16[256,8,128]{2,1,0:T(8,128)(2,1)S(1)}, bf16[256,8,128]{2,1,0:T(8,128)(2,1)S(1)}, u32[]{:S(2)}, u32[]{:S(2)}) collective-permute-start(bf16[256,8,128]{2,1,0:T(8,128)(2,1)S(1)} %bitcast.81), channel_id=1, source_target_pairs={{0,1},{2,3},{4,5},{6,7},{8,9},{10,11},{12,13},{14,15},{16,17},{18,... | collective-permute-start | bytes 1572872 | tf_op jit(solution)/shard_map/ppermute | solution.py:28
  110.5 1.9 %collective-permute-start.14 = (bf16[256,8,128]{2,1,0:T(8,128)(2,1)S(1)}, bf16[256,8,128]{2,1,0:T(8,128)(2,1)S(1)}, u32[]{:S(2)}, u32[]{:S(2)}) collective-permute-start(bf16[256,8,128]{2,1,0:T(8,128)(2,1)S(1)} %fusion), channel_id=1, source_target_pairs={{2,0},{3,1},{4,2},{5,3},{6,4},{7,5},{8,6},{9,7},{10,8},{11,9},{12,... | collective-permute-start | bytes 1572872 | tf_op jit(solution)/shard_map/ppermute | solution.py:22
  112.8 3.1 %collective-permute-start.22 = (bf16[256,8,128]{2,1,0:T(8,128)(2,1)S(1)}, bf16[256,8,128]{2,1,0:T(8,128)(2,1)S(1)}, u32[]{:S(2)}, u32[]{:S(2)}) collective-permute-start(bf16[256,8,128]{2,1,0:T(8,128)(2,1)S(1)} %bitcast.83), channel_id=1, source_target_pairs={{0,1},{2,3},{4,5},{6,7},{8,9},{10,11},{12,13},{14,15},{16,17},{18,... | collective-permute-start | bytes 1572872 | tf_op jit(solution)/shard_map/ppermute | solution.py:28
  117.4 1.9 %collective-permute-start.20 = (bf16[256,8,128]{2,1,0:T(8,128)(2,1)S(1)}, bf16[256,8,128]{2,1,0:T(8,128)(2,1)S(1)}, u32[]{:S(2)}, u32[]{:S(2)}) collective-permute-start(bf16[256,8,128]{2,1,0:T(8,128)(2,1)S(1)} %fusion.1), channel_id=1, source_target_pairs={{2,0},{3,1},{4,2},{5,3},{6,4},{7,5},{8,6},{9,7},{10,8},{11,9},{12,... | collective-permute-start | bytes 1572872 | tf_op jit(solution)/shard_map/ppermute | solution.py:22
  119.7 8.7 %collective-permute-done.14 = bf16[256,8,128]{2,1,0:T(8,128)(2,1)S(1)} collective-permute-done((bf16[256,8,128]{2,1,0:T(8,128)(2,1)S(1)}, bf16[256,8,128]{2,1,0:T(8,128)(2,1)S(1)}, u32[]{:S(2)}, u32[]{:S(2)}) %collective-permute-start.14) | collective-permute-done | bytes 524320 | tf_op jit(solution)/shard_map/ppermute | solution.py:22
  128.8 2.1 %collective-permute-start.17 = (bf16[256,8,128]{2,1,0:T(8,128)(2,1)S(1)}, bf16[256,8,128]{2,1,0:T(8,128)(2,1)S(1)}, u32[]{:S(2)}, u32[]{:S(2)}) collective-permute-start(bf16[256,8,128]{2,1,0:T(8,128)(2,1)S(1)} %fusion.9), channel_id=1, source_target_pairs={{2,0},{3,1},{4,2},{5,3},{6,4},{7,5},{8,6},{9,7},{10,8},{11,9},{12,... | collective-permute-start | bytes 1572872 | tf_op jit(solution)/shard_map/ppermute | solution.py:22
  130.9 8.7 %collective-permute-done.20 = bf16[256,8,128]{2,1,0:T(8,128)(2,1)S(1)} collective-permute-done((bf16[256,8,128]{2,1,0:T(8,128)(2,1)S(1)}, bf16[256,8,128]{2,1,0:T(8,128)(2,1)S(1)}, u32[]{:S(2)}, u32[]{:S(2)}) %collective-permute-start.20) | collective-permute-done | bytes 524320 | tf_op jit(solution)/shard_map/ppermute | solution.py:22
  140.0 1.9 %collective-permute-start.23 = (bf16[256,8,128]{2,1,0:T(8,128)(2,1)S(1)}, bf16[256,8,128]{2,1,0:T(8,128)(2,1)S(1)}, u32[]{:S(2)}, u32[]{:S(2)}) collective-permute-start(bf16[256,8,128]{2,1,0:T(8,128)(2,1)S(1)} %fusion.5), channel_id=1, source_target_pairs={{2,0},{3,1},{4,2},{5,3},{6,4},{7,5},{8,6},{9,7},{10,8},{11,9},{12,... | collective-permute-start | bytes 1572872 | tf_op jit(solution)/shard_map/ppermute | solution.py:22
  144.8 6.1 %collective-permute-done.17 = bf16[256,8,128]{2,1,0:T(8,128)(2,1)S(1)} collective-permute-done((bf16[256,8,128]{2,1,0:T(8,128)(2,1)S(1)}, bf16[256,8,128]{2,1,0:T(8,128)(2,1)S(1)}, u32[]{:S(2)}, u32[]{:S(2)}) %collective-permute-start.17) | collective-permute-done | bytes 524320 | tf_op jit(solution)/shard_map/ppermute | solution.py:22
  151.9 10.2 %collective-permute-done.23 = bf16[256,8,128]{2,1,0:T(8,128)(2,1)S(1)} collective-permute-done((bf16[256,8,128]{2,1,0:T(8,128)(2,1)S(1)}, bf16[256,8,128]{2,1,0:T(8,128)(2,1)S(1)}, u32[]{:S(2)}, u32[]{:S(2)}) %collective-permute-start.23) | collective-permute-done | bytes 524320 | tf_op jit(solution)/shard_map/ppermute | solution.py:22
  (65 shorter events, 19.0 us)
Async XLA Ops:
  0.6 44.7 %copy-start.5 = (s32[4096]{0:T(1024)S(1)}, s32[4096]{0:T(1024)}, u32[]{:S(2)}) copy-start(s32[4096]{0:T(1024)} %param.9) | copy-start | bytes 49156
  0.6 17.6 %collective-permute-start.6 = (bf16[256,8,128]{2,1,0:T(8,128)(2,1)}, bf16[256,8,128]{2,1,0:T(8,128)(2,1)S(1)}, u32[]{:S(2)}, u32[]{:S(2)}) collective-permute-start(bf16[256,8,128]{2,1,0:T(8,128)(2,1)} %param.7), channel_id=1, source_target_pairs={{0,2},{1,3},{2,4},{3,5},{4,6},{5,7},{6,8},{7,9},{8,10},{9,11},{10,... | collective-permute-start | bytes 1572872 | tf_op jit(solution)/shard_map/ppermute | solution.py:22
  5.7 23.8 %collective-permute-start = (bf16[256,8,128]{2,1,0:T(8,128)(2,1)}, bf16[256,8,128]{2,1,0:T(8,128)(2,1)S(1)}, u32[]{:S(2)}, u32[]{:S(2)}) collective-permute-start(bf16[256,8,128]{2,1,0:T(8,128)(2,1)} %param.6), channel_id=1, source_target_pairs={{0,2},{1,3},{2,4},{3,5},{4,6},{5,7},{6,8},{7,9},{8,10},{9,11},{10,... | collective-permute-start | bytes 1572872 | tf_op jit(solution)/shard_map/ppermute | solution.py:22
  18.3 22.4 %collective-permute-start.7 = (bf16[256,8,128]{2,1,0:T(8,128)(2,1)S(1)}, bf16[256,8,128]{2,1,0:T(8,128)(2,1)S(1)}, u32[]{:S(2)}, u32[]{:S(2)}) collective-permute-start(bf16[256,8,128]{2,1,0:T(8,128)(2,1)S(1)} %collective-permute-done.6), channel_id=1, source_target_pairs={{0,2},{1,3},{2,4},{3,5},{4,6},{5,7},{6,8},{7,9},{8,10},{9,11},{10,... | collective-permute-start | bytes 1572872 | tf_op jit(solution)/shard_map/ppermute | solution.py:22
  23.8 35.7 %collective-permute-start.5 = (bf16[256,8,128]{2,1,0:T(8,128)(2,1)}, bf16[256,8,128]{2,1,0:T(8,128)(2,1)}, u32[]{:S(2)}, u32[]{:S(2)}) collective-permute-start(bf16[256,8,128]{2,1,0:T(8,128)(2,1)} %param.6), channel_id=1, source_target_pairs={{0,1},{2,3},{4,5},{6,7},{8,9},{10,11},{12,13},{14,15},{16,17},{18,... | collective-permute-start | bytes 1572872 | tf_op jit(solution)/shard_map/ppermute | solution.py:28
  29.5 22.6 %collective-permute-start.3 = (bf16[256,8,128]{2,1,0:T(8,128)(2,1)S(1)}, bf16[256,8,128]{2,1,0:T(8,128)(2,1)S(1)}, u32[]{:S(2)}, u32[]{:S(2)}) collective-permute-start(bf16[256,8,128]{2,1,0:T(8,128)(2,1)S(1)} %collective-permute-done), channel_id=1, source_target_pairs={{0,1},{2,3},{4,5},{6,7},{8,9},{10,11},{12,13},{14,15},{16,17},{18,... | collective-permute-start | bytes 1572872 | tf_op jit(solution)/shard_map/ppermute | solution.py:28
  30.8 19.9 %collective-permute-start.1 = (bf16[256,8,128]{2,1,0:T(8,128)(2,1)S(1)}, bf16[256,8,128]{2,1,0:T(8,128)(2,1)S(1)}, u32[]{:S(2)}, u32[]{:S(2)}) collective-permute-start(bf16[256,8,128]{2,1,0:T(8,128)(2,1)S(1)} %collective-permute-done), channel_id=1, source_target_pairs={{0,2},{1,3},{2,4},{3,5},{4,6},{5,7},{6,8},{7,9},{8,10},{9,11},{10,... | collective-permute-start | bytes 1572872 | tf_op jit(solution)/shard_map/ppermute | solution.py:22
  36.3 18.9 %collective-permute-start.9 = (bf16[256,8,128]{2,1,0:T(8,128)(2,1)S(1)}, bf16[256,8,128]{2,1,0:T(8,128)(2,1)}, u32[]{:S(2)}, u32[]{:S(2)}) collective-permute-start(bf16[256,8,128]{2,1,0:T(8,128)(2,1)S(1)} %collective-permute-done.6), channel_id=1, source_target_pairs={{0,1},{2,3},{4,5},{6,7},{8,9},{10,11},{12,13},{14,15},{16,17},{18,... | collective-permute-start | bytes 1572872 | tf_op jit(solution)/shard_map/ppermute | solution.py:28
  40.7 15.9 %collective-permute-start.8 = (bf16[256,8,128]{2,1,0:T(8,128)(2,1)S(1)}, bf16[256,8,128]{2,1,0:T(8,128)(2,1)}, u32[]{:S(2)}, u32[]{:S(2)}) collective-permute-start(bf16[256,8,128]{2,1,0:T(8,128)(2,1)S(1)} %collective-permute-done.7), channel_id=1, source_target_pairs={{1,0},{3,2},{5,4},{7,6},{9,8},{11,10},{13,12},{15,14},{17,16},{19,... | collective-permute-start | bytes 1572872 | tf_op jit(solution)/shard_map/ppermute | solution.py:28
  41.9 10.2 %copy-start.3 = (bf16[256,8,128]{2,1,0:T(8,128)(2,1)S(1)}, bf16[256,8,128]{2,1,0:T(8,128)(2,1)}, u32[]{:S(2)}) copy-start(bf16[256,8,128]{2,1,0:T(8,128)(2,1)} %param.7) | copy-start | bytes 1572868
  50.8 8.4 %collective-permute-start.2 = (bf16[256,8,128]{2,1,0:T(8,128)(2,1)S(1)}, bf16[256,8,128]{2,1,0:T(8,128)(2,1)S(1)}, u32[]{:S(2)}, u32[]{:S(2)}) collective-permute-start(bf16[256,8,128]{2,1,0:T(8,128)(2,1)S(1)} %collective-permute-done.1), channel_id=1, source_target_pairs={{1,0},{3,2},{5,4},{7,6},{9,8},{11,10},{13,12},{15,14},{17,16},{19,... | collective-permute-start | bytes 1572872 | tf_op jit(solution)/shard_map/ppermute | solution.py:28
  52.2 7.3 %collective-permute-start.11 = (bf16[256,8,128]{2,1,0:T(8,128)(2,1)S(1)}, bf16[256,8,128]{2,1,0:T(8,128)(2,1)S(1)}, u32[]{:S(2)}, u32[]{:S(2)}) collective-permute-start(bf16[256,8,128]{2,1,0:T(8,128)(2,1)S(1)} %copy-done.3), channel_id=1, source_target_pairs={{0,1},{2,3},{4,5},{6,7},{8,9},{10,11},{12,13},{14,15},{16,17},{18,... | collective-permute-start | bytes 1572872 | tf_op jit(solution)/shard_map/ppermute | solution.py:28
  55.3 4.2 %collective-permute-start.4 = (bf16[256,8,128]{2,1,0:T(8,128)(2,1)S(1)}, bf16[256,8,128]{2,1,0:T(8,128)(2,1)S(1)}, u32[]{:S(2)}, u32[]{:S(2)}) collective-permute-start(bf16[256,8,128]{2,1,0:T(8,128)(2,1)S(1)} %collective-permute-done), channel_id=1, source_target_pairs={{1,0},{3,2},{5,4},{7,6},{9,8},{11,10},{13,12},{15,14},{17,16},{19,... | collective-permute-start | bytes 1572872 | tf_op jit(solution)/shard_map/ppermute | solution.py:28
  56.6 3.8 %collective-permute-start.10 = (bf16[256,8,128]{2,1,0:T(8,128)(2,1)S(1)}, bf16[256,8,128]{2,1,0:T(8,128)(2,1)S(1)}, u32[]{:S(2)}, u32[]{:S(2)}) collective-permute-start(bf16[256,8,128]{2,1,0:T(8,128)(2,1)S(1)} %collective-permute-done.6), channel_id=1, source_target_pairs={{1,0},{3,2},{5,4},{7,6},{9,8},{11,10},{13,12},{15,14},{17,16},{19,... | collective-permute-start | bytes 1572872 | tf_op jit(solution)/shard_map/ppermute | solution.py:28
  60.8 2.2 %copy-start.4 = (bf16[256,8,128]{2,1,0:T(8,128)(2,1)S(1)}, bf16[256,8,128]{2,1,0:T(8,128)(2,1)}, u32[]{:S(2)}) copy-start(bf16[256,8,128]{2,1,0:T(8,128)(2,1)} %param.6) | copy-start | bytes 1572868
  93.4 7.0 %copy-start = (bf16[1280,1024]{1,0:T(8,128)(2,1)S(1)}, bf16[1280,1024]{1,0:T(8,128)(2,1)}, u32[]{:S(2)}) copy-start(bf16[1280,1024]{1,0:T(8,128)(2,1)} %get-tuple-element.11) | copy-start | bytes 7864324
  95.8 13.1 %collective-permute-start.13 = (bf16[256,8,128]{2,1,0:T(8,128)(2,1)S(1)}, bf16[256,8,128]{2,1,0:T(8,128)(2,1)S(1)}, u32[]{:S(2)}, u32[]{:S(2)}) collective-permute-start(bf16[256,8,128]{2,1,0:T(8,128)(2,1)S(1)} %bitcast.87), channel_id=1, source_target_pairs={{0,1},{2,3},{4,5},{6,7},{8,9},{10,11},{12,13},{14,15},{16,17},{18,... | collective-permute-start | bytes 1572872 | tf_op jit(solution)/shard_map/ppermute | solution.py:28
  99.1 11.2 %collective-permute-start.12 = (bf16[256,8,128]{2,1,0:T(8,128)(2,1)S(1)}, bf16[256,8,128]{2,1,0:T(8,128)(2,1)S(1)}, u32[]{:S(2)}, u32[]{:S(2)}) collective-permute-start(bf16[256,8,128]{2,1,0:T(8,128)(2,1)S(1)} %bitcast.88), channel_id=1, source_target_pairs={{1,0},{3,2},{5,4},{7,6},{9,8},{11,10},{13,12},{15,14},{17,16},{19,... | collective-permute-start | bytes 1572872 | tf_op jit(solution)/shard_map/ppermute | solution.py:28
  101.1 11.6 %collective-permute-start.19 = (bf16[256,8,128]{2,1,0:T(8,128)(2,1)S(1)}, bf16[256,8,128]{2,1,0:T(8,128)(2,1)S(1)}, u32[]{:S(2)}, u32[]{:S(2)}) collective-permute-start(bf16[256,8,128]{2,1,0:T(8,128)(2,1)S(1)} %bitcast.85), channel_id=1, source_target_pairs={{0,1},{2,3},{4,5},{6,7},{8,9},{10,11},{12,13},{14,15},{16,17},{18,... | collective-permute-start | bytes 1572872 | tf_op jit(solution)/shard_map/ppermute | solution.py:28
  104.2 11.6 %collective-permute-start.18 = (bf16[256,8,128]{2,1,0:T(8,128)(2,1)S(1)}, bf16[256,8,128]{2,1,0:T(8,128)(2,1)S(1)}, u32[]{:S(2)}, u32[]{:S(2)}) collective-permute-start(bf16[256,8,128]{2,1,0:T(8,128)(2,1)S(1)} %bitcast.86), channel_id=1, source_target_pairs={{1,0},{3,2},{5,4},{7,6},{9,8},{11,10},{13,12},{15,14},{17,16},{19,... | collective-permute-start | bytes 1572872 | tf_op jit(solution)/shard_map/ppermute | solution.py:28
  105.6 11.7 %collective-permute-start.16 = (bf16[256,8,128]{2,1,0:T(8,128)(2,1)S(1)}, bf16[256,8,128]{2,1,0:T(8,128)(2,1)S(1)}, u32[]{:S(2)}, u32[]{:S(2)}) collective-permute-start(bf16[256,8,128]{2,1,0:T(8,128)(2,1)S(1)} %bitcast.81), channel_id=1, source_target_pairs={{0,1},{2,3},{4,5},{6,7},{8,9},{10,11},{12,13},{14,15},{16,17},{18,... | collective-permute-start | bytes 1572872 | tf_op jit(solution)/shard_map/ppermute | solution.py:28
  109.0 10.8 %collective-permute-start.15 = (bf16[256,8,128]{2,1,0:T(8,128)(2,1)S(1)}, bf16[256,8,128]{2,1,0:T(8,128)(2,1)S(1)}, u32[]{:S(2)}, u32[]{:S(2)}) collective-permute-start(bf16[256,8,128]{2,1,0:T(8,128)(2,1)S(1)} %bitcast.82), channel_id=1, source_target_pairs={{1,0},{3,2},{5,4},{7,6},{9,8},{11,10},{13,12},{15,14},{17,16},{19,... | collective-permute-start | bytes 1572872 | tf_op jit(solution)/shard_map/ppermute | solution.py:28
  110.5 17.9 %collective-permute-start.14 = (bf16[256,8,128]{2,1,0:T(8,128)(2,1)S(1)}, bf16[256,8,128]{2,1,0:T(8,128)(2,1)S(1)}, u32[]{:S(2)}, u32[]{:S(2)}) collective-permute-start(bf16[256,8,128]{2,1,0:T(8,128)(2,1)S(1)} %fusion), channel_id=1, source_target_pairs={{2,0},{3,1},{4,2},{5,3},{6,4},{7,5},{8,6},{9,7},{10,8},{11,9},{12,... | collective-permute-start | bytes 1572872 | tf_op jit(solution)/shard_map/ppermute | solution.py:22
  112.8 18.1 %collective-permute-start.22 = (bf16[256,8,128]{2,1,0:T(8,128)(2,1)S(1)}, bf16[256,8,128]{2,1,0:T(8,128)(2,1)S(1)}, u32[]{:S(2)}, u32[]{:S(2)}) collective-permute-start(bf16[256,8,128]{2,1,0:T(8,128)(2,1)S(1)} %bitcast.83), channel_id=1, source_target_pairs={{0,1},{2,3},{4,5},{6,7},{8,9},{10,11},{12,13},{14,15},{16,17},{18,... | collective-permute-start | bytes 1572872 | tf_op jit(solution)/shard_map/ppermute | solution.py:28
  115.9 15.0 %collective-permute-start.21 = (bf16[256,8,128]{2,1,0:T(8,128)(2,1)S(1)}, bf16[256,8,128]{2,1,0:T(8,128)(2,1)S(1)}, u32[]{:S(2)}, u32[]{:S(2)}) collective-permute-start(bf16[256,8,128]{2,1,0:T(8,128)(2,1)S(1)} %bitcast.84), channel_id=1, source_target_pairs={{1,0},{3,2},{5,4},{7,6},{9,8},{11,10},{13,12},{15,14},{17,16},{19,... | collective-permute-start | bytes 1572872 | tf_op jit(solution)/shard_map/ppermute | solution.py:28
  117.4 22.2 %collective-permute-start.20 = (bf16[256,8,128]{2,1,0:T(8,128)(2,1)S(1)}, bf16[256,8,128]{2,1,0:T(8,128)(2,1)S(1)}, u32[]{:S(2)}, u32[]{:S(2)}) collective-permute-start(bf16[256,8,128]{2,1,0:T(8,128)(2,1)S(1)} %fusion.1), channel_id=1, source_target_pairs={{2,0},{3,1},{4,2},{5,3},{6,4},{7,5},{8,6},{9,7},{10,8},{11,9},{12,... | collective-permute-start | bytes 1572872 | tf_op jit(solution)/shard_map/ppermute | solution.py:22
  128.8 13.2 %copy-start.2 = (bf16[256,2048]{1,0:T(8,128)(2,1)S(1)}, bf16[256,2048]{1,0:T(8,128)(2,1)}, u32[]{:S(2)}) copy-start(bf16[256,2048]{1,0:T(8,128)(2,1)} %get-tuple-element.8) | copy-start | bytes 3145732
  128.8 14.4 %copy-start.1 = (bf16[256,2048]{1,0:T(8,128)(2,1)S(1)}, bf16[256,2048]{1,0:T(8,128)(2,1)}, u32[]{:S(2)}) copy-start(bf16[256,2048]{1,0:T(8,128)(2,1)} %get-tuple-element.9) | copy-start | bytes 3145732
  128.8 22.1 %collective-permute-start.17 = (bf16[256,8,128]{2,1,0:T(8,128)(2,1)S(1)}, bf16[256,8,128]{2,1,0:T(8,128)(2,1)S(1)}, u32[]{:S(2)}, u32[]{:S(2)}) collective-permute-start(bf16[256,8,128]{2,1,0:T(8,128)(2,1)S(1)} %fusion.9), channel_id=1, source_target_pairs={{2,0},{3,1},{4,2},{5,3},{6,4},{7,5},{8,6},{9,7},{10,8},{11,9},{12,... | collective-permute-start | bytes 1572872 | tf_op jit(solution)/shard_map/ppermute | solution.py:22
  140.0 22.1 %collective-permute-start.23 = (bf16[256,8,128]{2,1,0:T(8,128)(2,1)S(1)}, bf16[256,8,128]{2,1,0:T(8,128)(2,1)S(1)}, u32[]{:S(2)}, u32[]{:S(2)}) collective-permute-start(bf16[256,8,128]{2,1,0:T(8,128)(2,1)S(1)} %fusion.5), channel_id=1, source_target_pairs={{2,0},{3,1},{4,2},{5,3},{6,4},{7,5},{8,6},{9,7},{10,8},{11,9},{12,... | collective-permute-start | bytes 1572872 | tf_op jit(solution)/shard_map/ppermute | solution.py:22

commit v2 on v1

v2 whole, which is shorter than its diff:
```python
import jax
import jax.numpy as jnp
from jax import lax
from jax.experimental import pallas as pl
from jax.experimental.pallas import tpu as pltpu
from jax.sharding import PartitionSpec as P

WINDOW = 1024
CHUNKS = 1


QUERY_SCALE = 168.0 ** (-0.5)

NT = (((1,), (1,)), ((), ()))
TN = (((0,), (0,)), ((), ()))


def shift(block, axis, distance):
    devices = range(lax.axis_size(axis))
    route = [(i, i + distance) for i in devices if i + distance in devices]
    return lax.ppermute(block, axis, route)


def swap(block, axis):
    return lax.ppermute(block, axis, [(i, i ^ 1) for i in range(lax.axis_size(axis))])


def attention_kernel(qd_ref, kd_ref, q_ref, g_ref, p4_ref, p3_ref, p2_ref, p1_ref, p0_ref,
                     o_ref, dq_ref, d13_ref, d4_ref, d2_ref, d0_ref):
    rows = q_ref.shape[0]
    head_size = p0_ref.shape[2]
    pieces = (p4_ref, p3_ref, p2_ref, p1_ref, p0_ref)
    cols = rows * len(pieces)
    q_pos = lax.broadcasted_iota(jnp.int32, (rows, cols), 0)
    k_pos = lax.broadcasted_iota(jnp.int32, (rows, cols), 1)
    allowed = (qd_ref[...] == kd_ref[...]) & (k_pos > q_pos) & (k_pos <= q_pos + WINDOW)
    k = jnp.concatenate([p[0] for p in pieces], axis=0)
    v = jnp.concatenate([p[1] for p in pieces], axis=0)
    dk_acc = jnp.zeros((cols, head_size), jnp.float32)
    dv_acc = jnp.zeros((cols, head_size), jnp.float32)
    for a in range(q_ref.shape[1] // head_size):
        lanes = slice(a * head_size, (a + 1) * head_size)
        q = q_ref[:, lanes]
        g = g_ref[:, lanes]
        scores = QUERY_SCALE * lax.dot_general(q, k, NT, preferred_element_type=jnp.float32)
        masked = jnp.where(allowed, scores, -jnp.inf)
        row_max = jnp.max(masked, axis=1, keepdims=True)
        unnorm = jnp.exp(masked - row_max)
        inv = 1.0 / jnp.sum(unnorm, axis=1, keepdims=True)
        weights = unnorm * inv
        weights_b = weights.astype(jnp.bfloat16)
        attended = jnp.dot(weights_b, v, preferred_element_type=jnp.float32).astype(jnp.bfloat16)
        o_ref[:, lanes] = attended
        row_dot = jnp.sum(g.astype(jnp.float32) * attended.astype(jnp.float32), axis=1, keepdims=True)
        dprob = lax.dot_general(g, v, NT, preferred_element_type=jnp.float32)
        dscore = (weights * (dprob - row_dot)).astype(jnp.bfloat16)
        dq = QUERY_SCALE * jnp.dot(dscore, k, preferred_element_type=jnp.float32)
        dq_ref[:, lanes] = dq.astype(jnp.bfloat16)
        dk_acc = dk_acc + lax.dot_general(dscore, q, TN, preferred_element_type=jnp.float32)
        dv_acc = dv_acc + lax.dot_general(weights_b, g, TN, preferred_element_type=jnp.float32)
    for j, term in enumerate(((QUERY_SCALE * dk_acc).astype(jnp.bfloat16), dv_acc.astype(jnp.bfloat16))):
        d4_ref[j] = term[0:rows]
        d13_ref[j, rows:2 * rows] = term[rows:2 * rows]
        d2_ref[j] = term[2 * rows:3 * rows]
        d13_ref[j, 0:rows] = term[3 * rows:4 * rows]
        d0_ref[j] = term[4 * rows:5 * rows]


def attention(q2, g2, pieces, q_docs, k_docs, head_size):
    rows = q2.shape[0]
    groups = pieces[0].shape[2] // head_size
    per_group = q2.shape[1] // groups
    cols = rows * len(pieces)
    q_spec = pl.BlockSpec((rows, per_group), lambda i: (0, i))
    kv_spec = pl.BlockSpec((2, rows, head_size), lambda i: (0, 0, i))
    pair_spec = pl.BlockSpec((2, 2 * rows, head_size), lambda i: (0, 0, i))
    piece_shape = jax.ShapeDtypeStruct(pieces[0].shape, jnp.bfloat16)
    flops = 12 * rows * cols * q2.shape[1]
    bytes_accessed = 2 * (4 * q2.size + 10 * pieces[0].size)
    return pl.pallas_call(
        attention_kernel,
        grid=(groups,),
        in_specs=[
            pl.BlockSpec((rows, 1), lambda i: (0, 0)),
            pl.BlockSpec((1, cols), lambda i: (0, 0)),
            q_spec,
            q_spec,
        ] + [kv_spec] * len(pieces),
        out_specs=[q_spec, q_spec, pair_spec, kv_spec, kv_spec, kv_spec],
        out_shape=[
            jax.ShapeDtypeStruct(q2.shape, jnp.bfloat16),
            jax.ShapeDtypeStruct(q2.shape, jnp.bfloat16),
            jax.ShapeDtypeStruct((2, 2 * rows, pieces[0].shape[2]), jnp.bfloat16),
            piece_shape,
            piece_shape,
            piece_shape,
        ],
        compiler_params=pltpu.CompilerParams(dimension_semantics=("arbitrary",)),
        cost_estimate=pl.CostEstimate(
            flops=flops, transcendentals=rows * cols * q2.shape[1] // head_size,
            bytes_accessed=bytes_accessed),
    )(q_docs, k_docs, q2, g2, *pieces)


def wide(x):
    return x.astype(jnp.float32)


def chunk_grads(q2, g2, own, is_odd, q_docs, k_docs, head_size):
    rows = q2.shape[0]
    back2 = shift(own, "ctx", 2)
    back4 = shift(back2, "ctx", 2)
    back1 = swap(jnp.where(is_odd, back2, own), "ctx")
    back3 = swap(jnp.where(is_odd, back4, back2), "ctx")
    attended, grad_q, t13, t4, t2, t0 = attention(
        q2, g2, (back4, back3, back2, back1, own), q_docs, k_docs, head_size)
    s13 = swap(t13, "ctx")
    s1 = s13[:, :rows]
    s3 = s13[:, rows:]
    first = jnp.where(is_odd, wide(t4) + wide(s3), wide(t4)).astype(jnp.bfloat16)
    got1 = shift(first, "ctx", -2)
    second = (wide(got1) + wide(t2) + wide(jnp.where(is_odd, s1, s3))).astype(jnp.bfloat16)
    got2 = shift(second, "ctx", -2)
    total = wide(got2) + wide(t0) + jnp.where(is_odd, 0.0, wide(s1))
    return attended, grad_q, total


def body(query_heads, key_heads, value_heads, grad_out, doc_ids):
    row_count = query_heads.shape[0]
    groups = key_heads.shape[1]
    head_size = key_heads.shape[2]
    assert WINDOW // row_count == 4
    piece_pos = lax.axis_index("ctx")
    is_odd = piece_pos % 2 == 1

    pad_docs = jnp.concatenate([jnp.full((WINDOW,), -1, jnp.int32), doc_ids], 0)
    first_row = piece_pos * row_count
    q_docs = lax.dynamic_slice_in_dim(doc_ids, first_row, row_count, 0).reshape(row_count, 1)
    k_docs = lax.dynamic_slice_in_dim(pad_docs, first_row, WINDOW + row_count, 0).reshape(1, -1)

    q2 = query_heads.reshape(row_count, -1)
    g2 = grad_out.reshape(row_count, -1)
    kv = jnp.stack([key_heads.reshape(row_count, -1), value_heads.reshape(row_count, -1)])
    q_width = q2.shape[1] // CHUNKS
    kv_width = kv.shape[2] // CHUNKS
    results = []
    for c in range(CHUNKS):
        results.append(chunk_grads(
            q2[:, c * q_width:(c + 1) * q_width],
            g2[:, c * q_width:(c + 1) * q_width],
            kv[:, :, c * kv_width:(c + 1) * kv_width],
            is_odd, q_docs, k_docs, head_size))
    attended = jnp.concatenate([r[0] for r in results], 1).reshape(query_heads.shape)
    grad_q = jnp.concatenate([r[1] for r in results], 1).reshape(query_heads.shape)
    total = jnp.concatenate([r[2] for r in results], 2)
    grad_k = total[0].astype(jnp.bfloat16).reshape(key_heads.shape)
    grad_v = total[1].astype(jnp.bfloat16).reshape(value_heads.shape)
    return (attended, grad_q, grad_k, grad_v)


def solution(mesh):
    placed = (
        P(("dp", "ctx"), None, None),
        P(("dp", "ctx"), None, None),
        P(("dp", "ctx"), None, None),
        P(("dp", "ctx"), None, None),
        P("dp"),
    )
    return jax.shard_map(
        body,
        mesh=mesh,
        in_specs=placed,
        out_specs=(
            P(("dp", "ctx"), None, None),
            P(("dp", "ctx"), None, None),
            P(("dp", "ctx"), None, None),
            P(("dp", "ctx"), None, None),
        ),
        check_vma=False,
    )
```

time: 164 us -> 160 us (0.976)
  waiting for transfers between devices: 54 us -> 99.6 us
  starting transfers between devices: 58.2 us -> 15.4 us
  local copies, waits for them, and re-layouts: 13.7 us -> 9.3 us
  other arithmetic: 8.03 us -> 6 us
    ppermute x8 -> x4, waiting for transfers between devices: 53 us -> 94.7 us  [shift(): return lax.ppermute(block, axis, route)]
    ppermute x16 -> x3, starting transfers between devices: 31.4 us -> 0.7 us  [swap(): lax.ppermute(block, axis, [(i, i ^ 1) for i in range(lax.axis_size(axis))])]
    ppermute x8 -> x4, starting transfers between devices: 26.8 us -> 14.7 us  [shift(): return lax.ppermute(block, axis, route)]
    unnamed x5 -> x0, other arithmetic: 4.66 us -> none
    unnamed x30 -> x24, local copies, waits for them, and re-layouts: 8.55 us -> 4.35 us
    ppermute x16 -> x3, waiting for transfers between devices: 0.98 us -> 4.88 us  [swap(): lax.ppermute(block, axis, [(i, i ^ 1) for i in range(lax.axis_size(axis))])]
    select_n x0 -> x1, other arithmetic: none -> 2.74 us  [chunk_grads(): back1 = swap(jnp.where(is_odd, back2, own), 'ctx')]
    convert_element_type x6 -> x2, other arithmetic: 3.36 us -> 2.58 us  [the longest x1 1.65 us: chunk_grads(): jnp.where(is_odd, wide(t4) + wide(s3), wide(t4)).astype(jnp.bfloat16)]
  transfers between devices with their start and end apart: 24 -> 7, of which waited for: 9 -> 6; matrix products, arithmetic and copies ran while one was open for 8% -> 4% of each run, Pallas kernels for 0% -> 0%
where the time goes in v2:
time: 160 us; the launch traced here: 159 us
  waiting for transfers between devices  99.6 us (62%)
  Pallas kernels  28.2 us (18%)
  starting transfers between devices  15.4 us (10%)
  local copies, waits for them, and re-layouts  9.3 us (6%)
  other arithmetic  6 us (4%)
    ppermute x4, waiting for transfers between devices, shift(): return lax.ppermute(block, axis, route)  94.7 us
    pallas_call x1, Pallas kernels, attention(): pl.pallas_call(attention_kernel, grid=(groups,), in_specs=[pl.BlockSpec((...  28.2 us
    ppermute x4, starting transfers between devices, shift(): return lax.ppermute(block, axis, route)  14.7 us
    ppermute x3, waiting for transfers between devices, swap(): lax.ppermute(block, axis, [(i, i ^ 1) for i in range(lax.axis_size(axis))])  4.88 us
    unnamed x24, local copies, waits for them, and re-layouts  4.35 us
  transfers between devices with their start and end apart: 7, of which 6 were waited for; matrix products, arithmetic and copies ran while one was open for 4% of the time, Pallas kernels for 0%

profile of v2, /device:TPU:100, one launch (start us, length us, event | category | flops | bytes accessed | tf_op | source)
XLA Modules:
  0.0 159.3 jit_solution(5993061964900019139)
XLA Ops:
  0.6 1.3 stack_reshape.6
  2.0 0.2 stack_reshape.7
  2.3 5.0 %collective-permute-start = (bf16[2,256,1024]{2,1,0:T(8,128)(2,1)S(1)}, bf16[2,256,1024]{2,1,0:T(8,128)(2,1)}, u32[]{:S(2)}, u32[]{:S(2)}) collective-permute-start(bf16[2,256,1024]{2,1,0:T(8,128)(2,1)S(1)} %constant_dynamic-update-slice_fusion.p0_ref), channel_id=1, source_target_pairs={{0,2},{1,3},{2,4},{3,5},{4,6},{5,7},{6,8},{7,9},{8,10},{9,11},{10,... | collective-permute-start | bytes 3145736 | tf_op jit(solution)/shard_map/ppermute | solution.py:21
  7.4 22.4 %collective-permute-done.p2_ref = bf16[2,256,1024]{2,1,0:T(8,128)(2,1)} collective-permute-done((bf16[2,256,1024]{2,1,0:T(8,128)(2,1)S(1)}, bf16[2,256,1024]{2,1,0:T(8,128)(2,1)}, u32[]{:S(2)}, u32[]{:S(2)}) %collective-permute-start) | collective-permute-done | bytes 1048608 | tf_op jit(solution)/shard_map/ppermute | solution.py:21
  29.7 5.7 %collective-permute-start.1 = (bf16[2,256,1024]{2,1,0:T(8,128)(2,1)}, bf16[2,256,1024]{2,1,0:T(8,128)(2,1)}, u32[]{:S(2)}, u32[]{:S(2)}) collective-permute-start(bf16[2,256,1024]{2,1,0:T(8,128)(2,1)} %collective-permute-done.p2_ref), channel_id=1, source_target_pairs={{0,2},{1,3},{2,4},{3,5},{4,6},{5,7},{6,8},{7,9},{8,10},{9,11},{10,... | collective-permute-start | bytes 3145736 | tf_op jit(solution)/shard_map/ppermute | solution.py:21
  35.5 0.0 copy-start.8
  35.5 0.0 copy-start.4
  35.5 0.0 copy-start.5
  35.5 21.8 %collective-permute-done.1.p4_ref = bf16[2,256,1024]{2,1,0:T(8,128)(2,1)} collective-permute-done((bf16[2,256,1024]{2,1,0:T(8,128)(2,1)}, bf16[2,256,1024]{2,1,0:T(8,128)(2,1)}, u32[]{:S(2)}, u32[]{:S(2)}) %collective-permute-start.1) | collective-permute-done | bytes 1048608 | tf_op jit(solution)/shard_map/ppermute | solution.py:21
  57.3 2.7 %broadcast_select_fusion = (bf16[2,256,1024]{2,1,0:T(8,128)(2,1)}, bf16[2,256,1024]{2,1,0:T(8,128)(2,1)}) fusion(bf16[2,256,1024]{2,1,0:T(8,128)(2,1)} %collective-permute-done.p2_ref, bf16[2,256,1024]{2,1,0:T(8,128)(2,1)S(1)} %constant_dynamic-update-slice_fusion.p0_ref, pred[]{:T(512)S(6)} %eq.5, bf16[2,256,1024]{2,1,0:T(8,128)(2,1)} %collective-permute-done.1.p4_ref), kind=kLoop, calls=%fused_computation.6 | loop fusion | flops 1048576 | bytes 5242881 | tf_op jit(solution)/shard_map/jit(_where)/select_n | solution.py:113
  60.1 0.5 collective-permute-start.2
  60.6 0.1 dynamic_slice.6
  60.6 0.1 pad_dynamic-slice_fusion
  60.7 0.6 reshape.33.kd_ref
  61.3 0.8 copy.9.qd_ref
  62.1 1.8 %copy_bitcast_fusion = (bf16[256,2048]{1,0:T(8,128)(2,1)}, bf16[256,2048]{1,0:T(8,128)(2,1)}) fusion(bf16[32,8,16,128]{3,2,1,0:T(8,128)(2,1)S(1)} %bitcast.23, bf16[32,8,16,128]{3,2,1,0:T(8,128)(2,1)S(1)} %bitcast.24), kind=kLoop, calls=%fused_computation.4 | loop fusion | bytes 4194304 | tf_op jit(solution)/shard_map/reshape | solution.py:142
  63.9 0.6 collective-permute-done.2.p3_ref
  64.6 28.2 %shard_map.84 = (bf16[256,2048]{1,0:T(8,128)(2,1)}, bf16[256,2048]{1,0:T(8,128)(2,1)}, bf16[2,512,1024]{2,1,0:T(8,128)(2,1)}, bf16[2,256,1024]{2,1,0:T(8,128)(2,...) custom-call(s32[256,1]{1,0:T(8,128)} %copy.9.qd_ref, s32[1,1280]{1,0:T(1,128)} %reshape.33.kd_ref, ...), custom_call_target="tpu_custom_call" | custom-call | flops 8053063680 | bytes 14680064 | tf_op jit(solution)/shard_map/pallas_call | solution.py:80
  92.8 0.2 collective-permute-start.4
  93.0 4.3 %collective-permute-done.4 = bf16[2,512,1024]{2,1,0:T(8,128)(2,1)S(1)} collective-permute-done((bf16[2,512,1024]{2,1,0:T(8,128)(2,1)}, bf16[2,512,1024]{2,1,0:T(8,128)(2,1)S(1)}, u32[]{:S(2)}, u32[]{:S(2)}) %collective-permute-start.4) | collective-permute-done | bytes 2097184 | tf_op jit(solution)/shard_map/ppermute | solution.py:25
  97.2 1.6 %fusion = bf16[2,256,1024]{2,1,0:T(8,128)(2,1)S(1)} fusion(bf16[2,256,1024]{2,1,0:T(8,128)(2,1)} %get-tuple-element.12, pred[]{:T(512)S(6)} %eq.5, bf16[2,512,1024]{2,1,0:T(8,128)(2,1)S(1)} %collective-permute-done.4), kind=kLoop, calls=%fused_computation.1 | loop fusion | flops 2621440 | bytes 3145729 | tf_op jit(solution)/shard_map/convert_element_type | solution.py:120
  98.9 1.9 %collective-permute-start.5 = (bf16[2,256,1024]{2,1,0:T(8,128)(2,1)S(1)}, bf16[2,256,1024]{2,1,0:T(8,128)(2,1)S(1)}, u32[]{:S(2)}, u32[]{:S(2)}) collective-permute-start(bf16[2,256,1024]{2,1,0:T(8,128)(2,1)S(1)} %fusion), channel_id=1, source_target_pairs={{2,0},{3,1},{4,2},{5,3},{6,4},{7,5},{8,6},{9,7},{10,8},{11,9},{12,... | collective-permute-start | bytes 3145736 | tf_op jit(solution)/shard_map/ppermute | solution.py:21
  100.8 27.1 %collective-permute-done.5 = bf16[2,256,1024]{2,1,0:T(8,128)(2,1)S(1)} collective-permute-done((bf16[2,256,1024]{2,1,0:T(8,128)(2,1)S(1)}, bf16[2,256,1024]{2,1,0:T(8,128)(2,1)S(1)}, u32[]{:S(2)}, u32[]{:S(2)}) %collective-permute-start.5) | collective-permute-done | bytes 1048608 | tf_op jit(solution)/shard_map/ppermute | solution.py:21
  127.9 0.9 add_convert_fusion.1
  128.9 2.1 %collective-permute-start.6 = (bf16[2,256,1024]{2,1,0:T(8,128)(2,1)S(1)}, bf16[2,256,1024]{2,1,0:T(8,128)(2,1)S(1)}, u32[]{:S(2)}, u32[]{:S(2)}) collective-permute-start(bf16[2,256,1024]{2,1,0:T(8,128)(2,1)S(1)} %add_convert_fusion.1), channel_id=1, source_target_pairs={{2,0},{3,1},{4,2},{5,3},{6,4},{7,5},{8,6},{9,7},{10,8},{11,9},{12,... | collective-permute-start | bytes 3145736 | tf_op jit(solution)/shard_map/ppermute | solution.py:21
  131.0 1.2 copy.12
  132.2 1.2 copy.13
  133.4 23.4 %collective-permute-done.6 = bf16[2,256,1024]{2,1,0:T(8,128)(2,1)S(1)} collective-permute-done((bf16[2,256,1024]{2,1,0:T(8,128)(2,1)S(1)}, bf16[2,256,1024]{2,1,0:T(8,128)(2,1)S(1)}, u32[]{:S(2)}, u32[]{:S(2)}) %collective-permute-start.6) | collective-permute-done | bytes 1048608 | tf_op jit(solution)/shard_map/ppermute | solution.py:21
  156.7 0.7 add_convert_fusion
  157.4 0.1 slice_bitcast_fusion
  157.5 0.9 copy.15
  158.4 0.9 copy.14
  (19 shorter events, 0.1 us)
Async XLA Ops:
  0.6 1.4 copy-start.7
  2.3 57.8 %copy-start = (bf16[2,256,1024]{2,1,0:T(8,128)(2,1)}, bf16[2,256,1024]{2,1,0:T(8,128)(2,1)S(1)}, u32[]{:S(2)}) copy-start(bf16[2,256,1024]{2,1,0:T(8,128)(2,1)S(1)} %constant_dynamic-update-slice_fusion.p0_ref) | copy-start | bytes 3145732
  2.3 27.4 %collective-permute-start = (bf16[2,256,1024]{2,1,0:T(8,128)(2,1)S(1)}, bf16[2,256,1024]{2,1,0:T(8,128)(2,1)}, u32[]{:S(2)}, u32[]{:S(2)}) collective-permute-start(bf16[2,256,1024]{2,1,0:T(8,128)(2,1)S(1)} %constant_dynamic-update-slice_fusion.p0_ref), channel_id=1, source_target_pairs={{0,2},{1,3},{2,4},{3,5},{4,6},{5,7},{6,8},{7,9},{8,10},{9,11},{10,... | collective-permute-start | bytes 3145736 | tf_op jit(solution)/shard_map/ppermute | solution.py:21
  29.7 27.6 %collective-permute-start.1 = (bf16[2,256,1024]{2,1,0:T(8,128)(2,1)}, bf16[2,256,1024]{2,1,0:T(8,128)(2,1)}, u32[]{:S(2)}, u32[]{:S(2)}) collective-permute-start(bf16[2,256,1024]{2,1,0:T(8,128)(2,1)} %collective-permute-done.p2_ref), channel_id=1, source_target_pairs={{0,2},{1,3},{2,4},{3,5},{4,6},{5,7},{6,8},{7,9},{8,10},{9,11},{10,... | collective-permute-start | bytes 3145736 | tf_op jit(solution)/shard_map/ppermute | solution.py:21
  35.5 25.1 %copy-start.8 = (s32[4096]{0:T(1024)S(1)}, s32[4096]{0:T(1024)}, u32[]{:S(2)}) copy-start(s32[4096]{0:T(1024)} %param.9) | copy-start | bytes 49156
  35.5 26.6 %copy-start.4 = (bf16[256,16,128]{2,1,0:T(8,128)(2,1)S(1)}, bf16[256,16,128]{2,1,0:T(8,128)(2,1)}, u32[]{:S(2)}) copy-start(bf16[256,16,128]{2,1,0:T(8,128)(2,1)} %param.8) | copy-start | bytes 3145732
  35.5 26.6 %copy-start.5 = (bf16[256,16,128]{2,1,0:T(8,128)(2,1)S(1)}, bf16[256,16,128]{2,1,0:T(8,128)(2,1)}, u32[]{:S(2)}) copy-start(bf16[256,16,128]{2,1,0:T(8,128)(2,1)} %param.5) | copy-start | bytes 3145732
  60.0 3.9 %collective-permute-start.3 = (bf16[2,256,1024]{2,1,0:T(8,128)(2,1)}, bf16[2,256,1024]{2,1,0:T(8,128)(2,1)}, u32[]{:S(2)}, u32[]{:S(2)}) collective-permute-start(bf16[2,256,1024]{2,1,0:T(8,128)(2,1)} %get-tuple-element.18), channel_id=1, source_target_pairs={{0,1},{1,0},{2,3},{3,2},{4,5},{5,4},{6,7},{7,6},{8,9},{9,8},{10,11... | collective-permute-start | bytes 3145736 | tf_op jit(solution)/shard_map/ppermute | solution.py:25
  60.1 4.5 %collective-permute-start.2 = (bf16[2,256,1024]{2,1,0:T(8,128)(2,1)}, bf16[2,256,1024]{2,1,0:T(8,128)(2,1)}, u32[]{:S(2)}, u32[]{:S(2)}) collective-permute-start(bf16[2,256,1024]{2,1,0:T(8,128)(2,1)} %get-tuple-element.19), channel_id=1, source_target_pairs={{0,1},{1,0},{2,3},{3,2},{4,5},{5,4},{6,7},{7,6},{8,9},{9,8},{10,11... | collective-permute-start | bytes 3145736 | tf_op jit(solution)/shard_map/ppermute | solution.py:25
  92.8 35.2 %copy-start.6 = (bf16[2,256,1024]{2,1,0:T(8,128)(2,1)S(1)}, bf16[2,256,1024]{2,1,0:T(8,128)(2,1)}, u32[]{:S(2)}) copy-start(bf16[2,256,1024]{2,1,0:T(8,128)(2,1)} %get-tuple-element.14) | copy-start | bytes 3145732
  92.8 4.5 %collective-permute-start.4 = (bf16[2,512,1024]{2,1,0:T(8,128)(2,1)}, bf16[2,512,1024]{2,1,0:T(8,128)(2,1)S(1)}, u32[]{:S(2)}, u32[]{:S(2)}) collective-permute-start(bf16[2,512,1024]{2,1,0:T(8,128)(2,1)} %get-tuple-element.13), channel_id=1, source_target_pairs={{0,1},{1,0},{2,3},{3,2},{4,5},{5,4},{6,7},{7,6},{8,9},{9,8},{10,11... | collective-permute-start | bytes 6291464 | tf_op jit(solution)/shard_map/ppermute | solution.py:25
  98.9 29.1 %collective-permute-start.5 = (bf16[2,256,1024]{2,1,0:T(8,128)(2,1)S(1)}, bf16[2,256,1024]{2,1,0:T(8,128)(2,1)S(1)}, u32[]{:S(2)}, u32[]{:S(2)}) collective-permute-start(bf16[2,256,1024]{2,1,0:T(8,128)(2,1)S(1)} %fusion), channel_id=1, source_target_pairs={{2,0},{3,1},{4,2},{5,3},{6,4},{7,5},{8,6},{9,7},{10,8},{11,9},{12,... | collective-permute-start | bytes 3145736 | tf_op jit(solution)/shard_map/ppermute | solution.py:21
  127.9 3.0 %copy-start.3 = (bf16[256,2048]{1,0:T(8,128)(2,1)S(1)}, bf16[256,2048]{1,0:T(8,128)(2,1)}, u32[]{:S(2)}) copy-start(bf16[256,2048]{1,0:T(8,128)(2,1)} %get-tuple-element.10) | copy-start | bytes 3145732
  128.9 3.3 %copy-start.2 = (bf16[256,2048]{1,0:T(8,128)(2,1)S(1)}, bf16[256,2048]{1,0:T(8,128)(2,1)}, u32[]{:S(2)}) copy-start(bf16[256,2048]{1,0:T(8,128)(2,1)} %get-tuple-element.11) | copy-start | bytes 3145732
  128.9 27.9 %collective-permute-start.6 = (bf16[2,256,1024]{2,1,0:T(8,128)(2,1)S(1)}, bf16[2,256,1024]{2,1,0:T(8,128)(2,1)S(1)}, u32[]{:S(2)}, u32[]{:S(2)}) collective-permute-start(bf16[2,256,1024]{2,1,0:T(8,128)(2,1)S(1)} %add_convert_fusion.1), channel_id=1, source_target_pairs={{2,0},{3,1},{4,2},{5,3},{6,4},{7,5},{8,6},{9,7},{10,8},{11,9},{12,... | collective-permute-start | bytes 3145736 | tf_op jit(solution)/shard_map/ppermute | solution.py:21
  131.0 25.8 %copy-start.1 = (bf16[2,256,1024]{2,1,0:T(8,128)(2,1)S(1)}, bf16[2,256,1024]{2,1,0:T(8,128)(2,1)}, u32[]{:S(2)}) copy-start(bf16[2,256,1024]{2,1,0:T(8,128)(2,1)} %get-tuple-element.15) | copy-start | bytes 3145732

commit v3 on v2

--- a/solution.py
+++ b/solution.py
@@ -5,8 +5,9 @@
 from jax.experimental.pallas import tpu as pltpu
 from jax.sharding import PartitionSpec as P
 
+
 WINDOW = 1024
-CHUNKS = 1
+CHUNKS = 4
 
 
 QUERY_SCALE = 168.0 ** (-0.5)
@@ -26,7 +27,7 @@
 
 
 def attention_kernel(qd_ref, kd_ref, q_ref, g_ref, p4_ref, p3_ref, p2_ref, p1_ref, p0_ref,
-                     o_ref, dq_ref, d13_ref, d4_ref, d2_ref, d0_ref):
+                     o_in, dq_in, o_ref, dq_ref, d13_ref, d4_ref, d2_ref, d0_ref):
     rows = q_ref.shape[0]
     head_size = p0_ref.shape[2]
     pieces = (p4_ref, p3_ref, p2_ref, p1_ref, p0_ref)
@@ -66,17 +67,17 @@
         d0_ref[j] = term[4 * rows:5 * rows]
 
 
-def attention(q2, g2, pieces, q_docs, k_docs, head_size):
+def attention(q2, g2, pieces, q_docs, k_docs, head_size, chunk, o_buf, dq_buf):
     rows = q2.shape[0]
     groups = pieces[0].shape[2] // head_size
-    per_group = q2.shape[1] // groups
+    per_group = 2 * head_size
     cols = rows * len(pieces)
-    q_spec = pl.BlockSpec((rows, per_group), lambda i: (0, i))
+    q_spec = pl.BlockSpec((rows, per_group), lambda i: (0, chunk * groups + i))
     kv_spec = pl.BlockSpec((2, rows, head_size), lambda i: (0, 0, i))
     pair_spec = pl.BlockSpec((2, 2 * rows, head_size), lambda i: (0, 0, i))
     piece_shape = jax.ShapeDtypeStruct(pieces[0].shape, jnp.bfloat16)
-    flops = 12 * rows * cols * q2.shape[1]
-    bytes_accessed = 2 * (4 * q2.size + 10 * pieces[0].size)
+    flops = 12 * rows * cols * per_group * groups
+    bytes_accessed = 2 * (4 * rows * per_group * groups + 10 * pieces[0].size)
     return pl.pallas_call(
         attention_kernel,
         grid=(groups,),
@@ -85,7 +86,7 @@
             pl.BlockSpec((1, cols), lambda i: (0, 0)),
             q_spec,
             q_spec,
-        ] + [kv_spec] * len(pieces),
+        ] + [kv_spec] * len(pieces) + [pl.BlockSpec(memory_space=pl.ANY)] * 2,
         out_specs=[q_spec, q_spec, pair_spec, kv_spec, kv_spec, kv_spec],
         out_shape=[
             jax.ShapeDtypeStruct(q2.shape, jnp.bfloat16),
@@ -95,25 +96,31 @@
             piece_shape,
             piece_shape,
         ],
+        input_output_aliases={4 + len(pieces): 0, 5 + len(pieces): 1},
         compiler_params=pltpu.CompilerParams(dimension_semantics=("arbitrary",)),
         cost_estimate=pl.CostEstimate(
-            flops=flops, transcendentals=rows * cols * q2.shape[1] // head_size,
+            flops=flops, transcendentals=rows * cols * per_group * groups // head_size,
             bytes_accessed=bytes_accessed),
-    )(q_docs, k_docs, q2, g2, *pieces)
+    )(q_docs, k_docs, q2, g2, *pieces, o_buf, dq_buf)
 
 
 def wide(x):
     return x.astype(jnp.float32)
 
 
-def chunk_grads(q2, g2, own, is_odd, q_docs, k_docs, head_size):
-    rows = q2.shape[0]
+def forward_exchange(own, is_odd):
+    rows = own.shape[1]
     back2 = shift(own, "ctx", 2)
     back4 = shift(back2, "ctx", 2)
-    back1 = swap(jnp.where(is_odd, back2, own), "ctx")
-    back3 = swap(jnp.where(is_odd, back4, back2), "ctx")
-    attended, grad_q, t13, t4, t2, t0 = attention(
-        q2, g2, (back4, back3, back2, back1, own), q_docs, k_docs, head_size)
+    odd_pieces = jnp.where(is_odd, jnp.concatenate([back2, back4], 1),
+                           jnp.concatenate([own, back2], 1))
+    back13 = swap(odd_pieces, "ctx")
+    return (back4, back13[:, rows:], back2, back13[:, :rows], own)
+
+
+def backward_exchange(terms, is_odd):
+    t13, t4, t2, t0 = terms
+    rows = t4.shape[1]
     s13 = swap(t13, "ctx")
     s1 = s13[:, :rows]
     s3 = s13[:, rows:]
@@ -121,13 +128,11 @@
     got1 = shift(first, "ctx", -2)
     second = (wide(got1) + wide(t2) + wide(jnp.where(is_odd, s1, s3))).astype(jnp.bfloat16)
     got2 = shift(second, "ctx", -2)
-    total = wide(got2) + wide(t0) + jnp.where(is_odd, 0.0, wide(s1))
-    return attended, grad_q, total
+    return wide(got2) + wide(t0) + jnp.where(is_odd, 0.0, wide(s1))
 
 
-def body(query_heads, key_heads, value_heads, grad_out, doc_ids):
+def staged(query_heads, key_heads, value_heads, grad_out, doc_ids):
     row_count = query_heads.shape[0]
-    groups = key_heads.shape[1]
     head_size = key_heads.shape[2]
     assert WINDOW // row_count == 4
     piece_pos = lax.axis_index("ctx")
@@ -140,19 +145,22 @@
 
     q2 = query_heads.reshape(row_count, -1)
     g2 = grad_out.reshape(row_count, -1)
-    kv = jnp.stack([key_heads.reshape(row_count, -1), value_heads.reshape(row_count, -1)])
-    q_width = q2.shape[1] // CHUNKS
-    kv_width = kv.shape[2] // CHUNKS
-    results = []
+    k2 = key_heads.reshape(row_count, -1)
+    v2 = value_heads.reshape(row_count, -1)
+    kv_width = k2.shape[1] // CHUNKS
+    o_buf = jnp.zeros(q2.shape, jnp.bfloat16)
+    dq_buf = jnp.zeros(q2.shape, jnp.bfloat16)
+    totals = []
     for c in range(CHUNKS):
-        results.append(chunk_grads(
-            q2[:, c * q_width:(c + 1) * q_width],
-            g2[:, c * q_width:(c + 1) * q_width],
-            kv[:, :, c * kv_width:(c + 1) * kv_width],
-            is_odd, q_docs, k_docs, head_size))
-    attended = jnp.concatenate([r[0] for r in results], 1).reshape(query_heads.shape)
-    grad_q = jnp.concatenate([r[1] for r in results], 1).reshape(query_heads.shape)
-    total = jnp.concatenate([r[2] for r in results], 2)
+        lanes = slice(c * kv_width, (c + 1) * kv_width)
+        own = jnp.stack([k2[:, lanes], v2[:, lanes]])
+        pieces = forward_exchange(own, is_odd)
+        o_buf, dq_buf, *terms = attention(
+            q2, g2, pieces, q_docs, k_docs, head_size, c, o_buf, dq_buf)
+        totals.append(backward_exchange(terms, is_odd))
+    attended = o_buf.reshape(query_heads.shape)
+    grad_q = dq_buf.reshape(query_heads.shape)
+    total = jnp.concatenate(totals, 2)
     grad_k = total[0].astype(jnp.bfloat16).reshape(key_heads.shape)
     grad_v = total[1].astype(jnp.bfloat16).reshape(value_heads.shape)
     return (attended, grad_q, grad_k, grad_v)
@@ -167,7 +175,7 @@
         P("dp"),
     )
     return jax.shard_map(
-        body,
+        staged,
         mesh=mesh,
         in_specs=placed,
         out_specs=(

time: 160 us -> 156 us (0.975)
  waiting for transfers between devices: 99.6 us -> 42.8 us
  starting transfers between devices: 15.4 us -> 49.1 us
  local copies, waits for them, and re-layouts: 9.3 us -> 18.7 us
  Pallas kernels: 28.2 us -> 34.6 us
  other arithmetic: 6 us -> 8.41 us
    ppermute x4 -> x16, waiting for transfers between devices: 94.7 us -> 42.7 us  [shift(): return lax.ppermute(block, axis, route)]
    ppermute x4 -> x16, starting transfers between devices: 14.7 us -> 47.3 us  [shift(): return lax.ppermute(block, axis, route)]
    pallas_call x1 -> x4, Pallas kernels: 28.2 us -> 34.6 us  [attention(): pl.pallas_call(attention_kernel, grid=(groups,), in_specs=[pl.BlockSpec((...]
    slice x0 -> x4, local copies, waits for them, and re-layouts: none -> 5.39 us  [forward_exchange(): return (back4, back13[:, rows:], back2, back13[:, :rows], own)]
    ppermute x3 -> x8, waiting for transfers between devices: 4.88 us -> 0.02 us  [swap(): lax.ppermute(block, axis, [(i, i ^ 1) for i in range(lax.axis_size(axis))])]
    unnamed x24 -> x47, local copies, waits for them, and re-layouts: 4.35 us -> 7.66 us
    select_n x1 -> x4, other arithmetic: 2.74 us -> 4.65 us  [forward_exchange(): jnp.where(is_odd, jnp.concatenate([back2, back4], 1), jnp.concatenate([ow...]
    another operation x1 -> x5, other arithmetic: 0.68 us -> 2.37 us  [the longest x4 2.24 us: staged(): own = jnp.stack([k2[:, lanes], v2[:, lanes]])]
  transfers between devices with their start and end apart: 7 -> 24, of which waited for: 6 -> 11; matrix products, arithmetic and copies ran while one was open for 4% -> 15% of each run, Pallas kernels for 0% -> 22%
where the time goes in v3:
time: 156 us; the launch traced here: 155 us
  starting transfers between devices  49.1 us (31%)
  waiting for transfers between devices  42.8 us (27%)
  Pallas kernels  34.6 us (22%)
  local copies, waits for them, and re-layouts  18.7 us (12%)
  other arithmetic  8.41 us (5%)
    ppermute x16, starting transfers between devices, shift(): return lax.ppermute(block, axis, route)  47.3 us
    ppermute x16, waiting for transfers between devices, shift(): return lax.ppermute(block, axis, route)  42.7 us
    pallas_call x4, Pallas kernels, attention(): pl.pallas_call(attention_kernel, grid=(groups,), in_specs=[pl.BlockSpec((...  34.6 us
    unnamed x47, local copies, waits for them, and re-layouts  7.66 us
    slice x4, local copies, waits for them, and re-layouts, forward_exchange(): return (back4, back13[:, rows:], back2, back13[:, :rows], own)  5.39 us
    select_n x4, other arithmetic, forward_exchange(): jnp.where(is_odd, jnp.concatenate([back2, back4], 1), jnp.concatenate([ow...  4.65 us
  transfers between devices with their start and end apart: 24, of which 11 were waited for; matrix products, arithmetic and copies ran while one was open for 15% of the time, Pallas kernels for 22%

profile of v3, /device:TPU:100, one launch (start us, length us, event | category | flops | bytes accessed | tf_op | source)
XLA Modules:
  0.0 154.7 jit_solution(4037894679923333580)
XLA Ops:
  2.1 5.0 %collective-permute-start.9 = (bf16[2,256,256]{2,1,0:T(8,128)(2,1)S(1)}, bf16[2,256,256]{2,1,0:T(8,128)(2,1)}, u32[]{:S(2)}, u32[]{:S(2)}) collective-permute-start(bf16[2,256,256]{2,1,0:T(8,128)(2,1)S(1)} %pad_maximum_fusion.3.p0_ref), channel_id=1, source_target_pairs={{0,2},{1,3},{2,4},{3,5},{4,6},{5,7},{6,8},{7,9},{8,10},{9,11},{10,... | collective-permute-start | bytes 786440 | tf_op jit(solution)/shard_map/ppermute | solution.py:22
  7.9 2.9 %collective-permute-start.6 = (bf16[2,256,256]{2,1,0:T(8,128)(2,1)}, bf16[2,256,256]{2,1,0:T(8,128)(2,1)}, u32[]{:S(2)}, u32[]{:S(2)}) collective-permute-start(bf16[2,256,256]{2,1,0:T(8,128)(2,1)} %pad_maximum_fusion.2.p0_ref), channel_id=1, source_target_pairs={{0,2},{1,3},{2,4},{3,5},{4,6},{5,7},{6,8},{7,9},{8,10},{9,11},{10,... | collective-permute-start | bytes 786440 | tf_op jit(solution)/shard_map/ppermute | solution.py:22
  11.5 3.0 %collective-permute-start.3 = (bf16[2,256,256]{2,1,0:T(8,128)(2,1)}, bf16[2,256,256]{2,1,0:T(8,128)(2,1)}, u32[]{:S(2)}, u32[]{:S(2)}) collective-permute-start(bf16[2,256,256]{2,1,0:T(8,128)(2,1)} %pad_maximum_fusion.1.p0_ref), channel_id=1, source_target_pairs={{0,2},{1,3},{2,4},{3,5},{4,6},{5,7},{6,8},{7,9},{8,10},{9,11},{10,... | collective-permute-start | bytes 786440 | tf_op jit(solution)/shard_map/ppermute | solution.py:22
  14.6 4.9 %collective-permute-start.10 = (bf16[2,256,256]{2,1,0:T(8,128)(2,1)}, bf16[2,256,256]{2,1,0:T(8,128)(2,1)}, u32[]{:S(2)}, u32[]{:S(2)}) collective-permute-start(bf16[2,256,256]{2,1,0:T(8,128)(2,1)} %collective-permute-done.9.p2_ref), channel_id=1, source_target_pairs={{0,2},{1,3},{2,4},{3,5},{4,6},{5,7},{6,8},{7,9},{8,10},{9,11},{10,... | collective-permute-start | bytes 786440 | tf_op jit(solution)/shard_map/ppermute | solution.py:22
  20.3 1.9 %collective-permute-start = (bf16[2,256,256]{2,1,0:T(8,128)(2,1)}, bf16[2,256,256]{2,1,0:T(8,128)(2,1)S(1)}, u32[]{:S(2)}, u32[]{:S(2)}) collective-permute-start(bf16[2,256,256]{2,1,0:T(8,128)(2,1)} %pad_maximum_fusion.p0_ref), channel_id=1, source_target_pairs={{0,2},{1,3},{2,4},{3,5},{4,6},{5,7},{6,8},{7,9},{8,10},{9,11},{10,... | collective-permute-start | bytes 786440 | tf_op jit(solution)/shard_map/ppermute | solution.py:22
  22.2 2.9 %collective-permute-start.7 = (bf16[2,256,256]{2,1,0:T(8,128)(2,1)}, bf16[2,256,256]{2,1,0:T(8,128)(2,1)}, u32[]{:S(2)}, u32[]{:S(2)}) collective-permute-start(bf16[2,256,256]{2,1,0:T(8,128)(2,1)} %collective-permute-done.6.p2_ref), channel_id=1, source_target_pairs={{0,2},{1,3},{2,4},{3,5},{4,6},{5,7},{6,8},{7,9},{8,10},{9,11},{10,... | collective-permute-start | bytes 786440 | tf_op jit(solution)/shard_map/ppermute | solution.py:22
  25.1 5.6 %collective-permute-start.4 = (bf16[2,256,256]{2,1,0:T(8,128)(2,1)}, bf16[2,256,256]{2,1,0:T(8,128)(2,1)}, u32[]{:S(2)}, u32[]{:S(2)}) collective-permute-start(bf16[2,256,256]{2,1,0:T(8,128)(2,1)} %collective-permute-done.3.p2_ref), channel_id=1, source_target_pairs={{0,2},{1,3},{2,4},{3,5},{4,6},{5,7},{6,8},{7,9},{8,10},{9,11},{10,... | collective-permute-start | bytes 786440 | tf_op jit(solution)/shard_map/ppermute | solution.py:22
  30.8 2.0 %maximum_select_fusion.3 = bf16[2,512,256]{2,1,0:T(8,128)(2,1)} fusion(bf16[2,256,256]{2,1,0:T(8,128)(2,1)} %collective-permute-done.10.p4_ref, bf16[2,256,256]{2,1,0:T(8,128)(2,1)} %collective-permute-done.9.p2_ref, bf16[1,256,256]{2,1,0:T(8,128)(2,1)S(1)} %get-tuple-element.60, bf16[1,256,256]{2,1,0:T(8,128)(2,1)S(1)} %get-tuple-element.73, pred[]{:T(512)S(6)} %eq.5), kind=kLoop, calls=%fused_computation.18 | loop fusion | flops 2883584 | bytes 1310721 | tf_op jit(solution)/shard_map/jit(_where)/select_n | solution.py:115
  36.4 5.5 %collective-permute-start.1 = (bf16[2,256,256]{2,1,0:T(8,128)(2,1)S(1)}, bf16[2,256,256]{2,1,0:T(8,128)(2,1)S(1)}, u32[]{:S(2)}, u32[]{:S(2)}) collective-permute-start(bf16[2,256,256]{2,1,0:T(8,128)(2,1)S(1)} %collective-permute-done.p2_ref), channel_id=1, source_target_pairs={{0,2},{1,3},{2,4},{3,5},{4,6},{5,7},{6,8},{7,9},{8,10},{9,11},{10,... | collective-permute-start | bytes 786440 | tf_op jit(solution)/shard_map/ppermute | solution.py:22
  44.8 2.8 %collective-permute-done.4.p4_ref = bf16[2,256,256]{2,1,0:T(8,128)(2,1)} collective-permute-done((bf16[2,256,256]{2,1,0:T(8,128)(2,1)}, bf16[2,256,256]{2,1,0:T(8,128)(2,1)}, u32[]{:S(2)}, u32[]{:S(2)}) %collective-permute-start.4) | collective-permute-done | bytes 262176 | tf_op jit(solution)/shard_map/ppermute | solution.py:22
  48.9 3.0 %collective-permute-done.1.p4_ref = bf16[2,256,256]{2,1,0:T(8,128)(2,1)S(1)} collective-permute-done((bf16[2,256,256]{2,1,0:T(8,128)(2,1)S(1)}, bf16[2,256,256]{2,1,0:T(8,128)(2,1)S(1)}, u32[]{:S(2)}, u32[]{:S(2)}) %collective-permute-start.1) | collective-permute-done | bytes 262176 | tf_op jit(solution)/shard_map/ppermute | solution.py:22
  57.0 8.6 %shard_map.84 = (bf16[256,2048]{1,0:T(8,128)(2,1)}, bf16[256,2048]{1,0:T(8,128)(2,1)}, bf16[2,512,256]{2,1,0:T(8,128)(2,1)}, bf16[2,256,256]{2,1,0:T(8,128)(2,1)...) custom-call(s32[256,1]{1,0:T(8,128)} %copy.20.qd_ref, ...), custom_call_target="tpu_custom_call", output_to_operand_aliasing={{0}: (9, {}), {1}: (10, {})} | custom-call | flops 2013265920 | bytes 3670016 | tf_op jit(solution)/shard_map/pallas_call | solution.py:81
  67.0 8.6 %shard_map.85 = (bf16[256,2048]{1,0:T(8,128)(2,1)}, bf16[256,2048]{1,0:T(8,128)(2,1)}, bf16[2,512,256]{2,1,0:T(8,128)(2,1)}, bf16[2,256,256]{2,1,0:T(8,128)(2,1)...) custom-call(s32[256,1]{1,0:T(8,128)} %copy.20.qd_ref, ...), custom_call_target="tpu_custom_call", output_to_operand_aliasing={{0}: (9, {}), {1}: (10, {})} | custom-call | flops 2013265920 | bytes 3670016 | tf_op jit(solution)/shard_map/pallas_call | solution.py:81
  77.8 8.7 %shard_map.86 = (bf16[256,2048]{1,0:T(8,128)(2,1)}, bf16[256,2048]{1,0:T(8,128)(2,1)}, bf16[2,512,256]{2,1,0:T(8,128)(2,1)}, bf16[2,256,256]{2,1,0:T(8,128)(2,1)...) custom-call(s32[256,1]{1,0:T(8,128)} %copy.20.qd_ref, ...), custom_call_target="tpu_custom_call", output_to_operand_aliasing={{0}: (9, {}), {1}: (10, {})} | custom-call | flops 2013265920 | bytes 3670016 | tf_op jit(solution)/shard_map/pallas_call | solution.py:81
  87.9 8.7 %shard_map.87 = (bf16[256,2048]{1,0:T(8,128)(2,1)}, bf16[256,2048]{1,0:T(8,128)(2,1)}, bf16[2,512,256]{2,1,0:T(8,128)(2,1)}, bf16[2,256,256]{2,1,0:T(8,128)(2,1)...) custom-call(s32[256,1]{1,0:T(8,128)} %copy.20.qd_ref, ...), custom_call_target="tpu_custom_call", output_to_operand_aliasing={{0}: (9, {}), {1}: (10, {})} | custom-call | flops 2013265920 | bytes 3670016 | tf_op jit(solution)/shard_map/pallas_call | solution.py:81
  96.8 2.5 %copy.25 = bf16[32,8,16,128]{3,2,1,0:T(8,128)(2,1)} copy(bf16[32,8,16,128]{3,1,2,0:T(8,128)(2,1)} %bitcast.43) | data formatting | bytes 2097152
  100.6 2.1 %collective-permute-start.13 = (bf16[2,256,256]{2,1,0:T(8,128)(2,1)S(1)}, bf16[2,256,256]{2,1,0:T(8,128)(2,1)S(1)}, u32[]{:S(2)}, u32[]{:S(2)}) collective-permute-start(bf16[2,256,256]{2,1,0:T(8,128)(2,1)S(1)} %fusion), channel_id=1, source_target_pairs={{2,0},{3,1},{4,2},{5,3},{6,4},{7,5},{8,6},{9,7},{10,8},{11,9},{12,... | collective-permute-start | bytes 786440 | tf_op jit(solution)/shard_map/ppermute | solution.py:22
  102.8 1.9 %collective-permute-start.16 = (bf16[2,256,256]{2,1,0:T(8,128)(2,1)S(1)}, bf16[2,256,256]{2,1,0:T(8,128)(2,1)S(1)}, u32[]{:S(2)}, u32[]{:S(2)}) collective-permute-start(bf16[2,256,256]{2,1,0:T(8,128)(2,1)S(1)} %fusion.1), channel_id=1, source_target_pairs={{2,0},{3,1},{4,2},{5,3},{6,4},{7,5},{8,6},{9,7},{10,8},{11,9},{12,... | collective-permute-start | bytes 786440 | tf_op jit(solution)/shard_map/ppermute | solution.py:22
  104.8 1.9 %collective-permute-start.19 = (bf16[2,256,256]{2,1,0:T(8,128)(2,1)S(1)}, bf16[2,256,256]{2,1,0:T(8,128)(2,1)S(1)}, u32[]{:S(2)}, u32[]{:S(2)}) collective-permute-start(bf16[2,256,256]{2,1,0:T(8,128)(2,1)S(1)} %fusion.2), channel_id=1, source_target_pairs={{2,0},{3,1},{4,2},{5,3},{6,4},{7,5},{8,6},{9,7},{10,8},{11,9},{12,... | collective-permute-start | bytes 786440 | tf_op jit(solution)/shard_map/ppermute | solution.py:22
  106.9 1.9 %collective-permute-start.22 = (bf16[2,256,256]{2,1,0:T(8,128)(2,1)S(1)}, bf16[2,256,256]{2,1,0:T(8,128)(2,1)S(1)}, u32[]{:S(2)}, u32[]{:S(2)}) collective-permute-start(bf16[2,256,256]{2,1,0:T(8,128)(2,1)S(1)} %fusion.3), channel_id=1, source_target_pairs={{2,0},{3,1},{4,2},{5,3},{6,4},{7,5},{8,6},{9,7},{10,8},{11,9},{12,... | collective-permute-start | bytes 786440 | tf_op jit(solution)/shard_map/ppermute | solution.py:22
  108.8 4.7 %collective-permute-done.13 = bf16[2,256,256]{2,1,0:T(8,128)(2,1)S(1)} collective-permute-done((bf16[2,256,256]{2,1,0:T(8,128)(2,1)S(1)}, bf16[2,256,256]{2,1,0:T(8,128)(2,1)S(1)}, u32[]{:S(2)}, u32[]{:S(2)}) %collective-permute-start.13) | collective-permute-done | bytes 262176 | tf_op jit(solution)/shard_map/ppermute | solution.py:22
  113.6 1.9 %collective-permute-start.14 = (bf16[2,256,256]{2,1,0:T(8,128)(2,1)S(1)}, bf16[2,256,256]{2,1,0:T(8,128)(2,1)S(1)}, u32[]{:S(2)}, u32[]{:S(2)}) collective-permute-start(bf16[2,256,256]{2,1,0:T(8,128)(2,1)S(1)} %add_convert_fusion.3), channel_id=1, source_target_pairs={{2,0},{3,1},{4,2},{5,3},{6,4},{7,5},{8,6},{9,7},{10,8},{11,9},{12,... | collective-permute-start | bytes 786440 | tf_op jit(solution)/shard_map/ppermute | solution.py:22
  115.5 3.5 %collective-permute-done.16 = bf16[2,256,256]{2,1,0:T(8,128)(2,1)S(1)} collective-permute-done((bf16[2,256,256]{2,1,0:T(8,128)(2,1)S(1)}, bf16[2,256,256]{2,1,0:T(8,128)(2,1)S(1)}, u32[]{:S(2)}, u32[]{:S(2)}) %collective-permute-start.16) | collective-permute-done | bytes 262176 | tf_op jit(solution)/shard_map/ppermute | solution.py:22
  119.2 1.9 %collective-permute-start.17 = (bf16[2,256,256]{2,1,0:T(8,128)(2,1)S(1)}, bf16[2,256,256]{2,1,0:T(8,128)(2,1)S(1)}, u32[]{:S(2)}, u32[]{:S(2)}) collective-permute-start(bf16[2,256,256]{2,1,0:T(8,128)(2,1)S(1)} %add_convert_fusion.2), channel_id=1, source_target_pairs={{2,0},{3,1},{4,2},{5,3},{6,4},{7,5},{8,6},{9,7},{10,8},{11,9},{12,... | collective-permute-start | bytes 786440 | tf_op jit(solution)/shard_map/ppermute | solution.py:22
  121.2 3.5 %collective-permute-done.19 = bf16[2,256,256]{2,1,0:T(8,128)(2,1)S(1)} collective-permute-done((bf16[2,256,256]{2,1,0:T(8,128)(2,1)S(1)}, bf16[2,256,256]{2,1,0:T(8,128)(2,1)S(1)}, u32[]{:S(2)}, u32[]{:S(2)}) %collective-permute-start.19) | collective-permute-done | bytes 262176 | tf_op jit(solution)/shard_map/ppermute | solution.py:22
  124.9 1.9 %collective-permute-start.20 = (bf16[2,256,256]{2,1,0:T(8,128)(2,1)S(1)}, bf16[2,256,256]{2,1,0:T(8,128)(2,1)S(1)}, u32[]{:S(2)}, u32[]{:S(2)}) collective-permute-start(bf16[2,256,256]{2,1,0:T(8,128)(2,1)S(1)} %add_convert_fusion.1), channel_id=1, source_target_pairs={{2,0},{3,1},{4,2},{5,3},{6,4},{7,5},{8,6},{9,7},{10,8},{11,9},{12,... | collective-permute-start | bytes 786440 | tf_op jit(solution)/shard_map/ppermute | solution.py:22
  126.8 3.5 %collective-permute-done.22 = bf16[2,256,256]{2,1,0:T(8,128)(2,1)S(1)} collective-permute-done((bf16[2,256,256]{2,1,0:T(8,128)(2,1)S(1)}, bf16[2,256,256]{2,1,0:T(8,128)(2,1)S(1)}, u32[]{:S(2)}, u32[]{:S(2)}) %collective-permute-start.22) | collective-permute-done | bytes 262176 | tf_op jit(solution)/shard_map/ppermute | solution.py:22
  130.5 1.9 %collective-permute-start.23 = (bf16[2,256,256]{2,1,0:T(8,128)(2,1)S(1)}, bf16[2,256,256]{2,1,0:T(8,128)(2,1)S(1)}, u32[]{:S(2)}, u32[]{:S(2)}) collective-permute-start(bf16[2,256,256]{2,1,0:T(8,128)(2,1)S(1)} %add_convert_fusion), channel_id=1, source_target_pairs={{2,0},{3,1},{4,2},{5,3},{6,4},{7,5},{8,6},{9,7},{10,8},{11,9},{12,... | collective-permute-start | bytes 786440 | tf_op jit(solution)/shard_map/ppermute | solution.py:22
  132.4 3.5 %collective-permute-done.14 = bf16[2,256,256]{2,1,0:T(8,128)(2,1)S(1)} collective-permute-done((bf16[2,256,256]{2,1,0:T(8,128)(2,1)S(1)}, bf16[2,256,256]{2,1,0:T(8,128)(2,1)S(1)}, u32[]{:S(2)}, u32[]{:S(2)}) %collective-permute-start.14) | collective-permute-done | bytes 262176 | tf_op jit(solution)/shard_map/ppermute | solution.py:22
  136.1 5.5 %collective-permute-done.17 = bf16[2,256,256]{2,1,0:T(8,128)(2,1)S(1)} collective-permute-done((bf16[2,256,256]{2,1,0:T(8,128)(2,1)S(1)}, bf16[2,256,256]{2,1,0:T(8,128)(2,1)S(1)}, u32[]{:S(2)}, u32[]{:S(2)}) %collective-permute-start.17) | collective-permute-done | bytes 262176 | tf_op jit(solution)/shard_map/ppermute | solution.py:22
  141.7 5.5 %collective-permute-done.20 = bf16[2,256,256]{2,1,0:T(8,128)(2,1)S(1)} collective-permute-done((bf16[2,256,256]{2,1,0:T(8,128)(2,1)S(1)}, bf16[2,256,256]{2,1,0:T(8,128)(2,1)S(1)}, u32[]{:S(2)}, u32[]{:S(2)}) %collective-permute-start.20) | collective-permute-done | bytes 262176 | tf_op jit(solution)/shard_map/ppermute | solution.py:22
  147.3 5.3 %collective-permute-done.23 = bf16[2,256,256]{2,1,0:T(8,128)(2,1)S(1)} collective-permute-done((bf16[2,256,256]{2,1,0:T(8,128)(2,1)S(1)}, bf16[2,256,256]{2,1,0:T(8,128)(2,1)S(1)}, u32[]{:S(2)}, u32[]{:S(2)}) %collective-permute-start.23) | collective-permute-done | bytes 262176 | tf_op jit(solution)/shard_map/ppermute | solution.py:22
  (100 shorter events, 26.2 us)
Async XLA Ops:
  2.1 17.4 %copy-start.10 = (bf16[2,256,256]{2,1,0:T(8,128)(2,1)}, bf16[2,256,256]{2,1,0:T(8,128)(2,1)S(1)}, u32[]{:S(2)}) copy-start(bf16[2,256,256]{2,1,0:T(8,128)(2,1)S(1)} %pad_maximum_fusion.3.p0_ref) | copy-start | bytes 786436
  2.1 12.5 %collective-permute-start.9 = (bf16[2,256,256]{2,1,0:T(8,128)(2,1)S(1)}, bf16[2,256,256]{2,1,0:T(8,128)(2,1)}, u32[]{:S(2)}, u32[]{:S(2)}) collective-permute-start(bf16[2,256,256]{2,1,0:T(8,128)(2,1)S(1)} %pad_maximum_fusion.3.p0_ref), channel_id=1, source_target_pairs={{0,2},{1,3},{2,4},{3,5},{4,6},{5,7},{6,8},{7,9},{8,10},{9,11},{10,... | collective-permute-start | bytes 786440 | tf_op jit(solution)/shard_map/ppermute | solution.py:22
  7.9 14.3 %collective-permute-start.6 = (bf16[2,256,256]{2,1,0:T(8,128)(2,1)}, bf16[2,256,256]{2,1,0:T(8,128)(2,1)}, u32[]{:S(2)}, u32[]{:S(2)}) collective-permute-start(bf16[2,256,256]{2,1,0:T(8,128)(2,1)} %pad_maximum_fusion.2.p0_ref), channel_id=1, source_target_pairs={{0,2},{1,3},{2,4},{3,5},{4,6},{5,7},{6,8},{7,9},{8,10},{9,11},{10,... | collective-permute-start | bytes 786440 | tf_op jit(solution)/shard_map/ppermute | solution.py:22
  10.8 22.0 %copy-start.2 = (bf16[256,16,128]{2,1,0:T(8,128)(2,1)S(1)}, bf16[256,16,128]{2,1,0:T(8,128)(2,1)}, u32[]{:S(2)}) copy-start(bf16[256,16,128]{2,1,0:T(8,128)(2,1)} %param.5) | copy-start | bytes 3145732
  11.5 21.3 %copy-start.1 = (bf16[256,16,128]{2,1,0:T(8,128)(2,1)S(1)}, bf16[256,16,128]{2,1,0:T(8,128)(2,1)}, u32[]{:S(2)}) copy-start(bf16[256,16,128]{2,1,0:T(8,128)(2,1)} %param.8) | copy-start | bytes 3145732
  11.5 13.6 %collective-permute-start.3 = (bf16[2,256,256]{2,1,0:T(8,128)(2,1)}, bf16[2,256,256]{2,1,0:T(8,128)(2,1)}, u32[]{:S(2)}, u32[]{:S(2)}) collective-permute-start(bf16[2,256,256]{2,1,0:T(8,128)(2,1)} %pad_maximum_fusion.1.p0_ref), channel_id=1, source_target_pairs={{0,2},{1,3},{2,4},{3,5},{4,6},{5,7},{6,8},{7,9},{8,10},{9,11},{10,... | collective-permute-start | bytes 786440 | tf_op jit(solution)/shard_map/ppermute | solution.py:22
  14.6 16.2 %collective-permute-start.10 = (bf16[2,256,256]{2,1,0:T(8,128)(2,1)}, bf16[2,256,256]{2,1,0:T(8,128)(2,1)}, u32[]{:S(2)}, u32[]{:S(2)}) collective-permute-start(bf16[2,256,256]{2,1,0:T(8,128)(2,1)} %collective-permute-done.9.p2_ref), channel_id=1, source_target_pairs={{0,2},{1,3},{2,4},{3,5},{4,6},{5,7},{6,8},{7,9},{8,10},{9,11},{10,... | collective-permute-start | bytes 786440 | tf_op jit(solution)/shard_map/ppermute | solution.py:22
  20.3 16.1 %collective-permute-start = (bf16[2,256,256]{2,1,0:T(8,128)(2,1)}, bf16[2,256,256]{2,1,0:T(8,128)(2,1)S(1)}, u32[]{:S(2)}, u32[]{:S(2)}) collective-permute-start(bf16[2,256,256]{2,1,0:T(8,128)(2,1)} %pad_maximum_fusion.p0_ref), channel_id=1, source_target_pairs={{0,2},{1,3},{2,4},{3,5},{4,6},{5,7},{6,8},{7,9},{8,10},{9,11},{10,... | collective-permute-start | bytes 786440 | tf_op jit(solution)/shard_map/ppermute | solution.py:22
  22.2 21.2 %collective-permute-start.7 = (bf16[2,256,256]{2,1,0:T(8,128)(2,1)}, bf16[2,256,256]{2,1,0:T(8,128)(2,1)}, u32[]{:S(2)}, u32[]{:S(2)}) collective-permute-start(bf16[2,256,256]{2,1,0:T(8,128)(2,1)} %collective-permute-done.6.p2_ref), channel_id=1, source_target_pairs={{0,2},{1,3},{2,4},{3,5},{4,6},{5,7},{6,8},{7,9},{8,10},{9,11},{10,... | collective-permute-start | bytes 786440 | tf_op jit(solution)/shard_map/ppermute | solution.py:22
  25.1 22.5 %collective-permute-start.4 = (bf16[2,256,256]{2,1,0:T(8,128)(2,1)}, bf16[2,256,256]{2,1,0:T(8,128)(2,1)}, u32[]{:S(2)}, u32[]{:S(2)}) collective-permute-start(bf16[2,256,256]{2,1,0:T(8,128)(2,1)} %collective-permute-done.3.p2_ref), channel_id=1, source_target_pairs={{0,2},{1,3},{2,4},{3,5},{4,6},{5,7},{6,8},{7,9},{8,10},{9,11},{10,... | collective-permute-start | bytes 786440 | tf_op jit(solution)/shard_map/ppermute | solution.py:22
  32.8 20.2 %collective-permute-start.11 = (bf16[2,512,256]{2,1,0:T(8,128)(2,1)}, bf16[2,512,256]{2,1,0:T(8,128)(2,1)}, u32[]{:S(2)}, u32[]{:S(2)}) collective-permute-start(bf16[2,512,256]{2,1,0:T(8,128)(2,1)} %maximum_select_fusion.3), channel_id=1, source_target_pairs={{0,1},{1,0},{2,3},{3,2},{4,5},{5,4},{6,7},{7,6},{8,9},{9,8},{10,11... | collective-permute-start | bytes 1572872 | tf_op jit(solution)/shard_map/ppermute | solution.py:26
  36.4 15.6 %copy-start.4 = (bf16[2,256,256]{2,1,0:T(8,128)(2,1)}, bf16[2,256,256]{2,1,0:T(8,128)(2,1)S(1)}, u32[]{:S(2)}) copy-start(bf16[2,256,256]{2,1,0:T(8,128)(2,1)S(1)} %collective-permute-done.p2_ref) | copy-start | bytes 786436
  36.4 15.6 %collective-permute-start.1 = (bf16[2,256,256]{2,1,0:T(8,128)(2,1)S(1)}, bf16[2,256,256]{2,1,0:T(8,128)(2,1)S(1)}, u32[]{:S(2)}, u32[]{:S(2)}) collective-permute-start(bf16[2,256,256]{2,1,0:T(8,128)(2,1)S(1)} %collective-permute-done.p2_ref), channel_id=1, source_target_pairs={{0,2},{1,3},{2,4},{3,5},{4,6},{5,7},{6,8},{7,9},{8,10},{9,11},{10,... | collective-permute-start | bytes 786440 | tf_op jit(solution)/shard_map/ppermute | solution.py:22
  44.7 21.6 %collective-permute-start.8 = (bf16[2,512,256]{2,1,0:T(8,128)(2,1)S(1)}, bf16[2,512,256]{2,1,0:T(8,128)(2,1)S(1)}, u32[]{:S(2)}, u32[]{:S(2)}) collective-permute-start(bf16[2,512,256]{2,1,0:T(8,128)(2,1)S(1)} %maximum_select_fusion.2), channel_id=1, source_target_pairs={{0,1},{1,0},{2,3},{3,2},{4,5},{5,4},{6,7},{7,6},{8,9},{9,8},{10,11... | collective-permute-start | bytes 1572872 | tf_op jit(solution)/shard_map/ppermute | solution.py:26
  48.8 27.1 %collective-permute-start.5 = (bf16[2,512,256]{2,1,0:T(8,128)(2,1)S(1)}, bf16[2,512,256]{2,1,0:T(8,128)(2,1)}, u32[]{:S(2)}, u32[]{:S(2)}) collective-permute-start(bf16[2,512,256]{2,1,0:T(8,128)(2,1)S(1)} %maximum_select_fusion.1), channel_id=1, source_target_pairs={{0,1},{1,0},{2,3},{3,2},{4,5},{5,4},{6,7},{7,6},{8,9},{9,8},{10,11... | collective-permute-start | bytes 1572872 | tf_op jit(solution)/shard_map/ppermute | solution.py:26
  52.9 34.2 %collective-permute-start.2 = (bf16[2,512,256]{2,1,0:T(8,128)(2,1)S(1)}, bf16[2,512,256]{2,1,0:T(8,128)(2,1)S(1)}, u32[]{:S(2)}, u32[]{:S(2)}) collective-permute-start(bf16[2,512,256]{2,1,0:T(8,128)(2,1)S(1)} %maximum_select_fusion), channel_id=1, source_target_pairs={{0,1},{1,0},{2,3},{3,2},{4,5},{5,4},{6,7},{7,6},{8,9},{9,8},{10,11... | collective-permute-start | bytes 1572872 | tf_op jit(solution)/shard_map/ppermute | solution.py:26
  65.7 34.8 %collective-permute-start.12 = (bf16[2,512,256]{2,1,0:T(8,128)(2,1)}, bf16[2,512,256]{2,1,0:T(8,128)(2,1)S(1)}, u32[]{:S(2)}, u32[]{:S(2)}) collective-permute-start(bf16[2,512,256]{2,1,0:T(8,128)(2,1)} %get-tuple-element.37), channel_id=1, source_target_pairs={{0,1},{1,0},{2,3},{3,2},{4,5},{5,4},{6,7},{7,6},{8,9},{9,8},{10,11... | collective-permute-start | bytes 1572872 | tf_op jit(solution)/shard_map/ppermute | solution.py:26
  75.7 27.0 %collective-permute-start.15 = (bf16[2,512,256]{2,1,0:T(8,128)(2,1)}, bf16[2,512,256]{2,1,0:T(8,128)(2,1)S(1)}, u32[]{:S(2)}, u32[]{:S(2)}) collective-permute-start(bf16[2,512,256]{2,1,0:T(8,128)(2,1)} %get-tuple-element.41), channel_id=1, source_target_pairs={{0,1},{1,0},{2,3},{3,2},{4,5},{5,4},{6,7},{7,6},{8,9},{9,8},{10,11... | collective-permute-start | bytes 1572872 | tf_op jit(solution)/shard_map/ppermute | solution.py:26
  86.5 18.2 %collective-permute-start.18 = (bf16[2,512,256]{2,1,0:T(8,128)(2,1)}, bf16[2,512,256]{2,1,0:T(8,128)(2,1)S(1)}, u32[]{:S(2)}, u32[]{:S(2)}) collective-permute-start(bf16[2,512,256]{2,1,0:T(8,128)(2,1)} %get-tuple-element.45), channel_id=1, source_target_pairs={{0,1},{1,0},{2,3},{3,2},{4,5},{5,4},{6,7},{7,6},{8,9},{9,8},{10,11... | collective-permute-start | bytes 1572872 | tf_op jit(solution)/shard_map/ppermute | solution.py:26
  96.6 10.1 %collective-permute-start.21 = (bf16[2,512,256]{2,1,0:T(8,128)(2,1)}, bf16[2,512,256]{2,1,0:T(8,128)(2,1)S(1)}, u32[]{:S(2)}, u32[]{:S(2)}) collective-permute-start(bf16[2,512,256]{2,1,0:T(8,128)(2,1)} %get-tuple-element.49), channel_id=1, source_target_pairs={{0,1},{1,0},{2,3},{3,2},{4,5},{5,4},{6,7},{7,6},{8,9},{9,8},{10,11... | collective-permute-start | bytes 1572872 | tf_op jit(solution)/shard_map/ppermute | solution.py:26
  100.6 12.9 %collective-permute-start.13 = (bf16[2,256,256]{2,1,0:T(8,128)(2,1)S(1)}, bf16[2,256,256]{2,1,0:T(8,128)(2,1)S(1)}, u32[]{:S(2)}, u32[]{:S(2)}) collective-permute-start(bf16[2,256,256]{2,1,0:T(8,128)(2,1)S(1)} %fusion), channel_id=1, source_target_pairs={{2,0},{3,1},{4,2},{5,3},{6,4},{7,5},{8,6},{9,7},{10,8},{11,9},{12,... | collective-permute-start | bytes 786440 | tf_op jit(solution)/shard_map/ppermute | solution.py:22
  102.8 16.3 %collective-permute-start.16 = (bf16[2,256,256]{2,1,0:T(8,128)(2,1)S(1)}, bf16[2,256,256]{2,1,0:T(8,128)(2,1)S(1)}, u32[]{:S(2)}, u32[]{:S(2)}) collective-permute-start(bf16[2,256,256]{2,1,0:T(8,128)(2,1)S(1)} %fusion.1), channel_id=1, source_target_pairs={{2,0},{3,1},{4,2},{5,3},{6,4},{7,5},{8,6},{9,7},{10,8},{11,9},{12,... | collective-permute-start | bytes 786440 | tf_op jit(solution)/shard_map/ppermute | solution.py:22
  104.8 19.9 %collective-permute-start.19 = (bf16[2,256,256]{2,1,0:T(8,128)(2,1)S(1)}, bf16[2,256,256]{2,1,0:T(8,128)(2,1)S(1)}, u32[]{:S(2)}, u32[]{:S(2)}) collective-permute-start(bf16[2,256,256]{2,1,0:T(8,128)(2,1)S(1)} %fusion.2), channel_id=1, source_target_pairs={{2,0},{3,1},{4,2},{5,3},{6,4},{7,5},{8,6},{9,7},{10,8},{11,9},{12,... | collective-permute-start | bytes 786440 | tf_op jit(solution)/shard_map/ppermute | solution.py:22
  106.8 12.3 %copy-start.7 = (bf16[2,256,256]{2,1,0:T(8,128)(2,1)S(1)}, bf16[2,256,256]{2,1,0:T(8,128)(2,1)}, u32[]{:S(2)}) copy-start(bf16[2,256,256]{2,1,0:T(8,128)(2,1)} %get-tuple-element.42) | copy-start | bytes 786436
  106.9 23.5 %collective-permute-start.22 = (bf16[2,256,256]{2,1,0:T(8,128)(2,1)S(1)}, bf16[2,256,256]{2,1,0:T(8,128)(2,1)S(1)}, u32[]{:S(2)}, u32[]{:S(2)}) collective-permute-start(bf16[2,256,256]{2,1,0:T(8,128)(2,1)S(1)} %fusion.3), channel_id=1, source_target_pairs={{2,0},{3,1},{4,2},{5,3},{6,4},{7,5},{8,6},{9,7},{10,8},{11,9},{12,... | collective-permute-start | bytes 786440 | tf_op jit(solution)/shard_map/ppermute | solution.py:22
  113.5 11.2 %copy-start.8 = (bf16[2,256,256]{2,1,0:T(8,128)(2,1)S(1)}, bf16[2,256,256]{2,1,0:T(8,128)(2,1)}, u32[]{:S(2)}) copy-start(bf16[2,256,256]{2,1,0:T(8,128)(2,1)} %get-tuple-element.46) | copy-start | bytes 786436
  113.6 22.3 %collective-permute-start.14 = (bf16[2,256,256]{2,1,0:T(8,128)(2,1)S(1)}, bf16[2,256,256]{2,1,0:T(8,128)(2,1)S(1)}, u32[]{:S(2)}, u32[]{:S(2)}) collective-permute-start(bf16[2,256,256]{2,1,0:T(8,128)(2,1)S(1)} %add_convert_fusion.3), channel_id=1, source_target_pairs={{2,0},{3,1},{4,2},{5,3},{6,4},{7,5},{8,6},{9,7},{10,8},{11,9},{12,... | collective-permute-start | bytes 786440 | tf_op jit(solution)/shard_map/ppermute | solution.py:22
  119.1 11.2 %copy-start.9 = (bf16[2,256,256]{2,1,0:T(8,128)(2,1)S(1)}, bf16[2,256,256]{2,1,0:T(8,128)(2,1)}, u32[]{:S(2)}) copy-start(bf16[2,256,256]{2,1,0:T(8,128)(2,1)} %get-tuple-element.50) | copy-start | bytes 786436
  119.2 22.3 %collective-permute-start.17 = (bf16[2,256,256]{2,1,0:T(8,128)(2,1)S(1)}, bf16[2,256,256]{2,1,0:T(8,128)(2,1)S(1)}, u32[]{:S(2)}, u32[]{:S(2)}) collective-permute-start(bf16[2,256,256]{2,1,0:T(8,128)(2,1)S(1)} %add_convert_fusion.2), channel_id=1, source_target_pairs={{2,0},{3,1},{4,2},{5,3},{6,4},{7,5},{8,6},{9,7},{10,8},{11,9},{12,... | collective-permute-start | bytes 786440 | tf_op jit(solution)/shard_map/ppermute | solution.py:22
  124.9 22.3 %collective-permute-start.20 = (bf16[2,256,256]{2,1,0:T(8,128)(2,1)S(1)}, bf16[2,256,256]{2,1,0:T(8,128)(2,1)S(1)}, u32[]{:S(2)}, u32[]{:S(2)}) collective-permute-start(bf16[2,256,256]{2,1,0:T(8,128)(2,1)S(1)} %add_convert_fusion.1), channel_id=1, source_target_pairs={{2,0},{3,1},{4,2},{5,3},{6,4},{7,5},{8,6},{9,7},{10,8},{11,9},{12,... | collective-permute-start | bytes 786440 | tf_op jit(solution)/shard_map/ppermute | solution.py:22
  130.3 11.2 %copy-start.12 = (bf16[2,256,256]{2,1,0:T(8,128)(2,1)S(1)}, bf16[2,256,256]{2,1,0:T(8,128)(2,1)}, u32[]{:S(2)}) copy-start(bf16[2,256,256]{2,1,0:T(8,128)(2,1)} %get-tuple-element.43) | copy-start | bytes 786436
  130.5 22.1 %collective-permute-start.23 = (bf16[2,256,256]{2,1,0:T(8,128)(2,1)S(1)}, bf16[2,256,256]{2,1,0:T(8,128)(2,1)S(1)}, u32[]{:S(2)}, u32[]{:S(2)}) collective-permute-start(bf16[2,256,256]{2,1,0:T(8,128)(2,1)S(1)} %add_convert_fusion), channel_id=1, source_target_pairs={{2,0},{3,1},{4,2},{5,3},{6,4},{7,5},{8,6},{9,7},{10,8},{11,9},{12,... | collective-permute-start | bytes 786440 | tf_op jit(solution)/shard_map/ppermute | solution.py:22
  (12 other events, 72.9 us)

commit v4 on v3

--- a/solution.py
+++ b/solution.py
@@ -17,9 +17,8 @@
 
 
 def shift(block, axis, distance):
-    devices = range(lax.axis_size(axis))
-    route = [(i, i + distance) for i in devices if i + distance in devices]
-    return lax.ppermute(block, axis, route)
+    size = lax.axis_size(axis)
+    return lax.ppermute(block, axis, [(i, (i + distance) % size) for i in range(size)])
 
 
 def swap(block, axis):

time: 156 us -> 154 us (0.987)
  starting transfers between devices: 49.1 us -> 27.6 us
  waiting for transfers between devices: 42.8 us -> 60.3 us
    ppermute x16, starting transfers between devices: 47.3 us -> 25.6 us  [shift(): lax.ppermute(block, axis, [(i, (i + distance) % size) for i in range(size)])]
    ppermute x16, waiting for transfers between devices: 42.7 us -> 60.3 us  [shift(): lax.ppermute(block, axis, [(i, (i + distance) % size) for i in range(size)])]
  transfers between devices with their start and end apart: 24 -> 24, of which waited for: 11 -> 16; matrix products, arithmetic and copies ran while one was open for 15% -> 15% of each run, Pallas kernels for 22% -> 23%
where the time goes in v4:
time: 154 us; the launch traced here: 151 us
  waiting for transfers between devices  60.3 us (39%)
  Pallas kernels  34.6 us (22%)
  starting transfers between devices  27.6 us (18%)
  local copies, waits for them, and re-layouts  19.2 us (12%)
  other arithmetic  8.4 us (5%)
    ppermute x16, waiting for transfers between devices, shift(): lax.ppermute(block, axis, [(i, (i + distance) % size) for i in range(size)])  60.3 us
    pallas_call x4, Pallas kernels, attention(): pl.pallas_call(attention_kernel, grid=(groups,), in_specs=[pl.BlockSpec((...  34.6 us
    ppermute x16, starting transfers between devices, shift(): lax.ppermute(block, axis, [(i, (i + distance) % size) for i in range(size)])  25.6 us
    unnamed x47, local copies, waits for them, and re-layouts  8.19 us
    slice x4, local copies, waits for them, and re-layouts, forward_exchange(): return (back4, back13[:, rows:], back2, back13[:, :rows], own)  5.4 us
    select_n x4, other arithmetic, forward_exchange(): jnp.where(is_odd, jnp.concatenate([back2, back4], 1), jnp.concatenate([ow...  4.65 us
  transfers between devices with their start and end apart: 24, of which 16 were waited for; matrix products, arithmetic and copies ran while one was open for 15% of the time, Pallas kernels for 23%

profile of v4, /device:TPU:100, one launch (start us, length us, event | category | flops | bytes accessed | tf_op | source)
XLA Modules:
  0.0 151.2 jit_solution(9448368227921935906)
XLA Ops:
  2.1 3.2 %collective-permute-start.9 = (bf16[2,256,256]{2,1,0:T(8,128)(2,1)S(1)}, bf16[2,256,256]{2,1,0:T(8,128)(2,1)}, u32[]{:S(2)}, u32[]{:S(2)}) collective-permute-start(bf16[2,256,256]{2,1,0:T(8,128)(2,1)S(1)} %pad_maximum_fusion.3.p0_ref), channel_id=1, source_target_pairs={{0,2},{1,3},{2,4},{3,5},{4,6},{5,7},{6,8},{7,9},{8,10},{9,11},{10,... | collective-permute-start | bytes 786440 | tf_op jit(solution)/shard_map/ppermute | solution.py:21
  8.8 3.2 %collective-permute-done.9.p2_ref = bf16[2,256,256]{2,1,0:T(8,128)(2,1)} collective-permute-done((bf16[2,256,256]{2,1,0:T(8,128)(2,1)S(1)}, bf16[2,256,256]{2,1,0:T(8,128)(2,1)}, u32[]{:S(2)}, u32[]{:S(2)}) %collective-permute-start.9) | collective-permute-done | bytes 262176 | tf_op jit(solution)/shard_map/ppermute | solution.py:21
  12.0 3.8 %collective-permute-start.10 = (bf16[2,256,256]{2,1,0:T(8,128)(2,1)}, bf16[2,256,256]{2,1,0:T(8,128)(2,1)}, u32[]{:S(2)}, u32[]{:S(2)}) collective-permute-start(bf16[2,256,256]{2,1,0:T(8,128)(2,1)} %collective-permute-done.9.p2_ref), channel_id=1, source_target_pairs={{0,2},{1,3},{2,4},{3,5},{4,6},{5,7},{6,8},{7,9},{8,10},{9,11},{10,... | collective-permute-start | bytes 786440 | tf_op jit(solution)/shard_map/ppermute | solution.py:21
  17.7 3.7 %collective-permute-start.7 = (bf16[2,256,256]{2,1,0:T(8,128)(2,1)}, bf16[2,256,256]{2,1,0:T(8,128)(2,1)}, u32[]{:S(2)}, u32[]{:S(2)}) collective-permute-start(bf16[2,256,256]{2,1,0:T(8,128)(2,1)} %collective-permute-done.6.p2_ref), channel_id=1, source_target_pairs={{0,2},{1,3},{2,4},{3,5},{4,6},{5,7},{6,8},{7,9},{8,10},{9,11},{10,... | collective-permute-start | bytes 786440 | tf_op jit(solution)/shard_map/ppermute | solution.py:21
  21.4 1.9 %collective-permute-done.3.p2_ref = bf16[2,256,256]{2,1,0:T(8,128)(2,1)} collective-permute-done((bf16[2,256,256]{2,1,0:T(8,128)(2,1)}, bf16[2,256,256]{2,1,0:T(8,128)(2,1)}, u32[]{:S(2)}, u32[]{:S(2)}) %collective-permute-start.3) | collective-permute-done | bytes 262176 | tf_op jit(solution)/shard_map/ppermute | solution.py:21
  23.3 3.7 %collective-permute-start.4 = (bf16[2,256,256]{2,1,0:T(8,128)(2,1)}, bf16[2,256,256]{2,1,0:T(8,128)(2,1)}, u32[]{:S(2)}, u32[]{:S(2)}) collective-permute-start(bf16[2,256,256]{2,1,0:T(8,128)(2,1)} %collective-permute-done.3.p2_ref), channel_id=1, source_target_pairs={{0,2},{1,3},{2,4},{3,5},{4,6},{5,7},{6,8},{7,9},{8,10},{9,11},{10,... | collective-permute-start | bytes 786440 | tf_op jit(solution)/shard_map/ppermute | solution.py:21
  27.0 1.9 %collective-permute-done.10.p4_ref = bf16[2,256,256]{2,1,0:T(8,128)(2,1)} collective-permute-done((bf16[2,256,256]{2,1,0:T(8,128)(2,1)}, bf16[2,256,256]{2,1,0:T(8,128)(2,1)}, u32[]{:S(2)}, u32[]{:S(2)}) %collective-permute-start.10) | collective-permute-done | bytes 262176 | tf_op jit(solution)/shard_map/ppermute | solution.py:21
  28.9 2.0 %maximum_select_fusion.3 = bf16[2,512,256]{2,1,0:T(8,128)(2,1)} fusion(bf16[2,256,256]{2,1,0:T(8,128)(2,1)} %collective-permute-done.10.p4_ref, bf16[2,256,256]{2,1,0:T(8,128)(2,1)} %collective-permute-done.9.p2_ref, bf16[1,256,256]{2,1,0:T(8,128)(2,1)S(1)} %get-tuple-element.60, bf16[1,256,256]{2,1,0:T(8,128)(2,1)S(1)} %get-tuple-element.73, pred[]{:T(512)S(6)} %eq.5), kind=kLoop, calls=%fused_computation.18 | loop fusion | flops 2883584 | bytes 1310721 | tf_op jit(solution)/shard_map/jit(_where)/select_n | solution.py:114
  31.0 1.8 %copy_bitcast_fusion = (bf16[256,2048]{1,0:T(8,128)(2,1)}, bf16[256,2048]{1,0:T(8,128)(2,1)}) fusion(bf16[32,8,16,128]{3,2,1,0:T(8,128)(2,1)S(1)} %bitcast.49, bf16[32,8,16,128]{3,2,1,0:T(8,128)(2,1)S(1)} %bitcast.50), kind=kLoop, calls=%fused_computation.1 | loop fusion | bytes 4194304 | tf_op jit(solution)/shard_map/reshape | solution.py:146
  32.8 1.7 %collective-permute-done.p2_ref = bf16[2,256,256]{2,1,0:T(8,128)(2,1)S(1)} collective-permute-done((bf16[2,256,256]{2,1,0:T(8,128)(2,1)}, bf16[2,256,256]{2,1,0:T(8,128)(2,1)S(1)}, u32[]{:S(2)}, u32[]{:S(2)}) %collective-permute-start) | collective-permute-done | bytes 262176 | tf_op jit(solution)/shard_map/ppermute | solution.py:21
  34.6 3.6 %collective-permute-start.1 = (bf16[2,256,256]{2,1,0:T(8,128)(2,1)S(1)}, bf16[2,256,256]{2,1,0:T(8,128)(2,1)S(1)}, u32[]{:S(2)}, u32[]{:S(2)}) collective-permute-start(bf16[2,256,256]{2,1,0:T(8,128)(2,1)S(1)} %collective-permute-done.p2_ref), channel_id=1, source_target_pairs={{0,2},{1,3},{2,4},{3,5},{4,6},{5,7},{6,8},{7,9},{8,10},{9,11},{10,... | collective-permute-start | bytes 786440 | tf_op jit(solution)/shard_map/ppermute | solution.py:21
  40.2 1.2 maximum_select_fusion.2
  41.5 4.3 %collective-permute-done.4.p4_ref = bf16[2,256,256]{2,1,0:T(8,128)(2,1)} collective-permute-done((bf16[2,256,256]{2,1,0:T(8,128)(2,1)}, bf16[2,256,256]{2,1,0:T(8,128)(2,1)}, u32[]{:S(2)}, u32[]{:S(2)}) %collective-permute-start.4) | collective-permute-done | bytes 262176 | tf_op jit(solution)/shard_map/ppermute | solution.py:21
  45.8 1.2 maximum_select_fusion.1
  47.1 3.0 %collective-permute-done.1.p4_ref = bf16[2,256,256]{2,1,0:T(8,128)(2,1)S(1)} collective-permute-done((bf16[2,256,256]{2,1,0:T(8,128)(2,1)S(1)}, bf16[2,256,256]{2,1,0:T(8,128)(2,1)S(1)}, u32[]{:S(2)}, u32[]{:S(2)}) %collective-permute-start.1) | collective-permute-done | bytes 262176 | tf_op jit(solution)/shard_map/ppermute | solution.py:21
  51.4 1.9 %fusion.4 = (bf16[2,256,256]{2,1,0:T(8,128)(2,1)}, bf16[2,256,256]{2,1,0:T(8,128)(2,1)}) fusion(bf16[2,512,256]{2,1,0:T(8,128)(2,1)} %collective-permute-done.11), kind=kLoop, calls=%fused_computation.40 | loop fusion | bytes 1048576 | tf_op jit(solution)/shard_map/slice | solution.py:117
  55.4 8.6 %shard_map.84 = (bf16[256,2048]{1,0:T(8,128)(2,1)}, bf16[256,2048]{1,0:T(8,128)(2,1)}, bf16[2,512,256]{2,1,0:T(8,128)(2,1)}, bf16[2,256,256]{2,1,0:T(8,128)(2,1)...) custom-call(s32[256,1]{1,0:T(8,128)} %copy.20.qd_ref, ...), custom_call_target="tpu_custom_call", output_to_operand_aliasing={{0}: (9, {}), {1}: (10, {})} | custom-call | flops 2013265920 | bytes 3670016 | tf_op jit(solution)/shard_map/pallas_call | solution.py:80
  65.4 8.6 %shard_map.85 = (bf16[256,2048]{1,0:T(8,128)(2,1)}, bf16[256,2048]{1,0:T(8,128)(2,1)}, bf16[2,512,256]{2,1,0:T(8,128)(2,1)}, bf16[2,256,256]{2,1,0:T(8,128)(2,1)...) custom-call(s32[256,1]{1,0:T(8,128)} %copy.20.qd_ref, ...), custom_call_target="tpu_custom_call", output_to_operand_aliasing={{0}: (9, {}), {1}: (10, {})} | custom-call | flops 2013265920 | bytes 3670016 | tf_op jit(solution)/shard_map/pallas_call | solution.py:80
  74.2 1.9 %fusion.6 = (bf16[2,256,256]{2,1,0:T(8,128)(2,1)}, bf16[2,256,256]{2,1,0:T(8,128)(2,1)}) fusion(bf16[2,512,256]{2,1,0:T(8,128)(2,1)} %collective-permute-done.5), kind=kLoop, calls=%fused_computation.42 | loop fusion | bytes 1048576 | tf_op jit(solution)/shard_map/slice | solution.py:117
  76.0 8.7 %shard_map.86 = (bf16[256,2048]{1,0:T(8,128)(2,1)}, bf16[256,2048]{1,0:T(8,128)(2,1)}, bf16[2,512,256]{2,1,0:T(8,128)(2,1)}, bf16[2,256,256]{2,1,0:T(8,128)(2,1)...) custom-call(s32[256,1]{1,0:T(8,128)} %copy.20.qd_ref, ...), custom_call_target="tpu_custom_call", output_to_operand_aliasing={{0}: (9, {}), {1}: (10, {})} | custom-call | flops 2013265920 | bytes 3670016 | tf_op jit(solution)/shard_map/pallas_call | solution.py:80
  86.4 8.7 %shard_map.87 = (bf16[256,2048]{1,0:T(8,128)(2,1)}, bf16[256,2048]{1,0:T(8,128)(2,1)}, bf16[2,512,256]{2,1,0:T(8,128)(2,1)}, bf16[2,256,256]{2,1,0:T(8,128)(2,1)...) custom-call(s32[256,1]{1,0:T(8,128)} %copy.20.qd_ref, ...), custom_call_target="tpu_custom_call", output_to_operand_aliasing={{0}: (9, {}), {1}: (10, {})} | custom-call | flops 2013265920 | bytes 3670016 | tf_op jit(solution)/shard_map/pallas_call | solution.py:80
  95.2 2.5 %copy.25 = bf16[32,8,16,128]{3,2,1,0:T(8,128)(2,1)} copy(bf16[32,8,16,128]{3,1,2,0:T(8,128)(2,1)} %bitcast.43) | data formatting | bytes 2097152
  99.9 3.3 %collective-permute-start.19 = (bf16[2,256,256]{2,1,0:T(8,128)(2,1)S(1)}, bf16[2,256,256]{2,1,0:T(8,128)(2,1)S(1)}, u32[]{:S(2)}, u32[]{:S(2)}) collective-permute-start(bf16[2,256,256]{2,1,0:T(8,128)(2,1)S(1)} %fusion.2), channel_id=1, source_target_pairs={{0,14},{1,15},{2,0},{3,1},{4,2},{5,3},{6,4},{7,5},{8,6},{9,7},{10,... | collective-permute-start | bytes 786440 | tf_op jit(solution)/shard_map/ppermute | solution.py:21
  103.3 1.8 %collective-permute-start.22 = (bf16[2,256,256]{2,1,0:T(8,128)(2,1)S(1)}, bf16[2,256,256]{2,1,0:T(8,128)(2,1)S(1)}, u32[]{:S(2)}, u32[]{:S(2)}) collective-permute-start(bf16[2,256,256]{2,1,0:T(8,128)(2,1)S(1)} %fusion.3), channel_id=1, source_target_pairs={{0,14},{1,15},{2,0},{3,1},{4,2},{5,3},{6,4},{7,5},{8,6},{9,7},{10,... | collective-permute-start | bytes 786440 | tf_op jit(solution)/shard_map/ppermute | solution.py:21
  105.1 4.8 %collective-permute-done.13 = bf16[2,256,256]{2,1,0:T(8,128)(2,1)S(1)} collective-permute-done((bf16[2,256,256]{2,1,0:T(8,128)(2,1)S(1)}, bf16[2,256,256]{2,1,0:T(8,128)(2,1)S(1)}, u32[]{:S(2)}, u32[]{:S(2)}) %collective-permute-start.13) | collective-permute-done | bytes 262176 | tf_op jit(solution)/shard_map/ppermute | solution.py:21
  110.2 5.4 %collective-permute-done.16 = bf16[2,256,256]{2,1,0:T(8,128)(2,1)S(1)} collective-permute-done((bf16[2,256,256]{2,1,0:T(8,128)(2,1)S(1)}, bf16[2,256,256]{2,1,0:T(8,128)(2,1)S(1)}, u32[]{:S(2)}, u32[]{:S(2)}) %collective-permute-start.16) | collective-permute-done | bytes 262176 | tf_op jit(solution)/shard_map/ppermute | solution.py:21
  115.8 5.4 %collective-permute-done.19 = bf16[2,256,256]{2,1,0:T(8,128)(2,1)S(1)} collective-permute-done((bf16[2,256,256]{2,1,0:T(8,128)(2,1)S(1)}, bf16[2,256,256]{2,1,0:T(8,128)(2,1)S(1)}, u32[]{:S(2)}, u32[]{:S(2)}) %collective-permute-start.19) | collective-permute-done | bytes 262176 | tf_op jit(solution)/shard_map/ppermute | solution.py:21
  121.4 5.4 %collective-permute-done.22 = bf16[2,256,256]{2,1,0:T(8,128)(2,1)S(1)} collective-permute-done((bf16[2,256,256]{2,1,0:T(8,128)(2,1)S(1)}, bf16[2,256,256]{2,1,0:T(8,128)(2,1)S(1)}, u32[]{:S(2)}, u32[]{:S(2)}) %collective-permute-start.22) | collective-permute-done | bytes 262176 | tf_op jit(solution)/shard_map/ppermute | solution.py:21
  127.0 5.4 %collective-permute-done.14 = bf16[2,256,256]{2,1,0:T(8,128)(2,1)S(1)} collective-permute-done((bf16[2,256,256]{2,1,0:T(8,128)(2,1)S(1)}, bf16[2,256,256]{2,1,0:T(8,128)(2,1)S(1)}, u32[]{:S(2)}, u32[]{:S(2)}) %collective-permute-start.14) | collective-permute-done | bytes 262176 | tf_op jit(solution)/shard_map/ppermute | solution.py:21
  132.5 5.5 %collective-permute-done.17 = bf16[2,256,256]{2,1,0:T(8,128)(2,1)S(1)} collective-permute-done((bf16[2,256,256]{2,1,0:T(8,128)(2,1)S(1)}, bf16[2,256,256]{2,1,0:T(8,128)(2,1)S(1)}, u32[]{:S(2)}, u32[]{:S(2)}) %collective-permute-start.17) | collective-permute-done | bytes 262176 | tf_op jit(solution)/shard_map/ppermute | solution.py:21
  138.1 5.5 %collective-permute-done.20 = bf16[2,256,256]{2,1,0:T(8,128)(2,1)S(1)} collective-permute-done((bf16[2,256,256]{2,1,0:T(8,128)(2,1)S(1)}, bf16[2,256,256]{2,1,0:T(8,128)(2,1)S(1)}, u32[]{:S(2)}, u32[]{:S(2)}) %collective-permute-start.20) | collective-permute-done | bytes 262176 | tf_op jit(solution)/shard_map/ppermute | solution.py:21
  143.8 5.3 %collective-permute-done.23 = bf16[2,256,256]{2,1,0:T(8,128)(2,1)S(1)} collective-permute-done((bf16[2,256,256]{2,1,0:T(8,128)(2,1)S(1)}, bf16[2,256,256]{2,1,0:T(8,128)(2,1)S(1)}, u32[]{:S(2)}, u32[]{:S(2)}) %collective-permute-start.23) | collective-permute-done | bytes 262176 | tf_op jit(solution)/shard_map/ppermute | solution.py:21
  (100 shorter events, 21.3 us)
Async XLA Ops:
  2.1 13.7 %copy-start.10 = (bf16[2,256,256]{2,1,0:T(8,128)(2,1)}, bf16[2,256,256]{2,1,0:T(8,128)(2,1)S(1)}, u32[]{:S(2)}) copy-start(bf16[2,256,256]{2,1,0:T(8,128)(2,1)S(1)} %pad_maximum_fusion.3.p0_ref) | copy-start | bytes 786436
  2.1 9.9 %collective-permute-start.9 = (bf16[2,256,256]{2,1,0:T(8,128)(2,1)S(1)}, bf16[2,256,256]{2,1,0:T(8,128)(2,1)}, u32[]{:S(2)}, u32[]{:S(2)}) collective-permute-start(bf16[2,256,256]{2,1,0:T(8,128)(2,1)S(1)} %pad_maximum_fusion.3.p0_ref), channel_id=1, source_target_pairs={{0,2},{1,3},{2,4},{3,5},{4,6},{5,7},{6,8},{7,9},{8,10},{9,11},{10,... | collective-permute-start | bytes 786440 | tf_op jit(solution)/shard_map/ppermute | solution.py:21
  6.0 11.7 %collective-permute-start.6 = (bf16[2,256,256]{2,1,0:T(8,128)(2,1)}, bf16[2,256,256]{2,1,0:T(8,128)(2,1)}, u32[]{:S(2)}, u32[]{:S(2)}) collective-permute-start(bf16[2,256,256]{2,1,0:T(8,128)(2,1)} %pad_maximum_fusion.2.p0_ref), channel_id=1, source_target_pairs={{0,2},{1,3},{2,4},{3,5},{4,6},{5,7},{6,8},{7,9},{8,10},{9,11},{10,... | collective-permute-start | bytes 786440 | tf_op jit(solution)/shard_map/ppermute | solution.py:21
  7.0 23.9 %copy-start.2 = (bf16[256,16,128]{2,1,0:T(8,128)(2,1)S(1)}, bf16[256,16,128]{2,1,0:T(8,128)(2,1)}, u32[]{:S(2)}) copy-start(bf16[256,16,128]{2,1,0:T(8,128)(2,1)} %param.5) | copy-start | bytes 3145732
  7.8 23.2 %copy-start.1 = (bf16[256,16,128]{2,1,0:T(8,128)(2,1)S(1)}, bf16[256,16,128]{2,1,0:T(8,128)(2,1)}, u32[]{:S(2)}) copy-start(bf16[256,16,128]{2,1,0:T(8,128)(2,1)} %param.8) | copy-start | bytes 3145732
  7.8 15.6 %collective-permute-start.3 = (bf16[2,256,256]{2,1,0:T(8,128)(2,1)}, bf16[2,256,256]{2,1,0:T(8,128)(2,1)}, u32[]{:S(2)}, u32[]{:S(2)}) collective-permute-start(bf16[2,256,256]{2,1,0:T(8,128)(2,1)} %pad_maximum_fusion.1.p0_ref), channel_id=1, source_target_pairs={{0,2},{1,3},{2,4},{3,5},{4,6},{5,7},{6,8},{7,9},{8,10},{9,11},{10,... | collective-permute-start | bytes 786440 | tf_op jit(solution)/shard_map/ppermute | solution.py:21
  12.0 17.0 %collective-permute-start.10 = (bf16[2,256,256]{2,1,0:T(8,128)(2,1)}, bf16[2,256,256]{2,1,0:T(8,128)(2,1)}, u32[]{:S(2)}, u32[]{:S(2)}) collective-permute-start(bf16[2,256,256]{2,1,0:T(8,128)(2,1)} %collective-permute-done.9.p2_ref), channel_id=1, source_target_pairs={{0,2},{1,3},{2,4},{3,5},{4,6},{5,7},{6,8},{7,9},{8,10},{9,11},{10,... | collective-permute-start | bytes 786440 | tf_op jit(solution)/shard_map/ppermute | solution.py:21
  16.5 18.0 %collective-permute-start = (bf16[2,256,256]{2,1,0:T(8,128)(2,1)}, bf16[2,256,256]{2,1,0:T(8,128)(2,1)S(1)}, u32[]{:S(2)}, u32[]{:S(2)}) collective-permute-start(bf16[2,256,256]{2,1,0:T(8,128)(2,1)} %pad_maximum_fusion.p0_ref), channel_id=1, source_target_pairs={{0,2},{1,3},{2,4},{3,5},{4,6},{5,7},{6,8},{7,9},{8,10},{9,11},{10,... | collective-permute-start | bytes 786440 | tf_op jit(solution)/shard_map/ppermute | solution.py:21
  17.7 22.5 %collective-permute-start.7 = (bf16[2,256,256]{2,1,0:T(8,128)(2,1)}, bf16[2,256,256]{2,1,0:T(8,128)(2,1)}, u32[]{:S(2)}, u32[]{:S(2)}) collective-permute-start(bf16[2,256,256]{2,1,0:T(8,128)(2,1)} %collective-permute-done.6.p2_ref), channel_id=1, source_target_pairs={{0,2},{1,3},{2,4},{3,5},{4,6},{5,7},{6,8},{7,9},{8,10},{9,11},{10,... | collective-permute-start | bytes 786440 | tf_op jit(solution)/shard_map/ppermute | solution.py:21
  23.3 22.5 %collective-permute-start.4 = (bf16[2,256,256]{2,1,0:T(8,128)(2,1)}, bf16[2,256,256]{2,1,0:T(8,128)(2,1)}, u32[]{:S(2)}, u32[]{:S(2)}) collective-permute-start(bf16[2,256,256]{2,1,0:T(8,128)(2,1)} %collective-permute-done.3.p2_ref), channel_id=1, source_target_pairs={{0,2},{1,3},{2,4},{3,5},{4,6},{5,7},{6,8},{7,9},{8,10},{9,11},{10,... | collective-permute-start | bytes 786440 | tf_op jit(solution)/shard_map/ppermute | solution.py:21
  31.0 20.4 %collective-permute-start.11 = (bf16[2,512,256]{2,1,0:T(8,128)(2,1)}, bf16[2,512,256]{2,1,0:T(8,128)(2,1)}, u32[]{:S(2)}, u32[]{:S(2)}) collective-permute-start(bf16[2,512,256]{2,1,0:T(8,128)(2,1)} %maximum_select_fusion.3), channel_id=1, source_target_pairs={{0,1},{1,0},{2,3},{3,2},{4,5},{5,4},{6,7},{7,6},{8,9},{9,8},{10,11... | collective-permute-start | bytes 1572872 | tf_op jit(solution)/shard_map/ppermute | solution.py:25
  34.6 15.6 %copy-start.4 = (bf16[2,256,256]{2,1,0:T(8,128)(2,1)}, bf16[2,256,256]{2,1,0:T(8,128)(2,1)S(1)}, u32[]{:S(2)}) copy-start(bf16[2,256,256]{2,1,0:T(8,128)(2,1)S(1)} %collective-permute-done.p2_ref) | copy-start | bytes 786436
  34.6 15.6 %collective-permute-start.1 = (bf16[2,256,256]{2,1,0:T(8,128)(2,1)S(1)}, bf16[2,256,256]{2,1,0:T(8,128)(2,1)S(1)}, u32[]{:S(2)}, u32[]{:S(2)}) collective-permute-start(bf16[2,256,256]{2,1,0:T(8,128)(2,1)S(1)} %collective-permute-done.p2_ref), channel_id=1, source_target_pairs={{0,2},{1,3},{2,4},{3,5},{4,6},{5,7},{6,8},{7,9},{8,10},{9,11},{10,... | collective-permute-start | bytes 786440 | tf_op jit(solution)/shard_map/ppermute | solution.py:21
  41.4 23.2 %collective-permute-start.8 = (bf16[2,512,256]{2,1,0:T(8,128)(2,1)S(1)}, bf16[2,512,256]{2,1,0:T(8,128)(2,1)S(1)}, u32[]{:S(2)}, u32[]{:S(2)}) collective-permute-start(bf16[2,512,256]{2,1,0:T(8,128)(2,1)S(1)} %maximum_select_fusion.2), channel_id=1, source_target_pairs={{0,1},{1,0},{2,3},{3,2},{4,5},{5,4},{6,7},{7,6},{8,9},{9,8},{10,11... | collective-permute-start | bytes 1572872 | tf_op jit(solution)/shard_map/ppermute | solution.py:25
  47.0 27.1 %collective-permute-start.5 = (bf16[2,512,256]{2,1,0:T(8,128)(2,1)S(1)}, bf16[2,512,256]{2,1,0:T(8,128)(2,1)}, u32[]{:S(2)}, u32[]{:S(2)}) collective-permute-start(bf16[2,512,256]{2,1,0:T(8,128)(2,1)S(1)} %maximum_select_fusion.1), channel_id=1, source_target_pairs={{0,1},{1,0},{2,3},{3,2},{4,5},{5,4},{6,7},{7,6},{8,9},{9,8},{10,11... | collective-permute-start | bytes 1572872 | tf_op jit(solution)/shard_map/ppermute | solution.py:25
  51.1 34.4 %collective-permute-start.2 = (bf16[2,512,256]{2,1,0:T(8,128)(2,1)S(1)}, bf16[2,512,256]{2,1,0:T(8,128)(2,1)S(1)}, u32[]{:S(2)}, u32[]{:S(2)}) collective-permute-start(bf16[2,512,256]{2,1,0:T(8,128)(2,1)S(1)} %maximum_select_fusion), channel_id=1, source_target_pairs={{0,1},{1,0},{2,3},{3,2},{4,5},{5,4},{6,7},{7,6},{8,9},{9,8},{10,11... | collective-permute-start | bytes 1572872 | tf_op jit(solution)/shard_map/ppermute | solution.py:25
  64.0 34.9 %collective-permute-start.12 = (bf16[2,512,256]{2,1,0:T(8,128)(2,1)}, bf16[2,512,256]{2,1,0:T(8,128)(2,1)S(1)}, u32[]{:S(2)}, u32[]{:S(2)}) collective-permute-start(bf16[2,512,256]{2,1,0:T(8,128)(2,1)} %get-tuple-element.37), channel_id=1, source_target_pairs={{0,1},{1,0},{2,3},{3,2},{4,5},{5,4},{6,7},{7,6},{8,9},{9,8},{10,11... | collective-permute-start | bytes 1572872 | tf_op jit(solution)/shard_map/ppermute | solution.py:25
  74.1 25.0 %collective-permute-start.15 = (bf16[2,512,256]{2,1,0:T(8,128)(2,1)}, bf16[2,512,256]{2,1,0:T(8,128)(2,1)S(1)}, u32[]{:S(2)}, u32[]{:S(2)}) collective-permute-start(bf16[2,512,256]{2,1,0:T(8,128)(2,1)} %get-tuple-element.41), channel_id=1, source_target_pairs={{0,1},{1,0},{2,3},{3,2},{4,5},{5,4},{6,7},{7,6},{8,9},{9,8},{10,11... | collective-permute-start | bytes 1572872 | tf_op jit(solution)/shard_map/ppermute | solution.py:25
  84.7 14.6 %collective-permute-start.18 = (bf16[2,512,256]{2,1,0:T(8,128)(2,1)}, bf16[2,512,256]{2,1,0:T(8,128)(2,1)S(1)}, u32[]{:S(2)}, u32[]{:S(2)}) collective-permute-start(bf16[2,512,256]{2,1,0:T(8,128)(2,1)} %get-tuple-element.45), channel_id=1, source_target_pairs={{0,1},{1,0},{2,3},{3,2},{4,5},{5,4},{6,7},{7,6},{8,9},{9,8},{10,11... | collective-permute-start | bytes 1572872 | tf_op jit(solution)/shard_map/ppermute | solution.py:25
  95.1 8.2 %collective-permute-start.21 = (bf16[2,512,256]{2,1,0:T(8,128)(2,1)}, bf16[2,512,256]{2,1,0:T(8,128)(2,1)S(1)}, u32[]{:S(2)}, u32[]{:S(2)}) collective-permute-start(bf16[2,512,256]{2,1,0:T(8,128)(2,1)} %get-tuple-element.49), channel_id=1, source_target_pairs={{0,1},{1,0},{2,3},{3,2},{4,5},{5,4},{6,7},{7,6},{8,9},{9,8},{10,11... | collective-permute-start | bytes 1572872 | tf_op jit(solution)/shard_map/ppermute | solution.py:25
  99.0 10.9 %collective-permute-start.13 = (bf16[2,256,256]{2,1,0:T(8,128)(2,1)S(1)}, bf16[2,256,256]{2,1,0:T(8,128)(2,1)S(1)}, u32[]{:S(2)}, u32[]{:S(2)}) collective-permute-start(bf16[2,256,256]{2,1,0:T(8,128)(2,1)S(1)} %fusion), channel_id=1, source_target_pairs={{0,14},{1,15},{2,0},{3,1},{4,2},{5,3},{6,4},{7,5},{8,6},{9,7},{10,... | collective-permute-start | bytes 786440 | tf_op jit(solution)/shard_map/ppermute | solution.py:21
  99.2 16.3 %collective-permute-start.16 = (bf16[2,256,256]{2,1,0:T(8,128)(2,1)S(1)}, bf16[2,256,256]{2,1,0:T(8,128)(2,1)S(1)}, u32[]{:S(2)}, u32[]{:S(2)}) collective-permute-start(bf16[2,256,256]{2,1,0:T(8,128)(2,1)S(1)} %fusion.1), channel_id=1, source_target_pairs={{0,14},{1,15},{2,0},{3,1},{4,2},{5,3},{6,4},{7,5},{8,6},{9,7},{10,... | collective-permute-start | bytes 786440 | tf_op jit(solution)/shard_map/ppermute | solution.py:21
  99.9 21.2 %collective-permute-start.19 = (bf16[2,256,256]{2,1,0:T(8,128)(2,1)S(1)}, bf16[2,256,256]{2,1,0:T(8,128)(2,1)S(1)}, u32[]{:S(2)}, u32[]{:S(2)}) collective-permute-start(bf16[2,256,256]{2,1,0:T(8,128)(2,1)S(1)} %fusion.2), channel_id=1, source_target_pairs={{0,14},{1,15},{2,0},{3,1},{4,2},{5,3},{6,4},{7,5},{8,6},{9,7},{10,... | collective-permute-start | bytes 786440 | tf_op jit(solution)/shard_map/ppermute | solution.py:21
  103.2 12.3 %copy-start.7 = (bf16[2,256,256]{2,1,0:T(8,128)(2,1)S(1)}, bf16[2,256,256]{2,1,0:T(8,128)(2,1)}, u32[]{:S(2)}) copy-start(bf16[2,256,256]{2,1,0:T(8,128)(2,1)} %get-tuple-element.42) | copy-start | bytes 786436
  103.3 23.5 %collective-permute-start.22 = (bf16[2,256,256]{2,1,0:T(8,128)(2,1)S(1)}, bf16[2,256,256]{2,1,0:T(8,128)(2,1)S(1)}, u32[]{:S(2)}, u32[]{:S(2)}) collective-permute-start(bf16[2,256,256]{2,1,0:T(8,128)(2,1)S(1)} %fusion.3), channel_id=1, source_target_pairs={{0,14},{1,15},{2,0},{3,1},{4,2},{5,3},{6,4},{7,5},{8,6},{9,7},{10,... | collective-permute-start | bytes 786440 | tf_op jit(solution)/shard_map/ppermute | solution.py:21
  109.9 11.2 %copy-start.8 = (bf16[2,256,256]{2,1,0:T(8,128)(2,1)S(1)}, bf16[2,256,256]{2,1,0:T(8,128)(2,1)}, u32[]{:S(2)}) copy-start(bf16[2,256,256]{2,1,0:T(8,128)(2,1)} %get-tuple-element.46) | copy-start | bytes 786436
  110.1 22.3 %collective-permute-start.14 = (bf16[2,256,256]{2,1,0:T(8,128)(2,1)S(1)}, bf16[2,256,256]{2,1,0:T(8,128)(2,1)S(1)}, u32[]{:S(2)}, u32[]{:S(2)}) collective-permute-start(bf16[2,256,256]{2,1,0:T(8,128)(2,1)S(1)} %add_convert_fusion.3), channel_id=1, source_target_pairs={{0,14},{1,15},{2,0},{3,1},{4,2},{5,3},{6,4},{7,5},{8,6},{9,7},{10,... | collective-permute-start | bytes 786440 | tf_op jit(solution)/shard_map/ppermute | solution.py:21
  115.5 11.2 %copy-start.9 = (bf16[2,256,256]{2,1,0:T(8,128)(2,1)S(1)}, bf16[2,256,256]{2,1,0:T(8,128)(2,1)}, u32[]{:S(2)}) copy-start(bf16[2,256,256]{2,1,0:T(8,128)(2,1)} %get-tuple-element.50) | copy-start | bytes 786436
  115.7 22.3 %collective-permute-start.17 = (bf16[2,256,256]{2,1,0:T(8,128)(2,1)S(1)}, bf16[2,256,256]{2,1,0:T(8,128)(2,1)S(1)}, u32[]{:S(2)}, u32[]{:S(2)}) collective-permute-start(bf16[2,256,256]{2,1,0:T(8,128)(2,1)S(1)} %add_convert_fusion.2), channel_id=1, source_target_pairs={{0,14},{1,15},{2,0},{3,1},{4,2},{5,3},{6,4},{7,5},{8,6},{9,7},{10,... | collective-permute-start | bytes 786440 | tf_op jit(solution)/shard_map/ppermute | solution.py:21
  121.2 11.2 %copy-start.11 = (bf16[2,256,256]{2,1,0:T(8,128)(2,1)S(1)}, bf16[2,256,256]{2,1,0:T(8,128)(2,1)}, u32[]{:S(2)}) copy-start(bf16[2,256,256]{2,1,0:T(8,128)(2,1)} %get-tuple-element.39) | copy-start | bytes 786436
  121.3 22.3 %collective-permute-start.20 = (bf16[2,256,256]{2,1,0:T(8,128)(2,1)S(1)}, bf16[2,256,256]{2,1,0:T(8,128)(2,1)S(1)}, u32[]{:S(2)}, u32[]{:S(2)}) collective-permute-start(bf16[2,256,256]{2,1,0:T(8,128)(2,1)S(1)} %add_convert_fusion.1), channel_id=1, source_target_pairs={{0,14},{1,15},{2,0},{3,1},{4,2},{5,3},{6,4},{7,5},{8,6},{9,7},{10,... | collective-permute-start | bytes 786440 | tf_op jit(solution)/shard_map/ppermute | solution.py:21
  126.9 22.1 %collective-permute-start.23 = (bf16[2,256,256]{2,1,0:T(8,128)(2,1)S(1)}, bf16[2,256,256]{2,1,0:T(8,128)(2,1)S(1)}, u32[]{:S(2)}, u32[]{:S(2)}) collective-permute-start(bf16[2,256,256]{2,1,0:T(8,128)(2,1)S(1)} %add_convert_fusion), channel_id=1, source_target_pairs={{0,14},{1,15},{2,0},{3,1},{4,2},{5,3},{6,4},{7,5},{8,6},{9,7},{10,... | collective-permute-start | bytes 786440 | tf_op jit(solution)/shard_map/ppermute | solution.py:21
  (12 other events, 63.8 us)

commit v5 on v4

--- a/solution.py
+++ b/solution.py
@@ -7,7 +7,7 @@
 
 
 WINDOW = 1024
-CHUNKS = 4
+CHUNKS = 2
 
 
 QUERY_SCALE = 168.0 ** (-0.5)
@@ -25,8 +25,8 @@
     return lax.ppermute(block, axis, [(i, i ^ 1) for i in range(lax.axis_size(axis))])
 
 
-def attention_kernel(qd_ref, kd_ref, q_ref, g_ref, p4_ref, p3_ref, p2_ref, p1_ref, p0_ref,
-                     o_in, dq_in, o_ref, dq_ref, d13_ref, d4_ref, d2_ref, d0_ref):
+def attention_kernel(qd_ref, kd_ref, q_ref, g_ref, p4_ref, p3_ref, p2_ref, p1_ref, p0_ref, *refs):
+    o_ref, dq_ref, d13_ref, d4_ref, d2_ref, d0_ref = refs[-6:]
     rows = q_ref.shape[0]
     head_size = p0_ref.shape[2]
     pieces = (p4_ref, p3_ref, p2_ref, p1_ref, p0_ref)
@@ -66,7 +66,7 @@
         d0_ref[j] = term[4 * rows:5 * rows]
 
 
-def attention(q2, g2, pieces, q_docs, k_docs, head_size, chunk, o_buf, dq_buf):
+def attention(q2, g2, pieces, q_docs, k_docs, head_size, chunk, bufs):
     rows = q2.shape[0]
     groups = pieces[0].shape[2] // head_size
     per_group = 2 * head_size
@@ -85,7 +85,7 @@
             pl.BlockSpec((1, cols), lambda i: (0, 0)),
             q_spec,
             q_spec,
-        ] + [kv_spec] * len(pieces) + [pl.BlockSpec(memory_space=pl.ANY)] * 2,
+        ] + [kv_spec] * len(pieces) + [pl.BlockSpec(memory_space=pl.ANY)] * len(bufs),
         out_specs=[q_spec, q_spec, pair_spec, kv_spec, kv_spec, kv_spec],
         out_shape=[
             jax.ShapeDtypeStruct(q2.shape, jnp.bfloat16),
@@ -95,12 +95,12 @@
             piece_shape,
             piece_shape,
         ],
-        input_output_aliases={4 + len(pieces): 0, 5 + len(pieces): 1},
+        input_output_aliases={4 + len(pieces) + j: j for j in range(len(bufs))},
         compiler_params=pltpu.CompilerParams(dimension_semantics=("arbitrary",)),
         cost_estimate=pl.CostEstimate(
             flops=flops, transcendentals=rows * cols * per_group * groups // head_size,
             bytes_accessed=bytes_accessed),
-    )(q_docs, k_docs, q2, g2, *pieces, o_buf, dq_buf)
+    )(q_docs, k_docs, q2, g2, *pieces, *bufs)
 
 
 def wide(x):
@@ -141,21 +141,20 @@
     first_row = piece_pos * row_count
     q_docs = lax.dynamic_slice_in_dim(doc_ids, first_row, row_count, 0).reshape(row_count, 1)
     k_docs = lax.dynamic_slice_in_dim(pad_docs, first_row, WINDOW + row_count, 0).reshape(1, -1)
-
     q2 = query_heads.reshape(row_count, -1)
     g2 = grad_out.reshape(row_count, -1)
     k2 = key_heads.reshape(row_count, -1)
     v2 = value_heads.reshape(row_count, -1)
     kv_width = k2.shape[1] // CHUNKS
-    o_buf = jnp.zeros(q2.shape, jnp.bfloat16)
-    dq_buf = jnp.zeros(q2.shape, jnp.bfloat16)
+    bufs = ()
     totals = []
     for c in range(CHUNKS):
         lanes = slice(c * kv_width, (c + 1) * kv_width)
         own = jnp.stack([k2[:, lanes], v2[:, lanes]])
         pieces = forward_exchange(own, is_odd)
         o_buf, dq_buf, *terms = attention(
-            q2, g2, pieces, q_docs, k_docs, head_size, c, o_buf, dq_buf)
+            q2, g2, pieces, q_docs, k_docs, head_size, c, bufs)
+        bufs = (o_buf, dq_buf)
         totals.append(backward_exchange(terms, is_odd))
     attended = o_buf.reshape(query_heads.shape)
     grad_q = dq_buf.reshape(query_heads.shape)

time: 154 us -> 144 us (0.935)
  waiting for transfers between devices: 60.3 us -> 78.3 us
  starting transfers between devices: 27.6 us -> 13.1 us
  local copies, waits for them, and re-layouts: 19.2 us -> 13.4 us
  Pallas kernels: 34.6 us -> 30.5 us
  other arithmetic: 8.4 us -> 5.82 us
    ppermute x16 -> x8, waiting for transfers between devices: 60.3 us -> 75.7 us  [shift(): lax.ppermute(block, axis, [(i, (i + distance) % size) for i in range(size)])]
    ppermute x16 -> x8, starting transfers between devices: 25.6 us -> 12.1 us  [shift(): lax.ppermute(block, axis, [(i, (i + distance) % size) for i in range(size)])]
    pallas_call x4 -> x2, Pallas kernels: 34.6 us -> 30.5 us  [attention(): pl.pallas_call(attention_kernel, grid=(groups,), in_specs=[pl.BlockSpec((...]
    ppermute x8 -> x4, waiting for transfers between devices: 0.02 us -> 2.58 us  [swap(): lax.ppermute(block, axis, [(i, i ^ 1) for i in range(lax.axis_size(axis))])]
    another operation x2 -> x0, local copies, waits for them, and re-layouts: 2.2 us -> none
    slice x4 -> x2, local copies, waits for them, and re-layouts: 5.4 us -> 3.26 us  [forward_exchange(): return (back4, back13[:, rows:], back2, back13[:, :rows], own)]
    another operation x4 -> x2, other arithmetic: 2.23 us -> 0.1 us  [staged(): own = jnp.stack([k2[:, lanes], v2[:, lanes]])]
    unnamed x47 -> x37, local copies, waits for them, and re-layouts: 8.19 us -> 6.64 us
  transfers between devices with their start and end apart: 24 -> 12, of which waited for: 16 -> 9; matrix products, arithmetic and copies ran while one was open for 15% -> 10% of each run, Pallas kernels for 23% -> 22%
where the time goes in v5:
time: 144 us; the launch traced here: 142 us
  waiting for transfers between devices  78.3 us (54%)
  Pallas kernels  30.5 us (21%)
  local copies, waits for them, and re-layouts  13.4 us (9%)
  starting transfers between devices  13.1 us (9%)
  other arithmetic  5.82 us (4%)
    ppermute x8, waiting for transfers between devices, shift(): lax.ppermute(block, axis, [(i, (i + distance) % size) for i in range(size)])  75.7 us
    pallas_call x2, Pallas kernels, attention(): pl.pallas_call(attention_kernel, grid=(groups,), in_specs=[pl.BlockSpec((...  30.5 us
    ppermute x8, starting transfers between devices, shift(): lax.ppermute(block, axis, [(i, (i + distance) % size) for i in range(size)])  12.1 us
    unnamed x37, local copies, waits for them, and re-layouts  6.64 us
    select_n x2, other arithmetic, forward_exchange(): jnp.where(is_odd, jnp.concatenate([back2, back4], 1), jnp.concatenate([ow...  4.25 us
    slice x2, local copies, waits for them, and re-layouts, forward_exchange(): return (back4, back13[:, rows:], back2, back13[:, :rows], own)  3.26 us
  transfers between devices with their start and end apart: 12, of which 9 were waited for; matrix products, arithmetic and copies ran while one was open for 10% of the time, Pallas kernels for 22%

profile of v5, /device:TPU:100, one launch (start us, length us, event | category | flops | bytes accessed | tf_op | source)
XLA Modules:
  0.0 141.9 jit_solution(10308863767416921563)
XLA Ops:
  0.6 1.2 copy.25
  2.1 3.2 %collective-permute-start.3 = (bf16[2,256,512]{2,1,0:T(8,128)(2,1)S(1)}, bf16[2,256,512]{2,1,0:T(8,128)(2,1)S(1)}, u32[]{:S(2)}, u32[]{:S(2)}) collective-permute-start(bf16[2,256,512]{2,1,0:T(8,128)(2,1)S(1)} %pad_maximum_fusion.1.p0_ref), channel_id=1, source_target_pairs={{0,2},{1,3},{2,4},{3,5},{4,6},{5,7},{6,8},{7,9},{8,10},{9,11},{10,... | collective-permute-start | bytes 1572872 | tf_op jit(solution)/shard_map/ppermute | solution.py:21
  5.4 1.1 collective-permute-start
  6.5 11.2 %collective-permute-done.3.p2_ref = bf16[2,256,512]{2,1,0:T(8,128)(2,1)S(1)} collective-permute-done((bf16[2,256,512]{2,1,0:T(8,128)(2,1)S(1)}, bf16[2,256,512]{2,1,0:T(8,128)(2,1)S(1)}, u32[]{:S(2)}, u32[]{:S(2)}) %collective-permute-start.3) | collective-permute-done | bytes 524320 | tf_op jit(solution)/shard_map/ppermute | solution.py:21
  17.6 3.7 %collective-permute-start.4 = (bf16[2,256,512]{2,1,0:T(8,128)(2,1)S(1)}, bf16[2,256,512]{2,1,0:T(8,128)(2,1)}, u32[]{:S(2)}, u32[]{:S(2)}) collective-permute-start(bf16[2,256,512]{2,1,0:T(8,128)(2,1)S(1)} %collective-permute-done.3.p2_ref), channel_id=1, source_target_pairs={{0,2},{1,3},{2,4},{3,5},{4,6},{5,7},{6,8},{7,9},{8,10},{9,11},{10,... | collective-permute-start | bytes 1572872 | tf_op jit(solution)/shard_map/ppermute | solution.py:21
  21.3 7.5 %collective-permute-done.p2_ref = bf16[2,256,512]{2,1,0:T(8,128)(2,1)} collective-permute-done((bf16[2,256,512]{2,1,0:T(8,128)(2,1)S(1)}, bf16[2,256,512]{2,1,0:T(8,128)(2,1)}, u32[]{:S(2)}, u32[]{:S(2)}) %collective-permute-start) | collective-permute-done | bytes 524320 | tf_op jit(solution)/shard_map/ppermute | solution.py:21
  28.9 3.8 %collective-permute-start.1 = (bf16[2,256,512]{2,1,0:T(8,128)(2,1)}, bf16[2,256,512]{2,1,0:T(8,128)(2,1)}, u32[]{:S(2)}, u32[]{:S(2)}) collective-permute-start(bf16[2,256,512]{2,1,0:T(8,128)(2,1)} %collective-permute-done.p2_ref), channel_id=1, source_target_pairs={{0,2},{1,3},{2,4},{3,5},{4,6},{5,7},{6,8},{7,9},{8,10},{9,11},{10,... | collective-permute-start | bytes 1572872 | tf_op jit(solution)/shard_map/ppermute | solution.py:21
  32.7 7.4 %collective-permute-done.4.p4_ref = bf16[2,256,512]{2,1,0:T(8,128)(2,1)} collective-permute-done((bf16[2,256,512]{2,1,0:T(8,128)(2,1)S(1)}, bf16[2,256,512]{2,1,0:T(8,128)(2,1)}, u32[]{:S(2)}, u32[]{:S(2)}) %collective-permute-start.4) | collective-permute-done | bytes 524320 | tf_op jit(solution)/shard_map/ppermute | solution.py:21
  40.1 1.6 %maximum_select_fusion.1 = bf16[2,512,512]{2,1,0:T(8,128)(2,1)S(1)} fusion(bf16[2,256,512]{2,1,0:T(8,128)(2,1)} %collective-permute-done.4.p4_ref, bf16[2,256,512]{2,1,0:T(8,128)(2,1)} %copy-done.11, bf16[1,256,512]{2,1,0:T(8,128)(2,1)S(1)} %get-tuple-element.36, bf16[1,256,512]{2,1,0:T(8,128)(2,1)S(1)} %get-tuple-element.39, pred[]{:T(512)S(6)} %eq.5), kind=kLoop, calls=%fused_computation.8 | loop fusion | flops 5767168 | bytes 2621441 | tf_op jit(solution)/shard_map/jit(_where)/select_n | solution.py:114
  42.0 0.8 copy.12.qd_ref
  42.8 0.6 reshape.39.kd_ref
  43.4 6.9 %collective-permute-done.1.p4_ref = bf16[2,256,512]{2,1,0:T(8,128)(2,1)} collective-permute-done((bf16[2,256,512]{2,1,0:T(8,128)(2,1)}, bf16[2,256,512]{2,1,0:T(8,128)(2,1)}, u32[]{:S(2)}, u32[]{:S(2)}) %collective-permute-start.1) | collective-permute-done | bytes 524320 | tf_op jit(solution)/shard_map/ppermute | solution.py:21
  50.3 2.6 %maximum_select_fusion = bf16[2,512,512]{2,1,0:T(8,128)(2,1)} fusion(bf16[2,256,512]{2,1,0:T(8,128)(2,1)} %collective-permute-done.1.p4_ref, bf16[2,256,512]{2,1,0:T(8,128)(2,1)} %collective-permute-done.p2_ref, bf16[1,256,512]{2,1,0:T(8,128)(2,1)S(1)} %get-tuple-element.37, bf16[1,256,512]{2,1,0:T(8,128)(2,1)S(1)} %get-tuple-element.38, pred[]{:T(512)S(6)} %eq.5), kind=kLoop, calls=%fused_computation.7 | loop fusion | flops 5767168 | bytes 2621441 | tf_op jit(solution)/shard_map/jit(_where)/select_n | solution.py:114
  52.9 1.8 %copy_bitcast_fusion = (bf16[256,2048]{1,0:T(8,128)(2,1)}, bf16[256,2048]{1,0:T(8,128)(2,1)}) fusion(bf16[32,8,16,128]{3,2,1,0:T(8,128)(2,1)S(1)} %bitcast.41, bf16[32,8,16,128]{3,2,1,0:T(8,128)(2,1)S(1)} %bitcast.42), kind=kLoop, calls=%fused_computation.5 | loop fusion | bytes 4194304 | tf_op jit(solution)/shard_map/reshape | solution.py:145
  54.8 1.0 fusion.2
  55.8 15.2 %shard_map.84 = (bf16[256,2048]{1,0:T(8,128)(2,1)}, bf16[256,2048]{1,0:T(8,128)(2,1)}, bf16[2,512,512]{2,1,0:T(8,128)(2,1)}, bf16[2,256,512]{2,1,0:T(8,128)(2,1)...) custom-call(s32[256,1]{1,0:T(8,128)} %copy.12.qd_ref, s32[1,1280]{1,0:T(1,128)} %reshape.39.kd_ref, ...), custom_call_target="tpu_custom_call" | custom-call | flops 4026531840 | bytes 7340032 | tf_op jit(solution)/shard_map/pallas_call | solution.py:80
  71.0 0.8 collective-permute-start.6
  71.8 2.2 %fusion.3 = (bf16[2,256,512]{2,1,0:T(8,128)(2,1)}, bf16[2,256,512]{2,1,0:T(8,128)(2,1)}) fusion(bf16[2,512,512]{2,1,0:T(8,128)(2,1)} %collective-permute-done.2), kind=kLoop, calls=%fused_computation.25 | loop fusion | bytes 2097152 | tf_op jit(solution)/shard_map/slice | solution.py:117
  74.0 15.3 %shard_map.85 = (bf16[256,2048]{1,0:T(8,128)(2,1)}, bf16[256,2048]{1,0:T(8,128)(2,1)}, bf16[2,512,512]{2,1,0:T(8,128)(2,1)}, bf16[2,256,512]{2,1,0:T(8,128)(2,1)...) custom-call(s32[256,1]{1,0:T(8,128)} %copy.12.qd_ref, ...), custom_call_target="tpu_custom_call", output_to_operand_aliasing={{0}: (9, {}), {1}: (10, {})} | custom-call | flops 4026531840 | bytes 7340032 | tf_op jit(solution)/shard_map/pallas_call | solution.py:80
  89.7 2.6 %collective-permute-done.9 = bf16[2,512,512]{2,1,0:T(8,128)(2,1)S(1)} collective-permute-done((bf16[2,512,512]{2,1,0:T(8,128)(2,1)}, bf16[2,512,512]{2,1,0:T(8,128)(2,1)S(1)}, u32[]{:S(2)}, u32[]{:S(2)}) %collective-permute-start.9) | collective-permute-done | bytes 1048608 | tf_op jit(solution)/shard_map/ppermute | solution.py:25
  92.6 13.6 %collective-permute-done.7 = bf16[2,256,512]{2,1,0:T(8,128)(2,1)S(1)} collective-permute-done((bf16[2,256,512]{2,1,0:T(8,128)(2,1)S(1)}, bf16[2,256,512]{2,1,0:T(8,128)(2,1)S(1)}, u32[]{:S(2)}, u32[]{:S(2)}) %collective-permute-start.7) | collective-permute-done | bytes 524320 | tf_op jit(solution)/shard_map/ppermute | solution.py:21
  106.2 0.3 add_convert_fusion.1
  106.5 10.9 %collective-permute-done.10 = bf16[2,256,512]{2,1,0:T(8,128)(2,1)S(1)} collective-permute-done((bf16[2,256,512]{2,1,0:T(8,128)(2,1)S(1)}, bf16[2,256,512]{2,1,0:T(8,128)(2,1)S(1)}, u32[]{:S(2)}, u32[]{:S(2)}) %collective-permute-start.10) | collective-permute-done | bytes 524320 | tf_op jit(solution)/shard_map/ppermute | solution.py:21
  117.4 0.3 add_convert_fusion
  117.8 0.9 copy-done
  118.6 1.2 copy.17
  120.0 1.2 copy.18
  121.2 7.4 %collective-permute-done.8 = bf16[2,256,512]{2,1,0:T(8,128)(2,1)S(1)} collective-permute-done((bf16[2,256,512]{2,1,0:T(8,128)(2,1)S(1)}, bf16[2,256,512]{2,1,0:T(8,128)(2,1)S(1)}, u32[]{:S(2)}, u32[]{:S(2)}) %collective-permute-start.8) | collective-permute-done | bytes 524320 | tf_op jit(solution)/shard_map/ppermute | solution.py:21
  128.7 0.2 select_add_fusion.1
  128.9 10.8 %collective-permute-done.11 = bf16[2,256,512]{2,1,0:T(8,128)(2,1)S(1)} collective-permute-done((bf16[2,256,512]{2,1,0:T(8,128)(2,1)S(1)}, bf16[2,256,512]{2,1,0:T(8,128)(2,1)S(1)}, u32[]{:S(2)}, u32[]{:S(2)}) %collective-permute-start.11) | collective-permute-done | bytes 524320 | tf_op jit(solution)/shard_map/ppermute | solution.py:21
  140.1 0.9 copy.19
  141.0 0.9 copy.20
  (50 shorter events, 2.0 us)
Async XLA Ops:
  0.6 1.2 copy-start.6
  2.1 38.0 %copy-start.8 = (bf16[2,256,512]{2,1,0:T(8,128)(2,1)}, bf16[2,256,512]{2,1,0:T(8,128)(2,1)S(1)}, u32[]{:S(2)}) copy-start(bf16[2,256,512]{2,1,0:T(8,128)(2,1)S(1)} %pad_maximum_fusion.1.p0_ref) | copy-start | bytes 1572868
  2.1 15.5 %collective-permute-start.3 = (bf16[2,256,512]{2,1,0:T(8,128)(2,1)S(1)}, bf16[2,256,512]{2,1,0:T(8,128)(2,1)S(1)}, u32[]{:S(2)}, u32[]{:S(2)}) collective-permute-start(bf16[2,256,512]{2,1,0:T(8,128)(2,1)S(1)} %pad_maximum_fusion.1.p0_ref), channel_id=1, source_target_pairs={{0,2},{1,3},{2,4},{3,5},{4,6},{5,7},{6,8},{7,9},{8,10},{9,11},{10,... | collective-permute-start | bytes 1572872 | tf_op jit(solution)/shard_map/ppermute | solution.py:21
  5.4 36.4 %copy-start.7 = (bf16[2,256,512]{2,1,0:T(8,128)(2,1)}, bf16[2,256,512]{2,1,0:T(8,128)(2,1)S(1)}, u32[]{:S(2)}) copy-start(bf16[2,256,512]{2,1,0:T(8,128)(2,1)S(1)} %pad_maximum_fusion.p0_ref) | copy-start | bytes 1572868
  5.4 23.5 %collective-permute-start = (bf16[2,256,512]{2,1,0:T(8,128)(2,1)S(1)}, bf16[2,256,512]{2,1,0:T(8,128)(2,1)}, u32[]{:S(2)}, u32[]{:S(2)}) collective-permute-start(bf16[2,256,512]{2,1,0:T(8,128)(2,1)S(1)} %pad_maximum_fusion.p0_ref), channel_id=1, source_target_pairs={{0,2},{1,3},{2,4},{3,5},{4,6},{5,7},{6,8},{7,9},{8,10},{9,11},{10,... | collective-permute-start | bytes 1572872 | tf_op jit(solution)/shard_map/ppermute | solution.py:21
  17.6 15.0 %copy-start.11 = (bf16[2,256,512]{2,1,0:T(8,128)(2,1)}, bf16[2,256,512]{2,1,0:T(8,128)(2,1)S(1)}, u32[]{:S(2)}) copy-start(bf16[2,256,512]{2,1,0:T(8,128)(2,1)S(1)} %collective-permute-done.3.p2_ref) | copy-start | bytes 1572868
  17.6 22.5 %collective-permute-start.4 = (bf16[2,256,512]{2,1,0:T(8,128)(2,1)S(1)}, bf16[2,256,512]{2,1,0:T(8,128)(2,1)}, u32[]{:S(2)}, u32[]{:S(2)}) collective-permute-start(bf16[2,256,512]{2,1,0:T(8,128)(2,1)S(1)} %collective-permute-done.3.p2_ref), channel_id=1, source_target_pairs={{0,2},{1,3},{2,4},{3,5},{4,6},{5,7},{6,8},{7,9},{8,10},{9,11},{10,... | collective-permute-start | bytes 1572872 | tf_op jit(solution)/shard_map/ppermute | solution.py:21
  28.9 21.4 %collective-permute-start.1 = (bf16[2,256,512]{2,1,0:T(8,128)(2,1)}, bf16[2,256,512]{2,1,0:T(8,128)(2,1)}, u32[]{:S(2)}, u32[]{:S(2)}) collective-permute-start(bf16[2,256,512]{2,1,0:T(8,128)(2,1)} %collective-permute-done.p2_ref), channel_id=1, source_target_pairs={{0,2},{1,3},{2,4},{3,5},{4,6},{5,7},{6,8},{7,9},{8,10},{9,11},{10,... | collective-permute-start | bytes 1572872 | tf_op jit(solution)/shard_map/ppermute | solution.py:21
  32.7 9.2 %copy-start.14 = (s32[4096]{0:T(1024)S(1)}, s32[4096]{0:T(1024)}, u32[]{:S(2)}) copy-start(s32[4096]{0:T(1024)} %param.9) | copy-start | bytes 49156
  41.8 13.0 %collective-permute-start.5 = (bf16[2,512,512]{2,1,0:T(8,128)(2,1)S(1)}, bf16[2,512,512]{2,1,0:T(8,128)(2,1)S(1)}, u32[]{:S(2)}, u32[]{:S(2)}) collective-permute-start(bf16[2,512,512]{2,1,0:T(8,128)(2,1)S(1)} %maximum_select_fusion.1), channel_id=1, source_target_pairs={{0,1},{1,0},{2,3},{3,2},{4,5},{5,4},{6,7},{7,6},{8,9},{9,8},{10,11... | collective-permute-start | bytes 3145736 | tf_op jit(solution)/shard_map/ppermute | solution.py:25
  43.4 9.5 %copy-start.2 = (bf16[256,16,128]{2,1,0:T(8,128)(2,1)S(1)}, bf16[256,16,128]{2,1,0:T(8,128)(2,1)}, u32[]{:S(2)}) copy-start(bf16[256,16,128]{2,1,0:T(8,128)(2,1)} %param.8) | copy-start | bytes 3145732
  43.4 9.5 %copy-start.3 = (bf16[256,16,128]{2,1,0:T(8,128)(2,1)S(1)}, bf16[256,16,128]{2,1,0:T(8,128)(2,1)}, u32[]{:S(2)}) copy-start(bf16[256,16,128]{2,1,0:T(8,128)(2,1)} %param.5) | copy-start | bytes 3145732
  52.9 18.9 %collective-permute-start.2 = (bf16[2,512,512]{2,1,0:T(8,128)(2,1)}, bf16[2,512,512]{2,1,0:T(8,128)(2,1)}, u32[]{:S(2)}, u32[]{:S(2)}) collective-permute-start(bf16[2,512,512]{2,1,0:T(8,128)(2,1)} %maximum_select_fusion), channel_id=1, source_target_pairs={{0,1},{1,0},{2,3},{3,2},{4,5},{5,4},{6,7},{7,6},{8,9},{9,8},{10,11... | collective-permute-start | bytes 3145736 | tf_op jit(solution)/shard_map/ppermute | solution.py:25
  71.0 18.4 %collective-permute-start.6 = (bf16[2,512,512]{2,1,0:T(8,128)(2,1)}, bf16[2,512,512]{2,1,0:T(8,128)(2,1)S(1)}, u32[]{:S(2)}, u32[]{:S(2)}) collective-permute-start(bf16[2,512,512]{2,1,0:T(8,128)(2,1)} %get-tuple-element.21), channel_id=1, source_target_pairs={{0,1},{1,0},{2,3},{3,2},{4,5},{5,4},{6,7},{7,6},{8,9},{9,8},{10,11... | collective-permute-start | bytes 3145736 | tf_op jit(solution)/shard_map/ppermute | solution.py:25
  74.0 15.4 %copy-start.9 = (bf16[2,256,512]{2,1,0:T(8,128)(2,1)S(1)}, bf16[2,256,512]{2,1,0:T(8,128)(2,1)}, u32[]{:S(2)}) copy-start(bf16[2,256,512]{2,1,0:T(8,128)(2,1)} %get-tuple-element.20) | copy-start | bytes 1572868
  89.3 3.0 %copy-start.10 = (bf16[2,256,512]{2,1,0:T(8,128)(2,1)S(1)}, bf16[2,256,512]{2,1,0:T(8,128)(2,1)}, u32[]{:S(2)}) copy-start(bf16[2,256,512]{2,1,0:T(8,128)(2,1)} %get-tuple-element.24) | copy-start | bytes 1572868
  89.4 3.0 %collective-permute-start.9 = (bf16[2,512,512]{2,1,0:T(8,128)(2,1)}, bf16[2,512,512]{2,1,0:T(8,128)(2,1)S(1)}, u32[]{:S(2)}, u32[]{:S(2)}) collective-permute-start(bf16[2,512,512]{2,1,0:T(8,128)(2,1)} %get-tuple-element.25), channel_id=1, source_target_pairs={{0,1},{1,0},{2,3},{3,2},{4,5},{5,4},{6,7},{7,6},{8,9},{9,8},{10,11... | collective-permute-start | bytes 3145736 | tf_op jit(solution)/shard_map/ppermute | solution.py:25
  89.6 16.5 %copy-start.12 = (bf16[2,256,512]{2,1,0:T(8,128)(2,1)S(1)}, bf16[2,256,512]{2,1,0:T(8,128)(2,1)}, u32[]{:S(2)}) copy-start(bf16[2,256,512]{2,1,0:T(8,128)(2,1)} %get-tuple-element.22) | copy-start | bytes 1572868
  89.6 16.5 %collective-permute-start.7 = (bf16[2,256,512]{2,1,0:T(8,128)(2,1)S(1)}, bf16[2,256,512]{2,1,0:T(8,128)(2,1)S(1)}, u32[]{:S(2)}, u32[]{:S(2)}) collective-permute-start(bf16[2,256,512]{2,1,0:T(8,128)(2,1)S(1)} %fusion), channel_id=1, source_target_pairs={{0,14},{1,15},{2,0},{3,1},{4,2},{5,3},{6,4},{7,5},{8,6},{9,7},{10,... | collective-permute-start | bytes 1572872 | tf_op jit(solution)/shard_map/ppermute | solution.py:21
  92.5 24.9 %collective-permute-start.10 = (bf16[2,256,512]{2,1,0:T(8,128)(2,1)S(1)}, bf16[2,256,512]{2,1,0:T(8,128)(2,1)S(1)}, u32[]{:S(2)}, u32[]{:S(2)}) collective-permute-start(bf16[2,256,512]{2,1,0:T(8,128)(2,1)S(1)} %fusion.1), channel_id=1, source_target_pairs={{0,14},{1,15},{2,0},{3,1},{4,2},{5,3},{6,4},{7,5},{8,6},{9,7},{10,... | collective-permute-start | bytes 1572872 | tf_op jit(solution)/shard_map/ppermute | solution.py:21
  106.2 11.2 %copy-start.13 = (bf16[2,256,512]{2,1,0:T(8,128)(2,1)S(1)}, bf16[2,256,512]{2,1,0:T(8,128)(2,1)}, u32[]{:S(2)}) copy-start(bf16[2,256,512]{2,1,0:T(8,128)(2,1)} %get-tuple-element.26) | copy-start | bytes 1572868
  106.5 22.2 %collective-permute-start.8 = (bf16[2,256,512]{2,1,0:T(8,128)(2,1)S(1)}, bf16[2,256,512]{2,1,0:T(8,128)(2,1)S(1)}, u32[]{:S(2)}, u32[]{:S(2)}) collective-permute-start(bf16[2,256,512]{2,1,0:T(8,128)(2,1)S(1)} %add_convert_fusion.1), channel_id=1, source_target_pairs={{0,14},{1,15},{2,0},{3,1},{4,2},{5,3},{6,4},{7,5},{8,6},{9,7},{10,... | collective-permute-start | bytes 1572872 | tf_op jit(solution)/shard_map/ppermute | solution.py:21
  117.4 1.2 copy-start
  117.7 22.0 %collective-permute-start.11 = (bf16[2,256,512]{2,1,0:T(8,128)(2,1)S(1)}, bf16[2,256,512]{2,1,0:T(8,128)(2,1)S(1)}, u32[]{:S(2)}, u32[]{:S(2)}) collective-permute-start(bf16[2,256,512]{2,1,0:T(8,128)(2,1)S(1)} %add_convert_fusion), channel_id=1, source_target_pairs={{0,14},{1,15},{2,0},{3,1},{4,2},{5,3},{6,4},{7,5},{8,6},{9,7},{10,... | collective-permute-start | bytes 1572872 | tf_op jit(solution)/shard_map/ppermute | solution.py:21
  118.6 1.4 copy-start.1
  120.0 8.6 %copy-start.4 = (bf16[2,256,512]{2,1,0:T(8,128)(2,1)S(1)}, bf16[2,256,512]{2,1,0:T(8,128)(2,1)}, u32[]{:S(2)}) copy-start(bf16[2,256,512]{2,1,0:T(8,128)(2,1)} %get-tuple-element.23) | copy-start | bytes 1572868
  128.7 11.0 %copy-start.5 = (bf16[2,256,512]{2,1,0:T(8,128)(2,1)S(1)}, bf16[2,256,512]{2,1,0:T(8,128)(2,1)}, u32[]{:S(2)}) copy-start(bf16[2,256,512]{2,1,0:T(8,128)(2,1)} %get-tuple-element.27) | copy-start | bytes 1572868

commit v6 on v5

v6 whole, which is shorter than its diff:
```python
import jax
import jax.numpy as jnp
from jax import lax
from jax.experimental import pallas as pl
from jax.experimental.pallas import tpu as pltpu
from jax.sharding import PartitionSpec as P


WINDOW = 1024
CHUNKS = 2


QUERY_SCALE = 168.0 ** (-0.5)

NT = (((1,), (1,)), ((), ()))
TN = (((0,), (0,)), ((), ()))


def shift(block, axis, distance):
    size = lax.axis_size(axis)
    return lax.ppermute(block, axis, [(i, (i + distance) % size) for i in range(size)])


def swap(block, axis):
    return lax.ppermute(block, axis, [(i, i ^ 1) for i in range(lax.axis_size(axis))])


def attention_kernel(flags_ref, qd_ref, kd_ref, q_ref, g_ref, p4_ref, p3_ref, p2_ref, p1_ref,
                     p0_ref, *refs):
    o_ref, dq_ref, d13_ref, d4_ref, d2_ref, d0_ref, s_scr, wb_scr, dk_scr, dv_scr = refs[-10:]
    rows = q_ref.shape[0]
    head_size = p0_ref.shape[2]
    pieces = (p4_ref, p3_ref, p2_ref, p1_ref, p0_ref)
    last = len(pieces) - 1
    dk_scr[...] = jnp.zeros_like(dk_scr)
    dv_scr[...] = jnp.zeros_like(dv_scr)

    def mask(j):
        allowed = qd_ref[...] == kd_ref[:, j * rows:(j + 1) * rows]
        q_pos = lax.broadcasted_iota(jnp.int32, (rows, rows), 0)
        k_pos = lax.broadcasted_iota(jnp.int32, (rows, rows), 1)
        if j == 0:
            allowed = allowed & (k_pos > q_pos)
        if j == last:
            allowed = allowed & (k_pos <= q_pos)
        return allowed

    def when(j, fn, keep):
        if j == last:
            return fn()
        return lax.cond(flags_ref[j] != 0, fn, lambda: keep)

    for a in range(q_ref.shape[1] // head_size):
        lanes = slice(a * head_size, (a + 1) * head_size)
        q = q_ref[:, lanes]
        g = g_ref[:, lanes]

        row_max = jnp.full((rows, 1), -jnp.inf, jnp.float32)
        for j in range(len(pieces)):
            def scores_of(j=j, row_max=row_max):
                scores = QUERY_SCALE * lax.dot_general(
                    q, pieces[j][0], NT, preferred_element_type=jnp.float32)
                masked = jnp.where(mask(j), scores, -jnp.inf)
                s_scr[j] = masked
                return jnp.maximum(row_max, jnp.max(masked, axis=1, keepdims=True))
            row_max = when(j, scores_of, row_max)

        total = jnp.zeros((rows, 1), jnp.float32)
        for j in range(len(pieces)):
            def exp_of(j=j, total=total):
                unnorm = jnp.exp(s_scr[j] - row_max)
                s_scr[j] = unnorm
                return total + jnp.sum(unnorm, axis=1, keepdims=True)
            total = when(j, exp_of, total)
        inv = 1.0 / total

        out = jnp.zeros((rows, head_size), jnp.float32)
        for j in range(len(pieces)):
            def attend(j=j, out=out):
                weights = s_scr[j] * inv
                s_scr[j] = weights
                weights_b = weights.astype(jnp.bfloat16)
                wb_scr[j] = weights_b
                return out + jnp.dot(weights_b, pieces[j][1], preferred_element_type=jnp.float32)
            out = when(j, attend, out)
        attended = out.astype(jnp.bfloat16)
        o_ref[:, lanes] = attended
        row_dot = jnp.sum(g.astype(jnp.float32) * attended.astype(jnp.float32), axis=1, keepdims=True)

        dq = jnp.zeros((rows, head_size), jnp.float32)
        for j in range(len(pieces)):
            def grads(j=j, dq=dq):
                dprob = lax.dot_general(g, pieces[j][1], NT, preferred_element_type=jnp.float32)
                dscore = (s_scr[j] * (dprob - row_dot)).astype(jnp.bfloat16)
                dk_scr[j] += lax.dot_general(dscore, q, TN, preferred_element_type=jnp.float32)
                dv_scr[j] += lax.dot_general(wb_scr[j], g, TN, preferred_element_type=jnp.float32)
                return dq + jnp.dot(dscore, pieces[j][0], preferred_element_type=jnp.float32)
            dq = when(j, grads, dq)
        dq_ref[:, lanes] = (QUERY_SCALE * dq).astype(jnp.bfloat16)

    for j, scr in enumerate((dk_scr, dv_scr)):
        scale = QUERY_SCALE if j == 0 else 1.0
        d4_ref[j] = (scale * scr[0]).astype(jnp.bfloat16)
        d13_ref[j, rows:2 * rows] = (scale * scr[1]).astype(jnp.bfloat16)
        d2_ref[j] = (scale * scr[2]).astype(jnp.bfloat16)
        d13_ref[j, 0:rows] = (scale * scr[3]).astype(jnp.bfloat16)
        d0_ref[j] = (scale * scr[4]).astype(jnp.bfloat16)


def attention(q2, g2, pieces, q_docs, k_docs, flags, head_size, chunk, bufs):
    rows = q2.shape[0]
    groups = pieces[0].shape[2] // head_size
    per_group = 2 * head_size
    cols = rows * len(pieces)
    q_spec = pl.BlockSpec((rows, per_group), lambda i, f: (0, chunk * groups + i))
    kv_spec = pl.BlockSpec((2, rows, head_size), lambda i, f: (0, 0, i))
    pair_spec = pl.BlockSpec((2, 2 * rows, head_size), lambda i, f: (0, 0, i))
    piece_shape = jax.ShapeDtypeStruct(pieces[0].shape, jnp.bfloat16)
    flops = 12 * rows * cols * per_group * groups
    bytes_accessed = 2 * (4 * rows * per_group * groups + 10 * pieces[0].size)
    return pl.pallas_call(
        attention_kernel,
        grid_spec=pltpu.PrefetchScalarGridSpec(
            num_scalar_prefetch=1,
            grid=(groups,),
            in_specs=[
                pl.BlockSpec((rows, 1), lambda i, f: (0, 0)),
                pl.BlockSpec((1, cols), lambda i, f: (0, 0)),
                q_spec,
                q_spec,
            ] + [kv_spec] * len(pieces) + [pl.BlockSpec(memory_space=pl.ANY)] * len(bufs),
            out_specs=[q_spec, q_spec, pair_spec, kv_spec, kv_spec, kv_spec],
            scratch_shapes=[
                pltpu.VMEM((len(pieces), rows, rows), jnp.float32),
                pltpu.VMEM((len(pieces), rows, rows), jnp.bfloat16),
                pltpu.VMEM((len(pieces), rows, head_size), jnp.float32),
                pltpu.VMEM((len(pieces), rows, head_size), jnp.float32),
            ],
        ),
        out_shape=[
            jax.ShapeDtypeStruct(q2.shape, jnp.bfloat16),
            jax.ShapeDtypeStruct(q2.shape, jnp.bfloat16),
            jax.ShapeDtypeStruct((2, 2 * rows, pieces[0].shape[2]), jnp.bfloat16),
            piece_shape,
            piece_shape,
            piece_shape,
        ],
        input_output_aliases={5 + len(pieces) + j: j for j in range(len(bufs))},
        compiler_params=pltpu.CompilerParams(dimension_semantics=("arbitrary",)),
        cost_estimate=pl.CostEstimate(
            flops=flops, transcendentals=rows * cols * per_group * groups // head_size,
            bytes_accessed=bytes_accessed),
    )(flags, q_docs, k_docs, q2, g2, *pieces, *bufs)


def wide(x):
    return x.astype(jnp.float32)


def forward_exchange(own, is_odd):
    rows = own.shape[1]
    back2 = shift(own, "ctx", 2)
    back4 = shift(back2, "ctx", 2)
    odd_pieces = jnp.where(is_odd, jnp.concatenate([back2, back4], 1),
                           jnp.concatenate([own, back2], 1))
    back13 = swap(odd_pieces, "ctx")
    return (back4, back13[:, rows:], back2, back13[:, :rows], own)


def backward_exchange(terms, is_odd):
    t13, t4, t2, t0 = terms
    rows = t4.shape[1]
    s13 = swap(t13, "ctx")
    s1 = s13[:, :rows]
    s3 = s13[:, rows:]
    first = jnp.where(is_odd, wide(t4) + wide(s3), wide(t4)).astype(jnp.bfloat16)
    got1 = shift(first, "ctx", -2)
    second = (wide(got1) + wide(t2) + wide(jnp.where(is_odd, s1, s3))).astype(jnp.bfloat16)
    got2 = shift(second, "ctx", -2)
    return wide(got2) + wide(t0) + jnp.where(is_odd, 0.0, wide(s1))


def staged(query_heads, key_heads, value_heads, grad_out, doc_ids):
    row_count = query_heads.shape[0]
    head_size = key_heads.shape[2]
    assert WINDOW // row_count == 4
    piece_pos = lax.axis_index("ctx")
    is_odd = piece_pos % 2 == 1

    pad_docs = jnp.concatenate([jnp.full((WINDOW,), -1, jnp.int32), doc_ids], 0)
    first_row = piece_pos * row_count
    q_docs = lax.dynamic_slice_in_dim(doc_ids, first_row, row_count, 0).reshape(row_count, 1)
    k_docs = lax.dynamic_slice_in_dim(pad_docs, first_row, WINDOW + row_count, 0).reshape(1, -1)
    ends = k_docs[0, row_count - 1:WINDOW:row_count]
    flags = (ends == q_docs[0, 0]).astype(jnp.int32)
    q2 = query_heads.reshape(row_count, -1)
    g2 = grad_out.reshape(row_count, -1)
    k2 = key_heads.reshape(row_count, -1)
    v2 = value_heads.reshape(row_count, -1)
    kv_width = k2.shape[1] // CHUNKS
    bufs = ()
    totals = []
    for c in range(CHUNKS):
        lanes = slice(c * kv_width, (c + 1) * kv_width)
        own = jnp.stack([k2[:, lanes], v2[:, lanes]])
        pieces = forward_exchange(own, is_odd)
        o_buf, dq_buf, *terms = attention(
            q2, g2, pieces, q_docs, k_docs, flags, head_size, c, bufs)
        bufs = (o_buf, dq_buf)
        totals.append(backward_exchange(terms, is_odd))
    attended = o_buf.reshape(query_heads.shape)
    grad_q = dq_buf.reshape(query_heads.shape)
    total = jnp.concatenate(totals, 2)
    grad_k = total[0].astype(jnp.bfloat16).reshape(key_heads.shape)
    grad_v = total[1].astype(jnp.bfloat16).reshape(value_heads.shape)
    return (attended, grad_q, grad_k, grad_v)


def solution(mesh):
    placed = (
        P(("dp", "ctx"), None, None),
        P(("dp", "ctx"), None, None),
        P(("dp", "ctx"), None, None),
        P(("dp", "ctx"), None, None),
        P("dp"),
    )
    return jax.shard_map(
        staged,
        mesh=mesh,
        in_specs=placed,
        out_specs=(
            P(("dp", "ctx"), None, None),
            P(("dp", "ctx"), None, None),
            P(("dp", "ctx"), None, None),
            P(("dp", "ctx"), None, None),
        ),
        check_vma=False,
    )
```

time: 144 us -> 210 us (1.46)
  Pallas kernels: 30.5 us -> 97.3 us
    pallas_call x2, Pallas kernels: 30.5 us -> 97.3 us  [attention(): pl.pallas_call(attention_kernel, grid_spec=pltpu.PrefetchScalarGridSpec(n...]
    unnamed x37 -> x39, local copies, waits for them, and re-layouts: 6.64 us -> 6.65 us
  transfers between devices with their start and end apart: 12 -> 12, of which waited for: 9 -> 9; matrix products, arithmetic and copies ran while one was open for 10% -> 8% of each run, Pallas kernels for 22% -> 47%
where the time goes in v6:
time: 210 us; the launch traced here: 208 us
  Pallas kernels  97.3 us (46%)
  waiting for transfers between devices  76.4 us (36%)
  local copies, waits for them, and re-layouts  13.4 us (6%)
  starting transfers between devices  12.6 us (6%)
  other arithmetic  6.95 us (3%)
    pallas_call x2, Pallas kernels, attention(): pl.pallas_call(attention_kernel, grid_spec=pltpu.PrefetchScalarGridSpec(n...  97.3 us
    ppermute x8, waiting for transfers between devices, shift(): lax.ppermute(block, axis, [(i, (i + distance) % size) for i in range(size)])  73.8 us
    ppermute x8, starting transfers between devices, shift(): lax.ppermute(block, axis, [(i, (i + distance) % size) for i in range(size)])  12.1 us
    unnamed x39, local copies, waits for them, and re-layouts  6.65 us
    select_n x2, other arithmetic, forward_exchange(): jnp.where(is_odd, jnp.concatenate([back2, back4], 1), jnp.concatenate([ow...  4.26 us
  transfers between devices with their start and end apart: 12, of which 9 were waited for; matrix products, arithmetic and copies ran while one was open for 8% of the time, Pallas kernels for 47%

profile of v6, /device:TPU:100, one launch (start us, length us, event | category | flops | bytes accessed | tf_op | source)
XLA Modules:
  0.0 207.6 jit_solution(5461620014926970484)
XLA Ops:
  0.6 1.2 copy.25
  2.1 3.2 %collective-permute-start.3 = (bf16[2,256,512]{2,1,0:T(8,128)(2,1)S(1)}, bf16[2,256,512]{2,1,0:T(8,128)(2,1)S(1)}, u32[]{:S(2)}, u32[]{:S(2)}) collective-permute-start(bf16[2,256,512]{2,1,0:T(8,128)(2,1)S(1)} %pad_maximum_fusion.1.p0_ref), channel_id=1, source_target_pairs={{0,2},{1,3},{2,4},{3,5},{4,6},{5,7},{6,8},{7,9},{8,10},{9,11},{10,... | collective-permute-start | bytes 1572872 | tf_op jit(solution)/shard_map/ppermute | solution.py:21
  5.4 1.1 collective-permute-start
  6.5 11.2 %collective-permute-done.3.p2_ref = bf16[2,256,512]{2,1,0:T(8,128)(2,1)S(1)} collective-permute-done((bf16[2,256,512]{2,1,0:T(8,128)(2,1)S(1)}, bf16[2,256,512]{2,1,0:T(8,128)(2,1)S(1)}, u32[]{:S(2)}, u32[]{:S(2)}) %collective-permute-start.3) | collective-permute-done | bytes 524320 | tf_op jit(solution)/shard_map/ppermute | solution.py:21
  17.6 3.7 %collective-permute-start.4 = (bf16[2,256,512]{2,1,0:T(8,128)(2,1)S(1)}, bf16[2,256,512]{2,1,0:T(8,128)(2,1)}, u32[]{:S(2)}, u32[]{:S(2)}) collective-permute-start(bf16[2,256,512]{2,1,0:T(8,128)(2,1)S(1)} %collective-permute-done.3.p2_ref), channel_id=1, source_target_pairs={{0,2},{1,3},{2,4},{3,5},{4,6},{5,7},{6,8},{7,9},{8,10},{9,11},{10,... | collective-permute-start | bytes 1572872 | tf_op jit(solution)/shard_map/ppermute | solution.py:21
  21.3 7.5 %collective-permute-done.p2_ref = bf16[2,256,512]{2,1,0:T(8,128)(2,1)} collective-permute-done((bf16[2,256,512]{2,1,0:T(8,128)(2,1)S(1)}, bf16[2,256,512]{2,1,0:T(8,128)(2,1)}, u32[]{:S(2)}, u32[]{:S(2)}) %collective-permute-start) | collective-permute-done | bytes 524320 | tf_op jit(solution)/shard_map/ppermute | solution.py:21
  28.9 3.8 %collective-permute-start.1 = (bf16[2,256,512]{2,1,0:T(8,128)(2,1)}, bf16[2,256,512]{2,1,0:T(8,128)(2,1)}, u32[]{:S(2)}, u32[]{:S(2)}) collective-permute-start(bf16[2,256,512]{2,1,0:T(8,128)(2,1)} %collective-permute-done.p2_ref), channel_id=1, source_target_pairs={{0,2},{1,3},{2,4},{3,5},{4,6},{5,7},{6,8},{7,9},{8,10},{9,11},{10,... | collective-permute-start | bytes 1572872 | tf_op jit(solution)/shard_map/ppermute | solution.py:21
  32.7 7.4 %collective-permute-done.4.p4_ref = bf16[2,256,512]{2,1,0:T(8,128)(2,1)} collective-permute-done((bf16[2,256,512]{2,1,0:T(8,128)(2,1)S(1)}, bf16[2,256,512]{2,1,0:T(8,128)(2,1)}, u32[]{:S(2)}, u32[]{:S(2)}) %collective-permute-start.4) | collective-permute-done | bytes 524320 | tf_op jit(solution)/shard_map/ppermute | solution.py:21
  40.1 1.6 maximum_select_fusion.1
  42.1 0.5 slice.52
  42.7 0.8 copy.12.qd_ref
  43.5 1.1 fusion.2.flags_ref
  44.6 5.7 %collective-permute-done.1.p4_ref = bf16[2,256,512]{2,1,0:T(8,128)(2,1)} collective-permute-done((bf16[2,256,512]{2,1,0:T(8,128)(2,1)}, bf16[2,256,512]{2,1,0:T(8,128)(2,1)}, u32[]{:S(2)}, u32[]{:S(2)}) %collective-permute-start.1) | collective-permute-done | bytes 524320 | tf_op jit(solution)/shard_map/ppermute | solution.py:21
  50.3 2.6 %maximum_select_fusion = bf16[2,512,512]{2,1,0:T(8,128)(2,1)} fusion(bf16[2,256,512]{2,1,0:T(8,128)(2,1)} %collective-permute-done.1.p4_ref, bf16[2,256,512]{2,1,0:T(8,128)(2,1)} %collective-permute-done.p2_ref, bf16[1,256,512]{2,1,0:T(8,128)(2,1)S(1)} %get-tuple-element.37, bf16[1,256,512]{2,1,0:T(8,128)(2,1)S(1)} %get-tuple-element.38, pred[]{:T(512)S(6)} %eq.14), kind=kLoop, calls=%fused_computation.7 | loop fusion | flops 5767168 | bytes 2621441 | tf_op jit(solution)/shard_map/jit(_where)/select_n | solution.py:164
  53.0 1.8 copy_bitcast_fusion
  54.8 1.0 fusion.3
  55.8 48.6 %shard_map.84 = (bf16[256,2048]{1,0:T(8,128)(2,1)}, bf16[256,2048]{1,0:T(8,128)(2,1)}, bf16[2,512,512]{2,1,0:T(8,128)(2,1)}, bf16[2,256,512]{2,1,0:T(8,128)(2,1)...) custom-call(s32[4]{0:T(128)} %fusion.2.flags_ref, s32[256,1]{1,0:T(8,128)} %copy.12.qd_ref, ...), custom_call_target="tpu_custom_call" | custom-call | flops 4026531840 | bytes 7340032 | tf_op jit(solution)/shard_map/pallas_call | solution.py:121
  104.4 0.3 collective-permute-start.6
  104.7 2.2 %fusion.4 = (bf16[2,256,512]{2,1,0:T(8,128)(2,1)}, bf16[2,256,512]{2,1,0:T(8,128)(2,1)}) fusion(bf16[2,512,512]{2,1,0:T(8,128)(2,1)} %collective-permute-done.2), kind=kLoop, calls=%fused_computation.27 | loop fusion | bytes 2097152 | tf_op jit(solution)/shard_map/slice | solution.py:167
  107.0 48.8 %shard_map.85 = (bf16[256,2048]{1,0:T(8,128)(2,1)}, bf16[256,2048]{1,0:T(8,128)(2,1)}, bf16[2,512,512]{2,1,0:T(8,128)(2,1)}, bf16[2,256,512]{2,1,0:T(8,128)(2,1)...) custom-call(s32[4]{0:T(128)} %fusion.2.flags_ref, ...), custom_call_target="tpu_custom_call", output_to_operand_aliasing={{0}: (10, {}), {1}: (11, {})} | custom-call | flops 4026531840 | bytes 7340032 | tf_op jit(solution)/shard_map/pallas_call | solution.py:121
  156.1 2.6 %collective-permute-done.9 = bf16[2,512,512]{2,1,0:T(8,128)(2,1)S(1)} collective-permute-done((bf16[2,512,512]{2,1,0:T(8,128)(2,1)}, bf16[2,512,512]{2,1,0:T(8,128)(2,1)S(1)}, u32[]{:S(2)}, u32[]{:S(2)}) %collective-permute-start.9) | collective-permute-done | bytes 1048608 | tf_op jit(solution)/shard_map/ppermute | solution.py:25
  158.9 13.2 %collective-permute-done.7 = bf16[2,256,512]{2,1,0:T(8,128)(2,1)S(1)} collective-permute-done((bf16[2,256,512]{2,1,0:T(8,128)(2,1)S(1)}, bf16[2,256,512]{2,1,0:T(8,128)(2,1)S(1)}, u32[]{:S(2)}, u32[]{:S(2)}) %collective-permute-start.7) | collective-permute-done | bytes 524320 | tf_op jit(solution)/shard_map/ppermute | solution.py:21
  172.1 0.3 add_convert_fusion.1
  172.5 10.9 %collective-permute-done.10 = bf16[2,256,512]{2,1,0:T(8,128)(2,1)S(1)} collective-permute-done((bf16[2,256,512]{2,1,0:T(8,128)(2,1)S(1)}, bf16[2,256,512]{2,1,0:T(8,128)(2,1)S(1)}, u32[]{:S(2)}, u32[]{:S(2)}) %collective-permute-start.10) | collective-permute-done | bytes 524320 | tf_op jit(solution)/shard_map/ppermute | solution.py:21
  183.3 0.3 add_convert_fusion
  183.7 0.9 copy-done
  184.6 1.2 copy.17
  186.0 1.2 copy.18
  187.2 7.4 %collective-permute-done.8 = bf16[2,256,512]{2,1,0:T(8,128)(2,1)S(1)} collective-permute-done((bf16[2,256,512]{2,1,0:T(8,128)(2,1)S(1)}, bf16[2,256,512]{2,1,0:T(8,128)(2,1)S(1)}, u32[]{:S(2)}, u32[]{:S(2)}) %collective-permute-start.8) | collective-permute-done | bytes 524320 | tf_op jit(solution)/shard_map/ppermute | solution.py:21
  194.8 10.5 %collective-permute-done.11 = bf16[2,256,512]{2,1,0:T(8,128)(2,1)S(1)} collective-permute-done((bf16[2,256,512]{2,1,0:T(8,128)(2,1)S(1)}, bf16[2,256,512]{2,1,0:T(8,128)(2,1)S(1)}, u32[]{:S(2)}, u32[]{:S(2)}) %collective-permute-start.11) | collective-permute-done | bytes 524320 | tf_op jit(solution)/shard_map/ppermute | solution.py:21
  205.8 0.9 copy.19
  206.7 0.9 copy.20
  (55 shorter events, 2.3 us)
Async XLA Ops:
  0.6 1.2 copy-start.6
  2.1 38.0 %copy-start.8 = (bf16[2,256,512]{2,1,0:T(8,128)(2,1)}, bf16[2,256,512]{2,1,0:T(8,128)(2,1)S(1)}, u32[]{:S(2)}) copy-start(bf16[2,256,512]{2,1,0:T(8,128)(2,1)S(1)} %pad_maximum_fusion.1.p0_ref) | copy-start | bytes 1572868
  2.1 15.5 %collective-permute-start.3 = (bf16[2,256,512]{2,1,0:T(8,128)(2,1)S(1)}, bf16[2,256,512]{2,1,0:T(8,128)(2,1)S(1)}, u32[]{:S(2)}, u32[]{:S(2)}) collective-permute-start(bf16[2,256,512]{2,1,0:T(8,128)(2,1)S(1)} %pad_maximum_fusion.1.p0_ref), channel_id=1, source_target_pairs={{0,2},{1,3},{2,4},{3,5},{4,6},{5,7},{6,8},{7,9},{8,10},{9,11},{10,... | collective-permute-start | bytes 1572872 | tf_op jit(solution)/shard_map/ppermute | solution.py:21
  5.4 36.4 %copy-start.7 = (bf16[2,256,512]{2,1,0:T(8,128)(2,1)}, bf16[2,256,512]{2,1,0:T(8,128)(2,1)S(1)}, u32[]{:S(2)}) copy-start(bf16[2,256,512]{2,1,0:T(8,128)(2,1)S(1)} %pad_maximum_fusion.p0_ref) | copy-start | bytes 1572868
  5.4 23.5 %collective-permute-start = (bf16[2,256,512]{2,1,0:T(8,128)(2,1)S(1)}, bf16[2,256,512]{2,1,0:T(8,128)(2,1)}, u32[]{:S(2)}, u32[]{:S(2)}) collective-permute-start(bf16[2,256,512]{2,1,0:T(8,128)(2,1)S(1)} %pad_maximum_fusion.p0_ref), channel_id=1, source_target_pairs={{0,2},{1,3},{2,4},{3,5},{4,6},{5,7},{6,8},{7,9},{8,10},{9,11},{10,... | collective-permute-start | bytes 1572872 | tf_op jit(solution)/shard_map/ppermute | solution.py:21
  17.6 15.0 %copy-start.11 = (bf16[2,256,512]{2,1,0:T(8,128)(2,1)}, bf16[2,256,512]{2,1,0:T(8,128)(2,1)S(1)}, u32[]{:S(2)}) copy-start(bf16[2,256,512]{2,1,0:T(8,128)(2,1)S(1)} %collective-permute-done.3.p2_ref) | copy-start | bytes 1572868
  17.6 22.5 %collective-permute-start.4 = (bf16[2,256,512]{2,1,0:T(8,128)(2,1)S(1)}, bf16[2,256,512]{2,1,0:T(8,128)(2,1)}, u32[]{:S(2)}, u32[]{:S(2)}) collective-permute-start(bf16[2,256,512]{2,1,0:T(8,128)(2,1)S(1)} %collective-permute-done.3.p2_ref), channel_id=1, source_target_pairs={{0,2},{1,3},{2,4},{3,5},{4,6},{5,7},{6,8},{7,9},{8,10},{9,11},{10,... | collective-permute-start | bytes 1572872 | tf_op jit(solution)/shard_map/ppermute | solution.py:21
  28.9 21.4 %collective-permute-start.1 = (bf16[2,256,512]{2,1,0:T(8,128)(2,1)}, bf16[2,256,512]{2,1,0:T(8,128)(2,1)}, u32[]{:S(2)}, u32[]{:S(2)}) collective-permute-start(bf16[2,256,512]{2,1,0:T(8,128)(2,1)} %collective-permute-done.p2_ref), channel_id=1, source_target_pairs={{0,2},{1,3},{2,4},{3,5},{4,6},{5,7},{6,8},{7,9},{8,10},{9,11},{10,... | collective-permute-start | bytes 1572872 | tf_op jit(solution)/shard_map/ppermute | solution.py:21
  32.7 9.2 %copy-start.14 = (s32[4096]{0:T(1024)S(1)}, s32[4096]{0:T(1024)}, u32[]{:S(2)}) copy-start(s32[4096]{0:T(1024)} %param.9) | copy-start | bytes 49156
  41.8 13.0 %collective-permute-start.5 = (bf16[2,512,512]{2,1,0:T(8,128)(2,1)S(1)}, bf16[2,512,512]{2,1,0:T(8,128)(2,1)S(1)}, u32[]{:S(2)}, u32[]{:S(2)}) collective-permute-start(bf16[2,512,512]{2,1,0:T(8,128)(2,1)S(1)} %maximum_select_fusion.1), channel_id=1, source_target_pairs={{0,1},{1,0},{2,3},{3,2},{4,5},{5,4},{6,7},{7,6},{8,9},{9,8},{10,11... | collective-permute-start | bytes 3145736 | tf_op jit(solution)/shard_map/ppermute | solution.py:25
  42.0 11.0 %copy-start.15 = (s32[1,1280]{1,0:T(1,128)}, s32[1,1280]{1,0:T(1,128)S(1)}, u32[]{:S(2)}) copy-start(s32[1,1280]{1,0:T(1,128)S(1)} %reshape.44.kd_ref) | copy-start | bytes 15364
  44.6 8.4 %copy-start.2 = (bf16[256,16,128]{2,1,0:T(8,128)(2,1)S(1)}, bf16[256,16,128]{2,1,0:T(8,128)(2,1)}, u32[]{:S(2)}) copy-start(bf16[256,16,128]{2,1,0:T(8,128)(2,1)} %param.8) | copy-start | bytes 3145732
  44.6 8.4 %copy-start.3 = (bf16[256,16,128]{2,1,0:T(8,128)(2,1)S(1)}, bf16[256,16,128]{2,1,0:T(8,128)(2,1)}, u32[]{:S(2)}) copy-start(bf16[256,16,128]{2,1,0:T(8,128)(2,1)} %param.5) | copy-start | bytes 3145732
  52.9 51.8 %collective-permute-start.2 = (bf16[2,512,512]{2,1,0:T(8,128)(2,1)}, bf16[2,512,512]{2,1,0:T(8,128)(2,1)}, u32[]{:S(2)}, u32[]{:S(2)}) collective-permute-start(bf16[2,512,512]{2,1,0:T(8,128)(2,1)} %maximum_select_fusion), channel_id=1, source_target_pairs={{0,1},{1,0},{2,3},{3,2},{4,5},{5,4},{6,7},{7,6},{8,9},{9,8},{10,11... | collective-permute-start | bytes 3145736 | tf_op jit(solution)/shard_map/ppermute | solution.py:25
  104.4 51.4 %collective-permute-start.6 = (bf16[2,512,512]{2,1,0:T(8,128)(2,1)}, bf16[2,512,512]{2,1,0:T(8,128)(2,1)S(1)}, u32[]{:S(2)}, u32[]{:S(2)}) collective-permute-start(bf16[2,512,512]{2,1,0:T(8,128)(2,1)} %get-tuple-element.21), channel_id=1, source_target_pairs={{0,1},{1,0},{2,3},{3,2},{4,5},{5,4},{6,7},{7,6},{8,9},{9,8},{10,11... | collective-permute-start | bytes 3145736 | tf_op jit(solution)/shard_map/ppermute | solution.py:25
  106.9 48.9 %copy-start.9 = (bf16[2,256,512]{2,1,0:T(8,128)(2,1)S(1)}, bf16[2,256,512]{2,1,0:T(8,128)(2,1)}, u32[]{:S(2)}) copy-start(bf16[2,256,512]{2,1,0:T(8,128)(2,1)} %get-tuple-element.20) | copy-start | bytes 1572868
  155.7 3.0 %copy-start.10 = (bf16[2,256,512]{2,1,0:T(8,128)(2,1)S(1)}, bf16[2,256,512]{2,1,0:T(8,128)(2,1)}, u32[]{:S(2)}) copy-start(bf16[2,256,512]{2,1,0:T(8,128)(2,1)} %get-tuple-element.24) | copy-start | bytes 1572868
  155.7 3.0 %collective-permute-start.9 = (bf16[2,512,512]{2,1,0:T(8,128)(2,1)}, bf16[2,512,512]{2,1,0:T(8,128)(2,1)S(1)}, u32[]{:S(2)}, u32[]{:S(2)}) collective-permute-start(bf16[2,512,512]{2,1,0:T(8,128)(2,1)} %get-tuple-element.25), channel_id=1, source_target_pairs={{0,1},{1,0},{2,3},{3,2},{4,5},{5,4},{6,7},{7,6},{8,9},{9,8},{10,11... | collective-permute-start | bytes 3145736 | tf_op jit(solution)/shard_map/ppermute | solution.py:25
  156.0 16.1 %copy-start.12 = (bf16[2,256,512]{2,1,0:T(8,128)(2,1)S(1)}, bf16[2,256,512]{2,1,0:T(8,128)(2,1)}, u32[]{:S(2)}) copy-start(bf16[2,256,512]{2,1,0:T(8,128)(2,1)} %get-tuple-element.22) | copy-start | bytes 1572868
  156.0 16.1 %collective-permute-start.7 = (bf16[2,256,512]{2,1,0:T(8,128)(2,1)S(1)}, bf16[2,256,512]{2,1,0:T(8,128)(2,1)S(1)}, u32[]{:S(2)}, u32[]{:S(2)}) collective-permute-start(bf16[2,256,512]{2,1,0:T(8,128)(2,1)S(1)} %fusion), channel_id=1, source_target_pairs={{0,14},{1,15},{2,0},{3,1},{4,2},{5,3},{6,4},{7,5},{8,6},{9,7},{10,... | collective-permute-start | bytes 1572872 | tf_op jit(solution)/shard_map/ppermute | solution.py:21
  158.8 24.5 %collective-permute-start.10 = (bf16[2,256,512]{2,1,0:T(8,128)(2,1)S(1)}, bf16[2,256,512]{2,1,0:T(8,128)(2,1)S(1)}, u32[]{:S(2)}, u32[]{:S(2)}) collective-permute-start(bf16[2,256,512]{2,1,0:T(8,128)(2,1)S(1)} %fusion.1), channel_id=1, source_target_pairs={{0,14},{1,15},{2,0},{3,1},{4,2},{5,3},{6,4},{7,5},{8,6},{9,7},{10,... | collective-permute-start | bytes 1572872 | tf_op jit(solution)/shard_map/ppermute | solution.py:21
  172.1 11.2 %copy-start.13 = (bf16[2,256,512]{2,1,0:T(8,128)(2,1)S(1)}, bf16[2,256,512]{2,1,0:T(8,128)(2,1)}, u32[]{:S(2)}) copy-start(bf16[2,256,512]{2,1,0:T(8,128)(2,1)} %get-tuple-element.26) | copy-start | bytes 1572868
  172.4 22.2 %collective-permute-start.8 = (bf16[2,256,512]{2,1,0:T(8,128)(2,1)S(1)}, bf16[2,256,512]{2,1,0:T(8,128)(2,1)S(1)}, u32[]{:S(2)}, u32[]{:S(2)}) collective-permute-start(bf16[2,256,512]{2,1,0:T(8,128)(2,1)S(1)} %add_convert_fusion.1), channel_id=1, source_target_pairs={{0,14},{1,15},{2,0},{3,1},{4,2},{5,3},{6,4},{7,5},{8,6},{9,7},{10,... | collective-permute-start | bytes 1572872 | tf_op jit(solution)/shard_map/ppermute | solution.py:21
  183.3 1.2 copy-start
  183.6 21.7 %collective-permute-start.11 = (bf16[2,256,512]{2,1,0:T(8,128)(2,1)S(1)}, bf16[2,256,512]{2,1,0:T(8,128)(2,1)S(1)}, u32[]{:S(2)}, u32[]{:S(2)}) collective-permute-start(bf16[2,256,512]{2,1,0:T(8,128)(2,1)S(1)} %add_convert_fusion), channel_id=1, source_target_pairs={{0,14},{1,15},{2,0},{3,1},{4,2},{5,3},{6,4},{7,5},{8,6},{9,7},{10,... | collective-permute-start | bytes 1572872 | tf_op jit(solution)/shard_map/ppermute | solution.py:21
  184.6 1.4 copy-start.1
  186.0 8.6 %copy-start.4 = (bf16[2,256,512]{2,1,0:T(8,128)(2,1)S(1)}, bf16[2,256,512]{2,1,0:T(8,128)(2,1)}, u32[]{:S(2)}) copy-start(bf16[2,256,512]{2,1,0:T(8,128)(2,1)} %get-tuple-element.23) | copy-start | bytes 1572868
  194.6 10.7 %copy-start.5 = (bf16[2,256,512]{2,1,0:T(8,128)(2,1)S(1)}, bf16[2,256,512]{2,1,0:T(8,128)(2,1)}, u32[]{:S(2)}) copy-start(bf16[2,256,512]{2,1,0:T(8,128)(2,1)} %get-tuple-element.27) | copy-start | bytes 1572868

commit v7 on v5

--- a/solution.py
+++ b/solution.py
@@ -7,7 +7,7 @@
 
 
 WINDOW = 1024
-CHUNKS = 2
+CHUNKS = 4
 
 
 QUERY_SCALE = 168.0 ** (-0.5)
@@ -68,15 +68,16 @@
 
 def attention(q2, g2, pieces, q_docs, k_docs, head_size, chunk, bufs):
     rows = q2.shape[0]
+    pieces, blocks = zip(*pieces)
     groups = pieces[0].shape[2] // head_size
     per_group = 2 * head_size
     cols = rows * len(pieces)
     q_spec = pl.BlockSpec((rows, per_group), lambda i: (0, chunk * groups + i))
     kv_spec = pl.BlockSpec((2, rows, head_size), lambda i: (0, 0, i))
     pair_spec = pl.BlockSpec((2, 2 * rows, head_size), lambda i: (0, 0, i))
-    piece_shape = jax.ShapeDtypeStruct(pieces[0].shape, jnp.bfloat16)
+    piece_shape = jax.ShapeDtypeStruct(pieces[-1].shape, jnp.bfloat16)
     flops = 12 * rows * cols * per_group * groups
-    bytes_accessed = 2 * (4 * rows * per_group * groups + 10 * pieces[0].size)
+    bytes_accessed = 2 * (4 * rows * per_group * groups + 10 * pieces[-1].size)
     return pl.pallas_call(
         attention_kernel,
         grid=(groups,),
@@ -85,7 +86,8 @@
             pl.BlockSpec((1, cols), lambda i: (0, 0)),
             q_spec,
             q_spec,
-        ] + [kv_spec] * len(pieces) + [pl.BlockSpec(memory_space=pl.ANY)] * len(bufs),
+        ] + [pl.BlockSpec((2, rows, head_size), lambda i, b=b: (0, b, i)) for b in blocks]
+        + [pl.BlockSpec(memory_space=pl.ANY)] * len(bufs),
         out_specs=[q_spec, q_spec, pair_spec, kv_spec, kv_spec, kv_spec],
         out_shape=[
             jax.ShapeDtypeStruct(q2.shape, jnp.bfloat16),
@@ -108,13 +110,12 @@
 
 
 def forward_exchange(own, is_odd):
-    rows = own.shape[1]
     back2 = shift(own, "ctx", 2)
     back4 = shift(back2, "ctx", 2)
     odd_pieces = jnp.where(is_odd, jnp.concatenate([back2, back4], 1),
                            jnp.concatenate([own, back2], 1))
     back13 = swap(odd_pieces, "ctx")
-    return (back4, back13[:, rows:], back2, back13[:, :rows], own)
+    return ((back4, 0), (back13, 1), (back2, 0), (back13, 0), (own, 0))
 
 
 def backward_exchange(terms, is_odd):

time: 144 us -> 146 us (1.014)
  waiting for transfers between devices: 78.3 us -> 60.3 us
  starting transfers between devices: 13.1 us -> 27.6 us
  Pallas kernels: 30.5 us -> 34.1 us
  other arithmetic: 5.82 us -> 8.41 us
    ppermute x8 -> x16, waiting for transfers between devices: 75.7 us -> 60.3 us  [shift(): lax.ppermute(block, axis, [(i, (i + distance) % size) for i in range(size)])]
    ppermute x8 -> x16, starting transfers between devices: 12.1 us -> 25.6 us  [shift(): lax.ppermute(block, axis, [(i, (i + distance) % size) for i in range(size)])]
    pallas_call x2 -> x4, Pallas kernels: 30.5 us -> 34.1 us  [attention(): pl.pallas_call(attention_kernel, grid=(groups,), in_specs=[pl.BlockSpec((...]
    slice x2 -> x0, local copies, waits for them, and re-layouts: 3.26 us -> none  [forward_exchange(): return (back4, back13[:, rows:], back2, back13[:, :rows], own)]
    ppermute x4 -> x8, waiting for transfers between devices: 2.58 us -> 0.02 us  [swap(): lax.ppermute(block, axis, [(i, i ^ 1) for i in range(lax.axis_size(axis))])]
    unnamed x37 -> x51, local copies, waits for them, and re-layouts: 6.64 us -> 9.06 us
    another operation x2 -> x4, other arithmetic: 0.1 us -> 2.24 us  [staged(): own = jnp.stack([k2[:, lanes], v2[:, lanes]])]
    select_n x2 -> x4, other arithmetic: 4.25 us -> 4.65 us  [forward_exchange(): jnp.where(is_odd, jnp.concatenate([back2, back4], 1), jnp.concatenate([ow...]
  transfers between devices with their start and end apart: 12 -> 24, of which waited for: 9 -> 16; matrix products, arithmetic and copies ran while one was open for 10% -> 11% of each run, Pallas kernels for 22% -> 24%
where the time goes in v7:
time: 146 us; the launch traced here: 144 us
  waiting for transfers between devices  60.3 us (41%)
  Pallas kernels  34.1 us (23%)
  starting transfers between devices  27.6 us (19%)
  local copies, waits for them, and re-layouts  12.5 us (9%)
  other arithmetic  8.41 us (6%)
    ppermute x16, waiting for transfers between devices, shift(): lax.ppermute(block, axis, [(i, (i + distance) % size) for i in range(size)])  60.3 us
    pallas_call x4, Pallas kernels, attention(): pl.pallas_call(attention_kernel, grid=(groups,), in_specs=[pl.BlockSpec((...  34.1 us
    ppermute x16, starting transfers between devices, shift(): lax.ppermute(block, axis, [(i, (i + distance) % size) for i in range(size)])  25.6 us
    unnamed x51, local copies, waits for them, and re-layouts  9.06 us
    select_n x4, other arithmetic, forward_exchange(): jnp.where(is_odd, jnp.concatenate([back2, back4], 1), jnp.concatenate([ow...  4.65 us
  transfers between devices with their start and end apart: 24, of which 16 were waited for; matrix products, arithmetic and copies ran while one was open for 11% of the time, Pallas kernels for 24%

profile of v7, /device:TPU:100, one launch (start us, length us, event | category | flops | bytes accessed | tf_op | source)
XLA Modules:
  0.0 143.9 jit_solution(6510893354970496698)
XLA Ops:
  2.1 3.2 %collective-permute-start.9 = (bf16[2,256,256]{2,1,0:T(8,128)(2,1)S(1)}, bf16[2,256,256]{2,1,0:T(8,128)(2,1)}, u32[]{:S(2)}, u32[]{:S(2)}) collective-permute-start(bf16[2,256,256]{2,1,0:T(8,128)(2,1)S(1)} %pad_maximum_fusion.3.p0_ref), channel_id=1, source_target_pairs={{0,2},{1,3},{2,4},{3,5},{4,6},{5,7},{6,8},{7,9},{8,10},{9,11},{10,... | collective-permute-start | bytes 786440 | tf_op jit(solution)/shard_map/ppermute | solution.py:21
  8.8 3.2 %collective-permute-done.9.p2_ref = bf16[2,256,256]{2,1,0:T(8,128)(2,1)} collective-permute-done((bf16[2,256,256]{2,1,0:T(8,128)(2,1)S(1)}, bf16[2,256,256]{2,1,0:T(8,128)(2,1)}, u32[]{:S(2)}, u32[]{:S(2)}) %collective-permute-start.9) | collective-permute-done | bytes 262176 | tf_op jit(solution)/shard_map/ppermute | solution.py:21
  12.0 3.8 %collective-permute-start.10 = (bf16[2,256,256]{2,1,0:T(8,128)(2,1)}, bf16[2,256,256]{2,1,0:T(8,128)(2,1)}, u32[]{:S(2)}, u32[]{:S(2)}) collective-permute-start(bf16[2,256,256]{2,1,0:T(8,128)(2,1)} %collective-permute-done.9.p2_ref), channel_id=1, source_target_pairs={{0,2},{1,3},{2,4},{3,5},{4,6},{5,7},{6,8},{7,9},{8,10},{9,11},{10,... | collective-permute-start | bytes 786440 | tf_op jit(solution)/shard_map/ppermute | solution.py:21
  17.7 3.7 %collective-permute-start.7 = (bf16[2,256,256]{2,1,0:T(8,128)(2,1)}, bf16[2,256,256]{2,1,0:T(8,128)(2,1)}, u32[]{:S(2)}, u32[]{:S(2)}) collective-permute-start(bf16[2,256,256]{2,1,0:T(8,128)(2,1)} %collective-permute-done.6.p2_ref), channel_id=1, source_target_pairs={{0,2},{1,3},{2,4},{3,5},{4,6},{5,7},{6,8},{7,9},{8,10},{9,11},{10,... | collective-permute-start | bytes 786440 | tf_op jit(solution)/shard_map/ppermute | solution.py:21
  21.4 1.9 %collective-permute-done.3.p2_ref = bf16[2,256,256]{2,1,0:T(8,128)(2,1)} collective-permute-done((bf16[2,256,256]{2,1,0:T(8,128)(2,1)}, bf16[2,256,256]{2,1,0:T(8,128)(2,1)}, u32[]{:S(2)}, u32[]{:S(2)}) %collective-permute-start.3) | collective-permute-done | bytes 262176 | tf_op jit(solution)/shard_map/ppermute | solution.py:21
  23.3 3.7 %collective-permute-start.4 = (bf16[2,256,256]{2,1,0:T(8,128)(2,1)}, bf16[2,256,256]{2,1,0:T(8,128)(2,1)}, u32[]{:S(2)}, u32[]{:S(2)}) collective-permute-start(bf16[2,256,256]{2,1,0:T(8,128)(2,1)} %collective-permute-done.3.p2_ref), channel_id=1, source_target_pairs={{0,2},{1,3},{2,4},{3,5},{4,6},{5,7},{6,8},{7,9},{8,10},{9,11},{10,... | collective-permute-start | bytes 786440 | tf_op jit(solution)/shard_map/ppermute | solution.py:21
  27.0 1.9 %collective-permute-done.10.p4_ref = bf16[2,256,256]{2,1,0:T(8,128)(2,1)} collective-permute-done((bf16[2,256,256]{2,1,0:T(8,128)(2,1)}, bf16[2,256,256]{2,1,0:T(8,128)(2,1)}, u32[]{:S(2)}, u32[]{:S(2)}) %collective-permute-start.10) | collective-permute-done | bytes 262176 | tf_op jit(solution)/shard_map/ppermute | solution.py:21
  28.9 2.0 %maximum_select_fusion.3 = bf16[2,512,256]{2,1,0:T(8,128)(2,1)} fusion(bf16[2,256,256]{2,1,0:T(8,128)(2,1)} %collective-permute-done.10.p4_ref, bf16[2,256,256]{2,1,0:T(8,128)(2,1)} %collective-permute-done.9.p2_ref, bf16[1,256,256]{2,1,0:T(8,128)(2,1)S(1)} %get-tuple-element.58, bf16[1,256,256]{2,1,0:T(8,128)(2,1)S(1)} %get-tuple-element.65, pred[]{:T(512)S(6)} %eq.5), kind=kLoop, calls=%fused_computation.18 | loop fusion | flops 2883584 | bytes 1310721 | tf_op jit(solution)/shard_map/jit(_where)/select_n | solution.py:115
  31.0 1.8 %copy_bitcast_fusion = (bf16[256,2048]{1,0:T(8,128)(2,1)}, bf16[256,2048]{1,0:T(8,128)(2,1)}) fusion(bf16[32,8,16,128]{3,2,1,0:T(8,128)(2,1)S(1)} %bitcast.49, bf16[32,8,16,128]{3,2,1,0:T(8,128)(2,1)S(1)} %bitcast.50), kind=kLoop, calls=%fused_computation.1 | loop fusion | bytes 4194304 | tf_op jit(solution)/shard_map/reshape | solution.py:146
  32.8 1.8 %collective-permute-done.p2_ref = bf16[2,256,256]{2,1,0:T(8,128)(2,1)S(1)} collective-permute-done((bf16[2,256,256]{2,1,0:T(8,128)(2,1)}, bf16[2,256,256]{2,1,0:T(8,128)(2,1)S(1)}, u32[]{:S(2)}, u32[]{:S(2)}) %collective-permute-start) | collective-permute-done | bytes 262176 | tf_op jit(solution)/shard_map/ppermute | solution.py:21
  34.6 3.6 %collective-permute-start.1 = (bf16[2,256,256]{2,1,0:T(8,128)(2,1)S(1)}, bf16[2,256,256]{2,1,0:T(8,128)(2,1)S(1)}, u32[]{:S(2)}, u32[]{:S(2)}) collective-permute-start(bf16[2,256,256]{2,1,0:T(8,128)(2,1)S(1)} %collective-permute-done.p2_ref), channel_id=1, source_target_pairs={{0,2},{1,3},{2,4},{3,5},{4,6},{5,7},{6,8},{7,9},{8,10},{9,11},{10,... | collective-permute-start | bytes 786440 | tf_op jit(solution)/shard_map/ppermute | solution.py:21
  38.1 2.0 %collective-permute-done.7.p4_ref = bf16[2,256,256]{2,1,0:T(8,128)(2,1)} collective-permute-done((bf16[2,256,256]{2,1,0:T(8,128)(2,1)}, bf16[2,256,256]{2,1,0:T(8,128)(2,1)}, u32[]{:S(2)}, u32[]{:S(2)}) %collective-permute-start.7) | collective-permute-done | bytes 262176 | tf_op jit(solution)/shard_map/ppermute | solution.py:21
  40.2 1.2 maximum_select_fusion.2
  41.5 4.3 %collective-permute-done.4.p4_ref = bf16[2,256,256]{2,1,0:T(8,128)(2,1)} collective-permute-done((bf16[2,256,256]{2,1,0:T(8,128)(2,1)}, bf16[2,256,256]{2,1,0:T(8,128)(2,1)}, u32[]{:S(2)}, u32[]{:S(2)}) %collective-permute-start.4) | collective-permute-done | bytes 262176 | tf_op jit(solution)/shard_map/ppermute | solution.py:21
  45.8 1.2 maximum_select_fusion.1
  48.7 1.5 %collective-permute-done.1.p4_ref = bf16[2,256,256]{2,1,0:T(8,128)(2,1)S(1)} collective-permute-done((bf16[2,256,256]{2,1,0:T(8,128)(2,1)S(1)}, bf16[2,256,256]{2,1,0:T(8,128)(2,1)S(1)}, u32[]{:S(2)}, u32[]{:S(2)}) %collective-permute-start.1) | collective-permute-done | bytes 262176 | tf_op jit(solution)/shard_map/ppermute | solution.py:21
  50.6 8.5 %shard_map.84 = (bf16[256,2048]{1,0:T(8,128)(2,1)}, bf16[256,2048]{1,0:T(8,128)(2,1)}, bf16[2,512,256]{2,1,0:T(8,128)(2,1)}, bf16[2,256,256]{2,1,0:T(8,128)(2,1)...) custom-call(s32[256,1]{1,0:T(8,128)} %copy.18.qd_ref, s32[1,1280]{1,0:T(1,128)} %reshape.39.kd_ref, ...), custom_call_target="tpu_custom_call" | custom-call | flops 2013265920 | bytes 3670016 | tf_op jit(solution)/shard_map/pallas_call | solution.py:81
  60.5 8.5 %shard_map.85 = (bf16[256,2048]{1,0:T(8,128)(2,1)}, bf16[256,2048]{1,0:T(8,128)(2,1)}, bf16[2,512,256]{2,1,0:T(8,128)(2,1)}, bf16[2,256,256]{2,1,0:T(8,128)(2,1)...) custom-call(s32[256,1]{1,0:T(8,128)} %copy.18.qd_ref, ...), custom_call_target="tpu_custom_call", output_to_operand_aliasing={{0}: (9, {}), {1}: (10, {})} | custom-call | flops 2013265920 | bytes 3670016 | tf_op jit(solution)/shard_map/pallas_call | solution.py:81
  69.2 8.5 %shard_map.86 = (bf16[256,2048]{1,0:T(8,128)(2,1)}, bf16[256,2048]{1,0:T(8,128)(2,1)}, bf16[2,512,256]{2,1,0:T(8,128)(2,1)}, bf16[2,256,256]{2,1,0:T(8,128)(2,1)...) custom-call(s32[256,1]{1,0:T(8,128)} %copy.18.qd_ref, ...), custom_call_target="tpu_custom_call", output_to_operand_aliasing={{0}: (9, {}), {1}: (10, {})} | custom-call | flops 2013265920 | bytes 3670016 | tf_op jit(solution)/shard_map/pallas_call | solution.py:81
  79.3 8.5 %shard_map.87 = (bf16[256,2048]{1,0:T(8,128)(2,1)}, bf16[256,2048]{1,0:T(8,128)(2,1)}, bf16[2,512,256]{2,1,0:T(8,128)(2,1)}, bf16[2,256,256]{2,1,0:T(8,128)(2,1)...) custom-call(s32[256,1]{1,0:T(8,128)} %copy.18.qd_ref, ...), custom_call_target="tpu_custom_call", output_to_operand_aliasing={{0}: (9, {}), {1}: (10, {})} | custom-call | flops 2013265920 | bytes 3670016 | tf_op jit(solution)/shard_map/pallas_call | solution.py:81
  87.9 2.5 %copy.23 = bf16[32,8,16,128]{3,2,1,0:T(8,128)(2,1)} copy(bf16[32,8,16,128]{3,1,2,0:T(8,128)(2,1)} %bitcast.47) | data formatting | bytes 2097152
  90.5 1.2 copy.24
  92.7 3.3 %collective-permute-start.19 = (bf16[2,256,256]{2,1,0:T(8,128)(2,1)S(1)}, bf16[2,256,256]{2,1,0:T(8,128)(2,1)S(1)}, u32[]{:S(2)}, u32[]{:S(2)}) collective-permute-start(bf16[2,256,256]{2,1,0:T(8,128)(2,1)S(1)} %fusion.2), channel_id=1, source_target_pairs={{0,14},{1,15},{2,0},{3,1},{4,2},{5,3},{6,4},{7,5},{8,6},{9,7},{10,... | collective-permute-start | bytes 786440 | tf_op jit(solution)/shard_map/ppermute | solution.py:21
  96.1 1.8 %collective-permute-start.22 = (bf16[2,256,256]{2,1,0:T(8,128)(2,1)S(1)}, bf16[2,256,256]{2,1,0:T(8,128)(2,1)S(1)}, u32[]{:S(2)}, u32[]{:S(2)}) collective-permute-start(bf16[2,256,256]{2,1,0:T(8,128)(2,1)S(1)} %fusion.3), channel_id=1, source_target_pairs={{0,14},{1,15},{2,0},{3,1},{4,2},{5,3},{6,4},{7,5},{8,6},{9,7},{10,... | collective-permute-start | bytes 786440 | tf_op jit(solution)/shard_map/ppermute | solution.py:21
  97.9 4.8 %collective-permute-done.13 = bf16[2,256,256]{2,1,0:T(8,128)(2,1)S(1)} collective-permute-done((bf16[2,256,256]{2,1,0:T(8,128)(2,1)S(1)}, bf16[2,256,256]{2,1,0:T(8,128)(2,1)S(1)}, u32[]{:S(2)}, u32[]{:S(2)}) %collective-permute-start.13) | collective-permute-done | bytes 262176 | tf_op jit(solution)/shard_map/ppermute | solution.py:21
  102.9 5.4 %collective-permute-done.16 = bf16[2,256,256]{2,1,0:T(8,128)(2,1)S(1)} collective-permute-done((bf16[2,256,256]{2,1,0:T(8,128)(2,1)S(1)}, bf16[2,256,256]{2,1,0:T(8,128)(2,1)S(1)}, u32[]{:S(2)}, u32[]{:S(2)}) %collective-permute-start.16) | collective-permute-done | bytes 262176 | tf_op jit(solution)/shard_map/ppermute | solution.py:21
  108.5 5.4 %collective-permute-done.19 = bf16[2,256,256]{2,1,0:T(8,128)(2,1)S(1)} collective-permute-done((bf16[2,256,256]{2,1,0:T(8,128)(2,1)S(1)}, bf16[2,256,256]{2,1,0:T(8,128)(2,1)S(1)}, u32[]{:S(2)}, u32[]{:S(2)}) %collective-permute-start.19) | collective-permute-done | bytes 262176 | tf_op jit(solution)/shard_map/ppermute | solution.py:21
  114.2 5.4 %collective-permute-done.22 = bf16[2,256,256]{2,1,0:T(8,128)(2,1)S(1)} collective-permute-done((bf16[2,256,256]{2,1,0:T(8,128)(2,1)S(1)}, bf16[2,256,256]{2,1,0:T(8,128)(2,1)S(1)}, u32[]{:S(2)}, u32[]{:S(2)}) %collective-permute-start.22) | collective-permute-done | bytes 262176 | tf_op jit(solution)/shard_map/ppermute | solution.py:21
  119.8 5.4 %collective-permute-done.14 = bf16[2,256,256]{2,1,0:T(8,128)(2,1)S(1)} collective-permute-done((bf16[2,256,256]{2,1,0:T(8,128)(2,1)S(1)}, bf16[2,256,256]{2,1,0:T(8,128)(2,1)S(1)}, u32[]{:S(2)}, u32[]{:S(2)}) %collective-permute-start.14) | collective-permute-done | bytes 262176 | tf_op jit(solution)/shard_map/ppermute | solution.py:21
  125.3 5.5 %collective-permute-done.17 = bf16[2,256,256]{2,1,0:T(8,128)(2,1)S(1)} collective-permute-done((bf16[2,256,256]{2,1,0:T(8,128)(2,1)S(1)}, bf16[2,256,256]{2,1,0:T(8,128)(2,1)S(1)}, u32[]{:S(2)}, u32[]{:S(2)}) %collective-permute-start.17) | collective-permute-done | bytes 262176 | tf_op jit(solution)/shard_map/ppermute | solution.py:21
  130.9 5.5 %collective-permute-done.20 = bf16[2,256,256]{2,1,0:T(8,128)(2,1)S(1)} collective-permute-done((bf16[2,256,256]{2,1,0:T(8,128)(2,1)S(1)}, bf16[2,256,256]{2,1,0:T(8,128)(2,1)S(1)}, u32[]{:S(2)}, u32[]{:S(2)}) %collective-permute-start.20) | collective-permute-done | bytes 262176 | tf_op jit(solution)/shard_map/ppermute | solution.py:21
  136.5 5.3 %collective-permute-done.23 = bf16[2,256,256]{2,1,0:T(8,128)(2,1)S(1)} collective-permute-done((bf16[2,256,256]{2,1,0:T(8,128)(2,1)S(1)}, bf16[2,256,256]{2,1,0:T(8,128)(2,1)S(1)}, u32[]{:S(2)}, u32[]{:S(2)}) %collective-permute-start.23) | collective-permute-done | bytes 262176 | tf_op jit(solution)/shard_map/ppermute | solution.py:21
  (98 shorter events, 16.6 us)
Async XLA Ops:
  2.1 13.7 %copy-start.10 = (bf16[2,256,256]{2,1,0:T(8,128)(2,1)}, bf16[2,256,256]{2,1,0:T(8,128)(2,1)S(1)}, u32[]{:S(2)}) copy-start(bf16[2,256,256]{2,1,0:T(8,128)(2,1)S(1)} %pad_maximum_fusion.3.p0_ref) | copy-start | bytes 786436
  2.1 9.9 %collective-permute-start.9 = (bf16[2,256,256]{2,1,0:T(8,128)(2,1)S(1)}, bf16[2,256,256]{2,1,0:T(8,128)(2,1)}, u32[]{:S(2)}, u32[]{:S(2)}) collective-permute-start(bf16[2,256,256]{2,1,0:T(8,128)(2,1)S(1)} %pad_maximum_fusion.3.p0_ref), channel_id=1, source_target_pairs={{0,2},{1,3},{2,4},{3,5},{4,6},{5,7},{6,8},{7,9},{8,10},{9,11},{10,... | collective-permute-start | bytes 786440 | tf_op jit(solution)/shard_map/ppermute | solution.py:21
  6.0 11.7 %collective-permute-start.6 = (bf16[2,256,256]{2,1,0:T(8,128)(2,1)}, bf16[2,256,256]{2,1,0:T(8,128)(2,1)}, u32[]{:S(2)}, u32[]{:S(2)}) collective-permute-start(bf16[2,256,256]{2,1,0:T(8,128)(2,1)} %pad_maximum_fusion.2.p0_ref), channel_id=1, source_target_pairs={{0,2},{1,3},{2,4},{3,5},{4,6},{5,7},{6,8},{7,9},{8,10},{9,11},{10,... | collective-permute-start | bytes 786440 | tf_op jit(solution)/shard_map/ppermute | solution.py:21
  7.0 23.9 %copy-start.2 = (bf16[256,16,128]{2,1,0:T(8,128)(2,1)S(1)}, bf16[256,16,128]{2,1,0:T(8,128)(2,1)}, u32[]{:S(2)}) copy-start(bf16[256,16,128]{2,1,0:T(8,128)(2,1)} %param.5) | copy-start | bytes 3145732
  7.8 23.2 %copy-start.1 = (bf16[256,16,128]{2,1,0:T(8,128)(2,1)S(1)}, bf16[256,16,128]{2,1,0:T(8,128)(2,1)}, u32[]{:S(2)}) copy-start(bf16[256,16,128]{2,1,0:T(8,128)(2,1)} %param.8) | copy-start | bytes 3145732
  7.8 15.5 %collective-permute-start.3 = (bf16[2,256,256]{2,1,0:T(8,128)(2,1)}, bf16[2,256,256]{2,1,0:T(8,128)(2,1)}, u32[]{:S(2)}, u32[]{:S(2)}) collective-permute-start(bf16[2,256,256]{2,1,0:T(8,128)(2,1)} %pad_maximum_fusion.1.p0_ref), channel_id=1, source_target_pairs={{0,2},{1,3},{2,4},{3,5},{4,6},{5,7},{6,8},{7,9},{8,10},{9,11},{10,... | collective-permute-start | bytes 786440 | tf_op jit(solution)/shard_map/ppermute | solution.py:21
  12.0 17.0 %collective-permute-start.10 = (bf16[2,256,256]{2,1,0:T(8,128)(2,1)}, bf16[2,256,256]{2,1,0:T(8,128)(2,1)}, u32[]{:S(2)}, u32[]{:S(2)}) collective-permute-start(bf16[2,256,256]{2,1,0:T(8,128)(2,1)} %collective-permute-done.9.p2_ref), channel_id=1, source_target_pairs={{0,2},{1,3},{2,4},{3,5},{4,6},{5,7},{6,8},{7,9},{8,10},{9,11},{10,... | collective-permute-start | bytes 786440 | tf_op jit(solution)/shard_map/ppermute | solution.py:21
  16.5 18.0 %collective-permute-start = (bf16[2,256,256]{2,1,0:T(8,128)(2,1)}, bf16[2,256,256]{2,1,0:T(8,128)(2,1)S(1)}, u32[]{:S(2)}, u32[]{:S(2)}) collective-permute-start(bf16[2,256,256]{2,1,0:T(8,128)(2,1)} %pad_maximum_fusion.p0_ref), channel_id=1, source_target_pairs={{0,2},{1,3},{2,4},{3,5},{4,6},{5,7},{6,8},{7,9},{8,10},{9,11},{10,... | collective-permute-start | bytes 786440 | tf_op jit(solution)/shard_map/ppermute | solution.py:21
  17.7 22.5 %collective-permute-start.7 = (bf16[2,256,256]{2,1,0:T(8,128)(2,1)}, bf16[2,256,256]{2,1,0:T(8,128)(2,1)}, u32[]{:S(2)}, u32[]{:S(2)}) collective-permute-start(bf16[2,256,256]{2,1,0:T(8,128)(2,1)} %collective-permute-done.6.p2_ref), channel_id=1, source_target_pairs={{0,2},{1,3},{2,4},{3,5},{4,6},{5,7},{6,8},{7,9},{8,10},{9,11},{10,... | collective-permute-start | bytes 786440 | tf_op jit(solution)/shard_map/ppermute | solution.py:21
  23.3 22.5 %collective-permute-start.4 = (bf16[2,256,256]{2,1,0:T(8,128)(2,1)}, bf16[2,256,256]{2,1,0:T(8,128)(2,1)}, u32[]{:S(2)}, u32[]{:S(2)}) collective-permute-start(bf16[2,256,256]{2,1,0:T(8,128)(2,1)} %collective-permute-done.3.p2_ref), channel_id=1, source_target_pairs={{0,2},{1,3},{2,4},{3,5},{4,6},{5,7},{6,8},{7,9},{8,10},{9,11},{10,... | collective-permute-start | bytes 786440 | tf_op jit(solution)/shard_map/ppermute | solution.py:21
  31.0 19.7 %collective-permute-start.11 = (bf16[2,512,256]{2,1,0:T(8,128)(2,1)}, bf16[2,512,256]{2,1,0:T(8,128)(2,1)}, u32[]{:S(2)}, u32[]{:S(2)}) collective-permute-start(bf16[2,512,256]{2,1,0:T(8,128)(2,1)} %maximum_select_fusion.3), channel_id=1, source_target_pairs={{0,1},{1,0},{2,3},{3,2},{4,5},{5,4},{6,7},{7,6},{8,9},{9,8},{10,11... | collective-permute-start | bytes 1572872 | tf_op jit(solution)/shard_map/ppermute | solution.py:25
  32.8 14.3 %copy-start.19 = (s32[4096]{0:T(1024)S(1)}, s32[4096]{0:T(1024)}, u32[]{:S(2)}) copy-start(s32[4096]{0:T(1024)} %param.9) | copy-start | bytes 49156
  34.6 15.6 %copy-start.4 = (bf16[2,256,256]{2,1,0:T(8,128)(2,1)}, bf16[2,256,256]{2,1,0:T(8,128)(2,1)S(1)}, u32[]{:S(2)}) copy-start(bf16[2,256,256]{2,1,0:T(8,128)(2,1)S(1)} %collective-permute-done.p2_ref) | copy-start | bytes 786436
  34.6 15.6 %collective-permute-start.1 = (bf16[2,256,256]{2,1,0:T(8,128)(2,1)S(1)}, bf16[2,256,256]{2,1,0:T(8,128)(2,1)S(1)}, u32[]{:S(2)}, u32[]{:S(2)}) collective-permute-start(bf16[2,256,256]{2,1,0:T(8,128)(2,1)S(1)} %collective-permute-done.p2_ref), channel_id=1, source_target_pairs={{0,2},{1,3},{2,4},{3,5},{4,6},{5,7},{6,8},{7,9},{8,10},{9,11},{10,... | collective-permute-start | bytes 786440 | tf_op jit(solution)/shard_map/ppermute | solution.py:21
  41.4 18.3 %collective-permute-start.8 = (bf16[2,512,256]{2,1,0:T(8,128)(2,1)S(1)}, bf16[2,512,256]{2,1,0:T(8,128)(2,1)S(1)}, u32[]{:S(2)}, u32[]{:S(2)}) collective-permute-start(bf16[2,512,256]{2,1,0:T(8,128)(2,1)S(1)} %maximum_select_fusion.2), channel_id=1, source_target_pairs={{0,1},{1,0},{2,3},{3,2},{4,5},{5,4},{6,7},{7,6},{8,9},{9,8},{10,11... | collective-permute-start | bytes 1572872 | tf_op jit(solution)/shard_map/ppermute | solution.py:25
  47.0 22.2 %collective-permute-start.5 = (bf16[2,512,256]{2,1,0:T(8,128)(2,1)S(1)}, bf16[2,512,256]{2,1,0:T(8,128)(2,1)}, u32[]{:S(2)}, u32[]{:S(2)}) collective-permute-start(bf16[2,512,256]{2,1,0:T(8,128)(2,1)S(1)} %maximum_select_fusion.1), channel_id=1, source_target_pairs={{0,1},{1,0},{2,3},{3,2},{4,5},{5,4},{6,7},{7,6},{8,9},{9,8},{10,11... | collective-permute-start | bytes 1572872 | tf_op jit(solution)/shard_map/ppermute | solution.py:25
  50.3 28.1 %collective-permute-start.2 = (bf16[2,512,256]{2,1,0:T(8,128)(2,1)S(1)}, bf16[2,512,256]{2,1,0:T(8,128)(2,1)S(1)}, u32[]{:S(2)}, u32[]{:S(2)}) collective-permute-start(bf16[2,512,256]{2,1,0:T(8,128)(2,1)S(1)} %maximum_select_fusion), channel_id=1, source_target_pairs={{0,1},{1,0},{2,3},{3,2},{4,5},{5,4},{6,7},{7,6},{8,9},{9,8},{10,11... | collective-permute-start | bytes 1572872 | tf_op jit(solution)/shard_map/ppermute | solution.py:25
  59.1 32.5 %collective-permute-start.12 = (bf16[2,512,256]{2,1,0:T(8,128)(2,1)}, bf16[2,512,256]{2,1,0:T(8,128)(2,1)S(1)}, u32[]{:S(2)}, u32[]{:S(2)}) collective-permute-start(bf16[2,512,256]{2,1,0:T(8,128)(2,1)} %get-tuple-element.37), channel_id=1, source_target_pairs={{0,1},{1,0},{2,3},{3,2},{4,5},{5,4},{6,7},{7,6},{8,9},{9,8},{10,11... | collective-permute-start | bytes 1572872 | tf_op jit(solution)/shard_map/ppermute | solution.py:25
  69.0 22.8 %collective-permute-start.15 = (bf16[2,512,256]{2,1,0:T(8,128)(2,1)}, bf16[2,512,256]{2,1,0:T(8,128)(2,1)S(1)}, u32[]{:S(2)}, u32[]{:S(2)}) collective-permute-start(bf16[2,512,256]{2,1,0:T(8,128)(2,1)} %get-tuple-element.41), channel_id=1, source_target_pairs={{0,1},{1,0},{2,3},{3,2},{4,5},{5,4},{6,7},{7,6},{8,9},{9,8},{10,11... | collective-permute-start | bytes 1572872 | tf_op jit(solution)/shard_map/ppermute | solution.py:25
  77.7 14.4 %collective-permute-start.18 = (bf16[2,512,256]{2,1,0:T(8,128)(2,1)}, bf16[2,512,256]{2,1,0:T(8,128)(2,1)S(1)}, u32[]{:S(2)}, u32[]{:S(2)}) collective-permute-start(bf16[2,512,256]{2,1,0:T(8,128)(2,1)} %get-tuple-element.45), channel_id=1, source_target_pairs={{0,1},{1,0},{2,3},{3,2},{4,5},{5,4},{6,7},{7,6},{8,9},{9,8},{10,11... | collective-permute-start | bytes 1572872 | tf_op jit(solution)/shard_map/ppermute | solution.py:25
  87.8 8.2 %collective-permute-start.21 = (bf16[2,512,256]{2,1,0:T(8,128)(2,1)}, bf16[2,512,256]{2,1,0:T(8,128)(2,1)S(1)}, u32[]{:S(2)}, u32[]{:S(2)}) collective-permute-start(bf16[2,512,256]{2,1,0:T(8,128)(2,1)} %get-tuple-element.49), channel_id=1, source_target_pairs={{0,1},{1,0},{2,3},{3,2},{4,5},{5,4},{6,7},{7,6},{8,9},{9,8},{10,11... | collective-permute-start | bytes 1572872 | tf_op jit(solution)/shard_map/ppermute | solution.py:25
  91.8 10.9 %collective-permute-start.13 = (bf16[2,256,256]{2,1,0:T(8,128)(2,1)S(1)}, bf16[2,256,256]{2,1,0:T(8,128)(2,1)S(1)}, u32[]{:S(2)}, u32[]{:S(2)}) collective-permute-start(bf16[2,256,256]{2,1,0:T(8,128)(2,1)S(1)} %fusion), channel_id=1, source_target_pairs={{0,14},{1,15},{2,0},{3,1},{4,2},{5,3},{6,4},{7,5},{8,6},{9,7},{10,... | collective-permute-start | bytes 786440 | tf_op jit(solution)/shard_map/ppermute | solution.py:21
  92.0 16.3 %collective-permute-start.16 = (bf16[2,256,256]{2,1,0:T(8,128)(2,1)S(1)}, bf16[2,256,256]{2,1,0:T(8,128)(2,1)S(1)}, u32[]{:S(2)}, u32[]{:S(2)}) collective-permute-start(bf16[2,256,256]{2,1,0:T(8,128)(2,1)S(1)} %fusion.1), channel_id=1, source_target_pairs={{0,14},{1,15},{2,0},{3,1},{4,2},{5,3},{6,4},{7,5},{8,6},{9,7},{10,... | collective-permute-start | bytes 786440 | tf_op jit(solution)/shard_map/ppermute | solution.py:21
  92.7 21.2 %collective-permute-start.19 = (bf16[2,256,256]{2,1,0:T(8,128)(2,1)S(1)}, bf16[2,256,256]{2,1,0:T(8,128)(2,1)S(1)}, u32[]{:S(2)}, u32[]{:S(2)}) collective-permute-start(bf16[2,256,256]{2,1,0:T(8,128)(2,1)S(1)} %fusion.2), channel_id=1, source_target_pairs={{0,14},{1,15},{2,0},{3,1},{4,2},{5,3},{6,4},{7,5},{8,6},{9,7},{10,... | collective-permute-start | bytes 786440 | tf_op jit(solution)/shard_map/ppermute | solution.py:21
  96.0 12.3 %copy-start.7 = (bf16[2,256,256]{2,1,0:T(8,128)(2,1)S(1)}, bf16[2,256,256]{2,1,0:T(8,128)(2,1)}, u32[]{:S(2)}) copy-start(bf16[2,256,256]{2,1,0:T(8,128)(2,1)} %get-tuple-element.42) | copy-start | bytes 786436
  96.1 23.5 %collective-permute-start.22 = (bf16[2,256,256]{2,1,0:T(8,128)(2,1)S(1)}, bf16[2,256,256]{2,1,0:T(8,128)(2,1)S(1)}, u32[]{:S(2)}, u32[]{:S(2)}) collective-permute-start(bf16[2,256,256]{2,1,0:T(8,128)(2,1)S(1)} %fusion.3), channel_id=1, source_target_pairs={{0,14},{1,15},{2,0},{3,1},{4,2},{5,3},{6,4},{7,5},{8,6},{9,7},{10,... | collective-permute-start | bytes 786440 | tf_op jit(solution)/shard_map/ppermute | solution.py:21
  102.7 11.2 %copy-start.8 = (bf16[2,256,256]{2,1,0:T(8,128)(2,1)S(1)}, bf16[2,256,256]{2,1,0:T(8,128)(2,1)}, u32[]{:S(2)}) copy-start(bf16[2,256,256]{2,1,0:T(8,128)(2,1)} %get-tuple-element.46) | copy-start | bytes 786436
  102.8 22.3 %collective-permute-start.14 = (bf16[2,256,256]{2,1,0:T(8,128)(2,1)S(1)}, bf16[2,256,256]{2,1,0:T(8,128)(2,1)S(1)}, u32[]{:S(2)}, u32[]{:S(2)}) collective-permute-start(bf16[2,256,256]{2,1,0:T(8,128)(2,1)S(1)} %add_convert_fusion.3), channel_id=1, source_target_pairs={{0,14},{1,15},{2,0},{3,1},{4,2},{5,3},{6,4},{7,5},{8,6},{9,7},{10,... | collective-permute-start | bytes 786440 | tf_op jit(solution)/shard_map/ppermute | solution.py:21
  108.3 11.2 %copy-start.9 = (bf16[2,256,256]{2,1,0:T(8,128)(2,1)S(1)}, bf16[2,256,256]{2,1,0:T(8,128)(2,1)}, u32[]{:S(2)}) copy-start(bf16[2,256,256]{2,1,0:T(8,128)(2,1)} %get-tuple-element.50) | copy-start | bytes 786436
  108.5 22.3 %collective-permute-start.17 = (bf16[2,256,256]{2,1,0:T(8,128)(2,1)S(1)}, bf16[2,256,256]{2,1,0:T(8,128)(2,1)S(1)}, u32[]{:S(2)}, u32[]{:S(2)}) collective-permute-start(bf16[2,256,256]{2,1,0:T(8,128)(2,1)S(1)} %add_convert_fusion.2), channel_id=1, source_target_pairs={{0,14},{1,15},{2,0},{3,1},{4,2},{5,3},{6,4},{7,5},{8,6},{9,7},{10,... | collective-permute-start | bytes 786440 | tf_op jit(solution)/shard_map/ppermute | solution.py:21
  114.1 22.3 %collective-permute-start.20 = (bf16[2,256,256]{2,1,0:T(8,128)(2,1)S(1)}, bf16[2,256,256]{2,1,0:T(8,128)(2,1)S(1)}, u32[]{:S(2)}, u32[]{:S(2)}) collective-permute-start(bf16[2,256,256]{2,1,0:T(8,128)(2,1)S(1)} %add_convert_fusion.1), channel_id=1, source_target_pairs={{0,14},{1,15},{2,0},{3,1},{4,2},{5,3},{6,4},{7,5},{8,6},{9,7},{10,... | collective-permute-start | bytes 786440 | tf_op jit(solution)/shard_map/ppermute | solution.py:21
  119.7 22.1 %collective-permute-start.23 = (bf16[2,256,256]{2,1,0:T(8,128)(2,1)S(1)}, bf16[2,256,256]{2,1,0:T(8,128)(2,1)S(1)}, u32[]{:S(2)}, u32[]{:S(2)}) collective-permute-start(bf16[2,256,256]{2,1,0:T(8,128)(2,1)S(1)} %add_convert_fusion), channel_id=1, source_target_pairs={{0,14},{1,15},{2,0},{3,1},{4,2},{5,3},{6,4},{7,5},{8,6},{9,7},{10,... | collective-permute-start | bytes 786440 | tf_op jit(solution)/shard_map/ppermute | solution.py:21
  (14 other events, 77.7 us)

commit v8 on v7

--- a/solution.py
+++ b/solution.py
@@ -7,7 +7,7 @@
 
 
 WINDOW = 1024
-CHUNKS = 4
+CHUNKS = 2
 
 
 QUERY_SCALE = 168.0 ** (-0.5)
@@ -25,39 +25,33 @@
     return lax.ppermute(block, axis, [(i, i ^ 1) for i in range(lax.axis_size(axis))])
 
 
-def attention_kernel(qd_ref, kd_ref, q_ref, g_ref, p4_ref, p3_ref, p2_ref, p1_ref, p0_ref, *refs):
+def attention_kernel(bias_ref, q_ref, g_ref, p4_ref, p3_ref, p2_ref, p1_ref, p0_ref, *refs):
     o_ref, dq_ref, d13_ref, d4_ref, d2_ref, d0_ref = refs[-6:]
     rows = q_ref.shape[0]
     head_size = p0_ref.shape[2]
     pieces = (p4_ref, p3_ref, p2_ref, p1_ref, p0_ref)
-    cols = rows * len(pieces)
-    q_pos = lax.broadcasted_iota(jnp.int32, (rows, cols), 0)
-    k_pos = lax.broadcasted_iota(jnp.int32, (rows, cols), 1)
-    allowed = (qd_ref[...] == kd_ref[...]) & (k_pos > q_pos) & (k_pos <= q_pos + WINDOW)
     k = jnp.concatenate([p[0] for p in pieces], axis=0)
     v = jnp.concatenate([p[1] for p in pieces], axis=0)
-    dk_acc = jnp.zeros((cols, head_size), jnp.float32)
-    dv_acc = jnp.zeros((cols, head_size), jnp.float32)
-    for a in range(q_ref.shape[1] // head_size):
-        lanes = slice(a * head_size, (a + 1) * head_size)
-        q = q_ref[:, lanes]
-        g = g_ref[:, lanes]
-        scores = QUERY_SCALE * lax.dot_general(q, k, NT, preferred_element_type=jnp.float32)
-        masked = jnp.where(allowed, scores, -jnp.inf)
-        row_max = jnp.max(masked, axis=1, keepdims=True)
-        unnorm = jnp.exp(masked - row_max)
-        inv = 1.0 / jnp.sum(unnorm, axis=1, keepdims=True)
-        weights = unnorm * inv
-        weights_b = weights.astype(jnp.bfloat16)
-        attended = jnp.dot(weights_b, v, preferred_element_type=jnp.float32).astype(jnp.bfloat16)
-        o_ref[:, lanes] = attended
-        row_dot = jnp.sum(g.astype(jnp.float32) * attended.astype(jnp.float32), axis=1, keepdims=True)
-        dprob = lax.dot_general(g, v, NT, preferred_element_type=jnp.float32)
-        dscore = (weights * (dprob - row_dot)).astype(jnp.bfloat16)
-        dq = QUERY_SCALE * jnp.dot(dscore, k, preferred_element_type=jnp.float32)
-        dq_ref[:, lanes] = dq.astype(jnp.bfloat16)
-        dk_acc = dk_acc + lax.dot_general(dscore, q, TN, preferred_element_type=jnp.float32)
-        dv_acc = dv_acc + lax.dot_general(weights_b, g, TN, preferred_element_type=jnp.float32)
+    heads = q_ref.shape[1] // head_size
+    q = jnp.concatenate([q_ref[:, a * head_size:(a + 1) * head_size] for a in range(heads)], 0)
+    g = jnp.concatenate([g_ref[:, a * head_size:(a + 1) * head_size] for a in range(heads)], 0)
+    scores = QUERY_SCALE * lax.dot_general(q, k, NT, preferred_element_type=jnp.float32)
+    masked = scores + bias_ref[...]
+    row_max = jnp.max(masked, axis=1, keepdims=True)
+    unnorm = jnp.exp(masked - row_max)
+    inv = 1.0 / jnp.sum(unnorm, axis=1, keepdims=True)
+    weights = unnorm * inv
+    weights_b = weights.astype(jnp.bfloat16)
+    attended = jnp.dot(weights_b, v, preferred_element_type=jnp.float32).astype(jnp.bfloat16)
+    row_dot = jnp.sum(g.astype(jnp.float32) * attended.astype(jnp.float32), axis=1, keepdims=True)
+    dprob = lax.dot_general(g, v, NT, preferred_element_type=jnp.float32)
+    dscore = (weights * (dprob - row_dot)).astype(jnp.bfloat16)
+    dq = (QUERY_SCALE * jnp.dot(dscore, k, preferred_element_type=jnp.float32)).astype(jnp.bfloat16)
+    for a in range(heads):
+        o_ref[:, a * head_size:(a + 1) * head_size] = attended[a * rows:(a + 1) * rows]
+        dq_ref[:, a * head_size:(a + 1) * head_size] = dq[a * rows:(a + 1) * rows]
+    dk_acc = lax.dot_general(dscore, q, TN, preferred_element_type=jnp.float32)
+    dv_acc = lax.dot_general(weights_b, g, TN, preferred_element_type=jnp.float32)
     for j, term in enumerate(((QUERY_SCALE * dk_acc).astype(jnp.bfloat16), dv_acc.astype(jnp.bfloat16))):
         d4_ref[j] = term[0:rows]
         d13_ref[j, rows:2 * rows] = term[rows:2 * rows]
@@ -66,7 +60,7 @@
         d0_ref[j] = term[4 * rows:5 * rows]
 
 
-def attention(q2, g2, pieces, q_docs, k_docs, head_size, chunk, bufs):
+def attention(q2, g2, pieces, bias, head_size, chunk, bufs):
     rows = q2.shape[0]
     pieces, blocks = zip(*pieces)
     groups = pieces[0].shape[2] // head_size
@@ -82,8 +76,7 @@
         attention_kernel,
         grid=(groups,),
         in_specs=[
-            pl.BlockSpec((rows, 1), lambda i: (0, 0)),
-            pl.BlockSpec((1, cols), lambda i: (0, 0)),
+            pl.BlockSpec(bias.shape, lambda i: (0, 0)),
             q_spec,
             q_spec,
         ] + [pl.BlockSpec((2, rows, head_size), lambda i, b=b: (0, b, i)) for b in blocks]
@@ -97,12 +90,12 @@
             piece_shape,
             piece_shape,
         ],
-        input_output_aliases={4 + len(pieces) + j: j for j in range(len(bufs))},
+        input_output_aliases={3 + len(pieces) + j: j for j in range(len(bufs))},
         compiler_params=pltpu.CompilerParams(dimension_semantics=("arbitrary",)),
         cost_estimate=pl.CostEstimate(
             flops=flops, transcendentals=rows * cols * per_group * groups // head_size,
             bytes_accessed=bytes_accessed),
-    )(q_docs, k_docs, q2, g2, *pieces, *bufs)
+    )(bias, q2, g2, *pieces, *bufs)
 
 
 def wide(x):
@@ -133,6 +126,7 @@
 
 def staged(query_heads, key_heads, value_heads, grad_out, doc_ids):
     row_count = query_heads.shape[0]
+    groups = key_heads.shape[1]
     head_size = key_heads.shape[2]
     assert WINDOW // row_count == 4
     piece_pos = lax.axis_index("ctx")
@@ -142,6 +136,12 @@
     first_row = piece_pos * row_count
     q_docs = lax.dynamic_slice_in_dim(doc_ids, first_row, row_count, 0).reshape(row_count, 1)
     k_docs = lax.dynamic_slice_in_dim(pad_docs, first_row, WINDOW + row_count, 0).reshape(1, -1)
+    cols = k_docs.shape[1]
+    q_pos = lax.broadcasted_iota(jnp.int32, (row_count, cols), 0)
+    k_pos = lax.broadcasted_iota(jnp.int32, (row_count, cols), 1)
+    allowed = (q_docs == k_docs) & (k_pos > q_pos) & (k_pos <= q_pos + WINDOW)
+    bias = jnp.where(allowed, 0.0, -jnp.inf).astype(jnp.float32)
+    bias = jnp.concatenate([bias] * (query_heads.shape[1] // groups), 0)
     q2 = query_heads.reshape(row_count, -1)
     g2 = grad_out.reshape(row_count, -1)
     k2 = key_heads.reshape(row_count, -1)
@@ -154,7 +154,7 @@
         own = jnp.stack([k2[:, lanes], v2[:, lanes]])
         pieces = forward_exchange(own, is_odd)
         o_buf, dq_buf, *terms = attention(
-            q2, g2, pieces, q_docs, k_docs, head_size, c, bufs)
+            q2, g2, pieces, bias, head_size, c, bufs)
         bufs = (o_buf, dq_buf)
         totals.append(backward_exchange(terms, is_odd))
     attended = o_buf.reshape(query_heads.shape)

time: 146 us -> 144 us (0.986)
  waiting for transfers between devices: 60.3 us -> 79 us
  starting transfers between devices: 27.6 us -> 13.1 us
  Pallas kernels: 34.1 us -> 30.7 us
  local copies, waits for them, and re-layouts: 12.5 us -> 10.1 us
    ppermute x16 -> x8, waiting for transfers between devices: 60.3 us -> 76.8 us  [shift(): lax.ppermute(block, axis, [(i, (i + distance) % size) for i in range(size)])]
    ppermute x16 -> x8, starting transfers between devices: 25.6 us -> 12 us  [shift(): lax.ppermute(block, axis, [(i, (i + distance) % size) for i in range(size)])]
    pallas_call x4 -> x2, Pallas kernels: 34.1 us -> 30.7 us  [attention(): pl.pallas_call(attention_kernel, grid=(groups,), in_specs=[pl.BlockSpec(b...]
    ppermute x8 -> x4, waiting for transfers between devices: 0.02 us -> 2.24 us  [swap(): lax.ppermute(block, axis, [(i, i ^ 1) for i in range(lax.axis_size(axis))])]
    another operation x4 -> x2, other arithmetic: 2.24 us -> 0.1 us  [staged(): own = jnp.stack([k2[:, lanes], v2[:, lanes]])]
    concatenate x0 -> x1, other arithmetic: none -> 1.71 us  [staged(): bias = jnp.concatenate([bias] * (query_heads.shape[1] // groups), 0)]
    select_n x4 -> x2, other arithmetic: 4.65 us -> 3.06 us  [forward_exchange(): jnp.where(is_odd, jnp.concatenate([back2, back4], 1), jnp.concatenate([ow...]
    unnamed x51 -> x39, local copies, waits for them, and re-layouts: 9.06 us -> 8.01 us
  transfers between devices with their start and end apart: 24 -> 12, of which waited for: 16 -> 9; matrix products, arithmetic and copies ran while one was open for 11% -> 8% of each run, Pallas kernels for 24% -> 22%
where the time goes in v8:
time: 144 us; the launch traced here: 142 us
  waiting for transfers between devices  79 us (55%)
  Pallas kernels  30.7 us (21%)
  starting transfers between devices  13.1 us (9%)
  local copies, waits for them, and re-layouts  10.1 us (7%)
  other arithmetic  7.85 us (5%)
    ppermute x8, waiting for transfers between devices, shift(): lax.ppermute(block, axis, [(i, (i + distance) % size) for i in range(size)])  76.8 us
    pallas_call x2, Pallas kernels, attention(): pl.pallas_call(attention_kernel, grid=(groups,), in_specs=[pl.BlockSpec(b...  30.7 us
    ppermute x8, starting transfers between devices, shift(): lax.ppermute(block, axis, [(i, (i + distance) % size) for i in range(size)])  12 us
    unnamed x39, local copies, waits for them, and re-layouts  8.01 us
    select_n x2, other arithmetic, forward_exchange(): jnp.where(is_odd, jnp.concatenate([back2, back4], 1), jnp.concatenate([ow...  3.06 us
  transfers between devices with their start and end apart: 12, of which 9 were waited for; matrix products, arithmetic and copies ran while one was open for 8% of the time, Pallas kernels for 22%

profile of v8, /device:TPU:100, one launch (start us, length us, event | category | flops | bytes accessed | tf_op | source)
XLA Modules:
  0.0 141.6 jit_solution(4664646018871992552)
XLA Ops:
  0.6 1.1 copy.23
  1.8 1.1 copy.24
  3.1 3.2 %collective-permute-start.3 = (bf16[2,256,512]{2,1,0:T(8,128)(2,1)S(1)}, bf16[2,256,512]{2,1,0:T(8,128)(2,1)S(1)}, u32[]{:S(2)}, u32[]{:S(2)}) collective-permute-start(bf16[2,256,512]{2,1,0:T(8,128)(2,1)S(1)} %pad_maximum_fusion.2.p0_ref), channel_id=1, source_target_pairs={{0,2},{1,3},{2,4},{3,5},{4,6},{5,7},{6,8},{7,9},{8,10},{9,11},{10,... | collective-permute-start | bytes 1572872 | tf_op jit(solution)/shard_map/ppermute | solution.py:21
  6.4 1.1 collective-permute-start
  7.5 11.2 %collective-permute-done.3.p2_ref = bf16[2,256,512]{2,1,0:T(8,128)(2,1)S(1)} collective-permute-done((bf16[2,256,512]{2,1,0:T(8,128)(2,1)S(1)}, bf16[2,256,512]{2,1,0:T(8,128)(2,1)S(1)}, u32[]{:S(2)}, u32[]{:S(2)}) %collective-permute-start.3) | collective-permute-done | bytes 524320 | tf_op jit(solution)/shard_map/ppermute | solution.py:21
  18.6 3.7 %collective-permute-start.4 = (bf16[2,256,512]{2,1,0:T(8,128)(2,1)S(1)}, bf16[2,256,512]{2,1,0:T(8,128)(2,1)}, u32[]{:S(2)}, u32[]{:S(2)}) collective-permute-start(bf16[2,256,512]{2,1,0:T(8,128)(2,1)S(1)} %collective-permute-done.3.p2_ref), channel_id=1, source_target_pairs={{0,2},{1,3},{2,4},{3,5},{4,6},{5,7},{6,8},{7,9},{8,10},{9,11},{10,... | collective-permute-start | bytes 1572872 | tf_op jit(solution)/shard_map/ppermute | solution.py:21
  22.5 7.4 %collective-permute-done.p2_ref = bf16[2,256,512]{2,1,0:T(8,128)(2,1)S(1)} collective-permute-done((bf16[2,256,512]{2,1,0:T(8,128)(2,1)S(1)}, bf16[2,256,512]{2,1,0:T(8,128)(2,1)S(1)}, u32[]{:S(2)}, u32[]{:S(2)}) %collective-permute-start) | collective-permute-done | bytes 524320 | tf_op jit(solution)/shard_map/ppermute | solution.py:21
  29.9 3.7 %collective-permute-start.1 = (bf16[2,256,512]{2,1,0:T(8,128)(2,1)S(1)}, bf16[2,256,512]{2,1,0:T(8,128)(2,1)S(1)}, u32[]{:S(2)}, u32[]{:S(2)}) collective-permute-start(bf16[2,256,512]{2,1,0:T(8,128)(2,1)S(1)} %collective-permute-done.p2_ref), channel_id=1, source_target_pairs={{0,2},{1,3},{2,4},{3,5},{4,6},{5,7},{6,8},{7,9},{8,10},{9,11},{10,... | collective-permute-start | bytes 1572872 | tf_op jit(solution)/shard_map/ppermute | solution.py:21
  33.5 7.5 %collective-permute-done.4.p4_ref = bf16[2,256,512]{2,1,0:T(8,128)(2,1)} collective-permute-done((bf16[2,256,512]{2,1,0:T(8,128)(2,1)S(1)}, bf16[2,256,512]{2,1,0:T(8,128)(2,1)}, u32[]{:S(2)}, u32[]{:S(2)}) %collective-permute-start.4) | collective-permute-done | bytes 524320 | tf_op jit(solution)/shard_map/ppermute | solution.py:21
  41.1 1.4 maximum_select_fusion.1
  42.6 0.4 fusion.2
  43.0 8.2 %collective-permute-done.1.p4_ref = bf16[2,256,512]{2,1,0:T(8,128)(2,1)S(1)} collective-permute-done((bf16[2,256,512]{2,1,0:T(8,128)(2,1)S(1)}, bf16[2,256,512]{2,1,0:T(8,128)(2,1)S(1)}, u32[]{:S(2)}, u32[]{:S(2)}) %collective-permute-start.1) | collective-permute-done | bytes 524320 | tf_op jit(solution)/shard_map/ppermute | solution.py:21
  51.2 1.7 %maximum_select_fusion = bf16[2,512,512]{2,1,0:T(8,128)(2,1)S(1)} fusion(bf16[2,256,512]{2,1,0:T(8,128)(2,1)S(1)} %collective-permute-done.1.p4_ref, bf16[2,256,512]{2,1,0:T(8,128)(2,1)} %copy-done.9, bf16[1,256,512]{2,1,0:T(8,128)(2,1)S(1)} %get-tuple-element.33, bf16[1,256,512]{2,1,0:T(8,128)(2,1)S(1)} %get-tuple-element.34, pred[]{:T(512)S(6)} %eq.21), kind=kLoop, calls=%fused_computation.13 | loop fusion | flops 5767168 | bytes 2621441 | tf_op jit(solution)/shard_map/jit(_where)/select_n | solution.py:108
  53.0 1.7 %pad_maximum_fusion.bias_ref = f32[512,1280]{1,0:T(8,128)} fusion(f32[256,1280]{1,0:T(8,128)S(1)} %fusion.2), kind=kLoop, calls=%fused_computation | loop fusion | flops 655360 | bytes 3932160 | tf_op jit(solution)/shard_map/concatenate | solution.py:144
  54.7 0.4 copy-done.3
  55.1 1.8 %copy_bitcast_fusion = (bf16[256,2048]{1,0:T(8,128)(2,1)}, bf16[256,2048]{1,0:T(8,128)(2,1)}) fusion(bf16[32,8,16,128]{3,2,1,0:T(8,128)(2,1)S(1)} %bitcast.40, bf16[32,8,16,128]{3,2,1,0:T(8,128)(2,1)S(1)} %bitcast.41), kind=kLoop, calls=%fused_computation.11 | loop fusion | bytes 4194304 | tf_op jit(solution)/shard_map/reshape | solution.py:146
  57.0 1.0 copy-done.15
  58.0 15.3 %shard_map.84 = (bf16[256,2048]{1,0:T(8,128)(2,1)}, bf16[256,2048]{1,0:T(8,128)(2,1)}, bf16[2,512,512]{2,1,0:T(8,128)(2,1)}, bf16[2,256,512]{2,1,0:T(8,128)(2,1)...) custom-call(f32[512,1280]{1,0:T(8,128)} %pad_maximum_fusion.bias_ref, ...), custom_call_target="tpu_custom_call" | custom-call | flops 4026531840 | bytes 7340032 | tf_op jit(solution)/shard_map/pallas_call | solution.py:75
  73.2 0.3 collective-permute-start.6
  73.6 15.4 %shard_map.85 = (bf16[256,2048]{1,0:T(8,128)(2,1)}, bf16[256,2048]{1,0:T(8,128)(2,1)}, bf16[2,512,512]{2,1,0:T(8,128)(2,1)}, bf16[2,256,512]{2,1,0:T(8,128)(2,1)...) custom-call(f32[512,1280]{1,0:T(8,128)} %pad_maximum_fusion.bias_ref, ...), custom_call_target="tpu_custom_call", output_to_operand_aliasing={{0}: (8, {}), {1}: (9, {})} | custom-call | flops 4026531840 | bytes 7340032 | tf_op jit(solution)/shard_map/pallas_call | solution.py:75
  89.0 0.5 collective-permute-start.9
  89.8 2.2 %collective-permute-done.9 = bf16[2,512,512]{2,1,0:T(8,128)(2,1)S(1)} collective-permute-done((bf16[2,512,512]{2,1,0:T(8,128)(2,1)}, bf16[2,512,512]{2,1,0:T(8,128)(2,1)S(1)}, u32[]{:S(2)}, u32[]{:S(2)}) %collective-permute-start.9) | collective-permute-done | bytes 1048608 | tf_op jit(solution)/shard_map/ppermute | solution.py:25
  92.1 1.3 fusion.4
  93.4 12.9 %collective-permute-done.7 = bf16[2,256,512]{2,1,0:T(8,128)(2,1)S(1)} collective-permute-done((bf16[2,256,512]{2,1,0:T(8,128)(2,1)S(1)}, bf16[2,256,512]{2,1,0:T(8,128)(2,1)S(1)}, u32[]{:S(2)}, u32[]{:S(2)}) %collective-permute-start.7) | collective-permute-done | bytes 524320 | tf_op jit(solution)/shard_map/ppermute | solution.py:21
  106.3 0.3 add_convert_fusion.1
  106.7 10.9 %collective-permute-done.10 = bf16[2,256,512]{2,1,0:T(8,128)(2,1)S(1)} collective-permute-done((bf16[2,256,512]{2,1,0:T(8,128)(2,1)S(1)}, bf16[2,256,512]{2,1,0:T(8,128)(2,1)S(1)}, u32[]{:S(2)}, u32[]{:S(2)}) %collective-permute-start.10) | collective-permute-done | bytes 524320 | tf_op jit(solution)/shard_map/ppermute | solution.py:21
  117.9 1.2 copy.15
  119.1 1.2 copy.16
  120.3 8.4 %collective-permute-done.8 = bf16[2,256,512]{2,1,0:T(8,128)(2,1)S(1)} collective-permute-done((bf16[2,256,512]{2,1,0:T(8,128)(2,1)S(1)}, bf16[2,256,512]{2,1,0:T(8,128)(2,1)S(1)}, u32[]{:S(2)}, u32[]{:S(2)}) %collective-permute-start.8) | collective-permute-done | bytes 524320 | tf_op jit(solution)/shard_map/ppermute | solution.py:21
  129.0 10.4 %collective-permute-done.11 = bf16[2,256,512]{2,1,0:T(8,128)(2,1)S(1)} collective-permute-done((bf16[2,256,512]{2,1,0:T(8,128)(2,1)S(1)}, bf16[2,256,512]{2,1,0:T(8,128)(2,1)S(1)}, u32[]{:S(2)}, u32[]{:S(2)}) %collective-permute-start.11) | collective-permute-done | bytes 524320 | tf_op jit(solution)/shard_map/ppermute | solution.py:21
  139.8 0.9 copy.17
  140.7 0.9 copy.18
  (51 shorter events, 2.0 us)
Async XLA Ops:
  2.9 19.4 %copy-start.14 = (s32[4096]{0:T(1024)S(1)}, s32[4096]{0:T(1024)}, u32[]{:S(2)}) copy-start(s32[4096]{0:T(1024)} %param.9) | copy-start | bytes 49156
  3.1 39.9 %copy-start.7 = (bf16[2,256,512]{2,1,0:T(8,128)(2,1)}, bf16[2,256,512]{2,1,0:T(8,128)(2,1)S(1)}, u32[]{:S(2)}) copy-start(bf16[2,256,512]{2,1,0:T(8,128)(2,1)S(1)} %pad_maximum_fusion.2.p0_ref) | copy-start | bytes 1572868
  3.1 15.5 %collective-permute-start.3 = (bf16[2,256,512]{2,1,0:T(8,128)(2,1)S(1)}, bf16[2,256,512]{2,1,0:T(8,128)(2,1)S(1)}, u32[]{:S(2)}, u32[]{:S(2)}) collective-permute-start(bf16[2,256,512]{2,1,0:T(8,128)(2,1)S(1)} %pad_maximum_fusion.2.p0_ref), channel_id=1, source_target_pairs={{0,2},{1,3},{2,4},{3,5},{4,6},{5,7},{6,8},{7,9},{8,10},{9,11},{10,... | collective-permute-start | bytes 1572872 | tf_op jit(solution)/shard_map/ppermute | solution.py:21
  6.4 46.5 %copy-start.6 = (bf16[2,256,512]{2,1,0:T(8,128)(2,1)}, bf16[2,256,512]{2,1,0:T(8,128)(2,1)S(1)}, u32[]{:S(2)}) copy-start(bf16[2,256,512]{2,1,0:T(8,128)(2,1)S(1)} %pad_maximum_fusion.1.p0_ref) | copy-start | bytes 1572868
  6.4 23.5 %collective-permute-start = (bf16[2,256,512]{2,1,0:T(8,128)(2,1)S(1)}, bf16[2,256,512]{2,1,0:T(8,128)(2,1)S(1)}, u32[]{:S(2)}, u32[]{:S(2)}) collective-permute-start(bf16[2,256,512]{2,1,0:T(8,128)(2,1)S(1)} %pad_maximum_fusion.1.p0_ref), channel_id=1, source_target_pairs={{0,2},{1,3},{2,4},{3,5},{4,6},{5,7},{6,8},{7,9},{8,10},{9,11},{10,... | collective-permute-start | bytes 1572872 | tf_op jit(solution)/shard_map/ppermute | solution.py:21
  18.6 24.4 %copy-start.10 = (bf16[2,256,512]{2,1,0:T(8,128)(2,1)}, bf16[2,256,512]{2,1,0:T(8,128)(2,1)S(1)}, u32[]{:S(2)}) copy-start(bf16[2,256,512]{2,1,0:T(8,128)(2,1)S(1)} %collective-permute-done.3.p2_ref) | copy-start | bytes 1572868
  18.6 22.5 %collective-permute-start.4 = (bf16[2,256,512]{2,1,0:T(8,128)(2,1)S(1)}, bf16[2,256,512]{2,1,0:T(8,128)(2,1)}, u32[]{:S(2)}, u32[]{:S(2)}) collective-permute-start(bf16[2,256,512]{2,1,0:T(8,128)(2,1)S(1)} %collective-permute-done.3.p2_ref), channel_id=1, source_target_pairs={{0,2},{1,3},{2,4},{3,5},{4,6},{5,7},{6,8},{7,9},{8,10},{9,11},{10,... | collective-permute-start | bytes 1572872 | tf_op jit(solution)/shard_map/ppermute | solution.py:21
  29.8 13.2 %copy-start.9 = (bf16[2,256,512]{2,1,0:T(8,128)(2,1)}, bf16[2,256,512]{2,1,0:T(8,128)(2,1)S(1)}, u32[]{:S(2)}) copy-start(bf16[2,256,512]{2,1,0:T(8,128)(2,1)S(1)} %collective-permute-done.p2_ref) | copy-start | bytes 1572868
  29.9 21.3 %collective-permute-start.1 = (bf16[2,256,512]{2,1,0:T(8,128)(2,1)S(1)}, bf16[2,256,512]{2,1,0:T(8,128)(2,1)S(1)}, u32[]{:S(2)}, u32[]{:S(2)}) collective-permute-start(bf16[2,256,512]{2,1,0:T(8,128)(2,1)S(1)} %collective-permute-done.p2_ref), channel_id=1, source_target_pairs={{0,2},{1,3},{2,4},{3,5},{4,6},{5,7},{6,8},{7,9},{8,10},{9,11},{10,... | collective-permute-start | bytes 1572872 | tf_op jit(solution)/shard_map/ppermute | solution.py:21
  42.5 14.5 %collective-permute-start.5 = (bf16[2,512,512]{2,1,0:T(8,128)(2,1)S(1)}, bf16[2,512,512]{2,1,0:T(8,128)(2,1)S(1)}, u32[]{:S(2)}, u32[]{:S(2)}) collective-permute-start(bf16[2,512,512]{2,1,0:T(8,128)(2,1)S(1)} %maximum_select_fusion.1), channel_id=1, source_target_pairs={{0,1},{1,0},{2,3},{3,2},{4,5},{5,4},{6,7},{7,6},{8,9},{9,8},{10,11... | collective-permute-start | bytes 3145736 | tf_op jit(solution)/shard_map/ppermute | solution.py:25
  51.2 1.7 %copy-start.11 = (bf16[2,256,512]{2,1,0:T(8,128)(2,1)}, bf16[2,256,512]{2,1,0:T(8,128)(2,1)S(1)}, u32[]{:S(2)}) copy-start(bf16[2,256,512]{2,1,0:T(8,128)(2,1)S(1)} %collective-permute-done.1.p4_ref) | copy-start | bytes 1572868
  52.9 1.8 %copy-start.2 = (bf16[256,16,128]{2,1,0:T(8,128)(2,1)S(1)}, bf16[256,16,128]{2,1,0:T(8,128)(2,1)}, u32[]{:S(2)}) copy-start(bf16[256,16,128]{2,1,0:T(8,128)(2,1)} %param.8) | copy-start | bytes 3145732
  52.9 2.2 %copy-start.3 = (bf16[256,16,128]{2,1,0:T(8,128)(2,1)S(1)}, bf16[256,16,128]{2,1,0:T(8,128)(2,1)}, u32[]{:S(2)}) copy-start(bf16[256,16,128]{2,1,0:T(8,128)(2,1)} %param.5) | copy-start | bytes 3145732
  52.9 20.7 %collective-permute-start.2 = (bf16[2,512,512]{2,1,0:T(8,128)(2,1)S(1)}, bf16[2,512,512]{2,1,0:T(8,128)(2,1)}, u32[]{:S(2)}, u32[]{:S(2)}) collective-permute-start(bf16[2,512,512]{2,1,0:T(8,128)(2,1)S(1)} %maximum_select_fusion), channel_id=1, source_target_pairs={{0,1},{1,0},{2,3},{3,2},{4,5},{5,4},{6,7},{7,6},{8,9},{9,8},{10,11... | collective-permute-start | bytes 3145736 | tf_op jit(solution)/shard_map/ppermute | solution.py:25
  57.0 1.0 copy-start.15
  73.2 16.3 %collective-permute-start.6 = (bf16[2,512,512]{2,1,0:T(8,128)(2,1)}, bf16[2,512,512]{2,1,0:T(8,128)(2,1)S(1)}, u32[]{:S(2)}, u32[]{:S(2)}) collective-permute-start(bf16[2,512,512]{2,1,0:T(8,128)(2,1)} %get-tuple-element.21), channel_id=1, source_target_pairs={{0,1},{1,0},{2,3},{3,2},{4,5},{5,4},{6,7},{7,6},{8,9},{9,8},{10,11... | collective-permute-start | bytes 3145736 | tf_op jit(solution)/shard_map/ppermute | solution.py:25
  73.6 16.0 %copy-start.8 = (bf16[2,256,512]{2,1,0:T(8,128)(2,1)S(1)}, bf16[2,256,512]{2,1,0:T(8,128)(2,1)}, u32[]{:S(2)}) copy-start(bf16[2,256,512]{2,1,0:T(8,128)(2,1)} %get-tuple-element.20) | copy-start | bytes 1572868
  89.0 17.3 %copy-start.12 = (bf16[2,256,512]{2,1,0:T(8,128)(2,1)S(1)}, bf16[2,256,512]{2,1,0:T(8,128)(2,1)}, u32[]{:S(2)}) copy-start(bf16[2,256,512]{2,1,0:T(8,128)(2,1)} %get-tuple-element.22) | copy-start | bytes 1572868
  89.0 3.0 %collective-permute-start.9 = (bf16[2,512,512]{2,1,0:T(8,128)(2,1)}, bf16[2,512,512]{2,1,0:T(8,128)(2,1)S(1)}, u32[]{:S(2)}, u32[]{:S(2)}) collective-permute-start(bf16[2,512,512]{2,1,0:T(8,128)(2,1)} %get-tuple-element.25), channel_id=1, source_target_pairs={{0,1},{1,0},{2,3},{3,2},{4,5},{5,4},{6,7},{7,6},{8,9},{9,8},{10,11... | collective-permute-start | bytes 3145736 | tf_op jit(solution)/shard_map/ppermute | solution.py:25
  89.7 16.6 %collective-permute-start.7 = (bf16[2,256,512]{2,1,0:T(8,128)(2,1)S(1)}, bf16[2,256,512]{2,1,0:T(8,128)(2,1)S(1)}, u32[]{:S(2)}, u32[]{:S(2)}) collective-permute-start(bf16[2,256,512]{2,1,0:T(8,128)(2,1)S(1)} %fusion.3), channel_id=1, source_target_pairs={{0,14},{1,15},{2,0},{3,1},{4,2},{5,3},{6,4},{7,5},{8,6},{9,7},{10,... | collective-permute-start | bytes 1572872 | tf_op jit(solution)/shard_map/ppermute | solution.py:21
  92.1 25.5 %copy-start.13 = (bf16[2,256,512]{2,1,0:T(8,128)(2,1)S(1)}, bf16[2,256,512]{2,1,0:T(8,128)(2,1)}, u32[]{:S(2)}) copy-start(bf16[2,256,512]{2,1,0:T(8,128)(2,1)} %get-tuple-element.26) | copy-start | bytes 1572868
  93.3 24.2 %collective-permute-start.10 = (bf16[2,256,512]{2,1,0:T(8,128)(2,1)S(1)}, bf16[2,256,512]{2,1,0:T(8,128)(2,1)S(1)}, u32[]{:S(2)}, u32[]{:S(2)}) collective-permute-start(bf16[2,256,512]{2,1,0:T(8,128)(2,1)S(1)} %fusion.4), channel_id=1, source_target_pairs={{0,14},{1,15},{2,0},{3,1},{4,2},{5,3},{6,4},{7,5},{8,6},{9,7},{10,... | collective-permute-start | bytes 1572872 | tf_op jit(solution)/shard_map/ppermute | solution.py:21
  106.3 11.6 %copy-start = (bf16[256,2048]{1,0:T(8,128)(2,1)S(1)}, bf16[256,2048]{1,0:T(8,128)(2,1)}, u32[]{:S(2)}) copy-start(bf16[256,2048]{1,0:T(8,128)(2,1)} %get-tuple-element.18) | copy-start | bytes 3145732
  106.6 22.2 %collective-permute-start.8 = (bf16[2,256,512]{2,1,0:T(8,128)(2,1)S(1)}, bf16[2,256,512]{2,1,0:T(8,128)(2,1)S(1)}, u32[]{:S(2)}, u32[]{:S(2)}) collective-permute-start(bf16[2,256,512]{2,1,0:T(8,128)(2,1)S(1)} %add_convert_fusion.1), channel_id=1, source_target_pairs={{0,14},{1,15},{2,0},{3,1},{4,2},{5,3},{6,4},{7,5},{8,6},{9,7},{10,... | collective-permute-start | bytes 1572872 | tf_op jit(solution)/shard_map/ppermute | solution.py:21
  117.5 1.6 %copy-start.1 = (bf16[256,2048]{1,0:T(8,128)(2,1)S(1)}, bf16[256,2048]{1,0:T(8,128)(2,1)}, u32[]{:S(2)}) copy-start(bf16[256,2048]{1,0:T(8,128)(2,1)} %get-tuple-element.19) | copy-start | bytes 3145732
  117.8 21.6 %collective-permute-start.11 = (bf16[2,256,512]{2,1,0:T(8,128)(2,1)S(1)}, bf16[2,256,512]{2,1,0:T(8,128)(2,1)S(1)}, u32[]{:S(2)}, u32[]{:S(2)}) collective-permute-start(bf16[2,256,512]{2,1,0:T(8,128)(2,1)S(1)} %add_convert_fusion), channel_id=1, source_target_pairs={{0,14},{1,15},{2,0},{3,1},{4,2},{5,3},{6,4},{7,5},{8,6},{9,7},{10,... | collective-permute-start | bytes 1572872 | tf_op jit(solution)/shard_map/ppermute | solution.py:21
  117.9 10.9 %copy-start.4 = (bf16[2,256,512]{2,1,0:T(8,128)(2,1)S(1)}, bf16[2,256,512]{2,1,0:T(8,128)(2,1)}, u32[]{:S(2)}) copy-start(bf16[2,256,512]{2,1,0:T(8,128)(2,1)} %get-tuple-element.23) | copy-start | bytes 1572868
  119.1 20.3 %copy-start.5 = (bf16[2,256,512]{2,1,0:T(8,128)(2,1)S(1)}, bf16[2,256,512]{2,1,0:T(8,128)(2,1)}, u32[]{:S(2)}) copy-start(bf16[2,256,512]{2,1,0:T(8,128)(2,1)} %get-tuple-element.27) | copy-start | bytes 1572868

commit v9 on v8

--- a/solution.py
+++ b/solution.py
@@ -25,18 +25,23 @@
     return lax.ppermute(block, axis, [(i, i ^ 1) for i in range(lax.axis_size(axis))])
 
 
-def attention_kernel(bias_ref, q_ref, g_ref, p4_ref, p3_ref, p2_ref, p1_ref, p0_ref, *refs):
+def attention_kernel(qd_ref, kd_ref, q_ref, g_ref, p4_ref, p3_ref, p2_ref, p1_ref, p0_ref, *refs):
     o_ref, dq_ref, d13_ref, d4_ref, d2_ref, d0_ref = refs[-6:]
     rows = q_ref.shape[0]
     head_size = p0_ref.shape[2]
     pieces = (p4_ref, p3_ref, p2_ref, p1_ref, p0_ref)
+    cols = rows * len(pieces)
+    q_pos = lax.broadcasted_iota(jnp.int32, (rows, cols), 0)
+    k_pos = lax.broadcasted_iota(jnp.int32, (rows, cols), 1)
+    allowed = (qd_ref[...] == kd_ref[...]) & (k_pos > q_pos) & (k_pos <= q_pos + WINDOW)
     k = jnp.concatenate([p[0] for p in pieces], axis=0)
     v = jnp.concatenate([p[1] for p in pieces], axis=0)
     heads = q_ref.shape[1] // head_size
     q = jnp.concatenate([q_ref[:, a * head_size:(a + 1) * head_size] for a in range(heads)], 0)
     g = jnp.concatenate([g_ref[:, a * head_size:(a + 1) * head_size] for a in range(heads)], 0)
+    allowed = jnp.concatenate([allowed] * heads, 0)
     scores = QUERY_SCALE * lax.dot_general(q, k, NT, preferred_element_type=jnp.float32)
-    masked = scores + bias_ref[...]
+    masked = jnp.where(allowed, scores, -jnp.inf)
     row_max = jnp.max(masked, axis=1, keepdims=True)
     unnorm = jnp.exp(masked - row_max)
     inv = 1.0 / jnp.sum(unnorm, axis=1, keepdims=True)
@@ -60,7 +65,7 @@
         d0_ref[j] = term[4 * rows:5 * rows]
 
 
-def attention(q2, g2, pieces, bias, head_size, chunk, bufs):
+def attention(q2, g2, pieces, q_docs, k_docs, head_size, chunk, bufs):
     rows = q2.shape[0]
     pieces, blocks = zip(*pieces)
     groups = pieces[0].shape[2] // head_size
@@ -76,7 +81,8 @@
         attention_kernel,
         grid=(groups,),
         in_specs=[
-            pl.BlockSpec(bias.shape, lambda i: (0, 0)),
+            pl.BlockSpec((rows, 1), lambda i: (0, 0)),
+            pl.BlockSpec((1, cols), lambda i: (0, 0)),
             q_spec,
             q_spec,
         ] + [pl.BlockSpec((2, rows, head_size), lambda i, b=b: (0, b, i)) for b in blocks]
@@ -90,12 +96,13 @@
             piece_shape,
             piece_shape,
         ],
-        input_output_aliases={3 + len(pieces) + j: j for j in range(len(bufs))},
-        compiler_params=pltpu.CompilerParams(dimension_semantics=("arbitrary",)),
+        input_output_aliases={4 + len(pieces) + j: j for j in range(len(bufs))},
+        compiler_params=pltpu.CompilerParams(
+            dimension_semantics=("arbitrary",)),
         cost_estimate=pl.CostEstimate(
             flops=flops, transcendentals=rows * cols * per_group * groups // head_size,
             bytes_accessed=bytes_accessed),
-    )(bias, q2, g2, *pieces, *bufs)
+    )(q_docs, k_docs, q2, g2, *pieces, *bufs)
 
 
 def wide(x):
@@ -126,7 +133,6 @@
 
 def staged(query_heads, key_heads, value_heads, grad_out, doc_ids):
     row_count = query_heads.shape[0]
-    groups = key_heads.shape[1]
     head_size = key_heads.shape[2]
     assert WINDOW // row_count == 4
     piece_pos = lax.axis_index("ctx")
@@ -136,12 +142,6 @@
     first_row = piece_pos * row_count
     q_docs = lax.dynamic_slice_in_dim(doc_ids, first_row, row_count, 0).reshape(row_count, 1)
     k_docs = lax.dynamic_slice_in_dim(pad_docs, first_row, WINDOW + row_count, 0).reshape(1, -1)
-    cols = k_docs.shape[1]
-    q_pos = lax.broadcasted_iota(jnp.int32, (row_count, cols), 0)
-    k_pos = lax.broadcasted_iota(jnp.int32, (row_count, cols), 1)
-    allowed = (q_docs == k_docs) & (k_pos > q_pos) & (k_pos <= q_pos + WINDOW)
-    bias = jnp.where(allowed, 0.0, -jnp.inf).astype(jnp.float32)
-    bias = jnp.concatenate([bias] * (query_heads.shape[1] // groups), 0)
     q2 = query_heads.reshape(row_count, -1)
     g2 = grad_out.reshape(row_count, -1)
     k2 = key_heads.reshape(row_count, -1)
@@ -154,7 +154,7 @@
         own = jnp.stack([k2[:, lanes], v2[:, lanes]])
         pieces = forward_exchange(own, is_odd)
         o_buf, dq_buf, *terms = attention(
-            q2, g2, pieces, bias, head_size, c, bufs)
+            q2, g2, pieces, q_docs, k_docs, head_size, c, bufs)
         bufs = (o_buf, dq_buf)
         totals.append(backward_exchange(terms, is_odd))
     attended = o_buf.reshape(query_heads.shape)

time: 144 us -> 142 us (0.986)
  other arithmetic: 7.85 us -> 4.6 us
  local copies, waits for them, and re-layouts: 10.1 us -> 12.4 us
  Pallas kernels: 30.7 us -> 29.2 us
    concatenate x1 -> x0, other arithmetic: 1.71 us -> none  [staged(): bias = jnp.concatenate([bias] * (query_heads.shape[1] // groups), 0)]
    reshape x1, local copies, waits for them, and re-layouts: 1.82 us -> 3.36 us  [staged(): g2 = grad_out.reshape(row_count, -1)]
    pallas_call x2, Pallas kernels: 30.7 us -> 29.2 us  [attention(): pl.pallas_call(attention_kernel, grid=(groups,), in_specs=[pl.BlockSpec((...]
    unnamed x39 -> x35, local copies, waits for them, and re-layouts: 8.01 us -> 7.43 us
  transfers between devices with their start and end apart: 12 -> 12, of which waited for: 9 -> 9; matrix products, arithmetic and copies ran while one was open for 8% -> 8% of each run, Pallas kernels for 22% -> 21%
where the time goes in v9:
time: 142 us; the launch traced here: 140 us
  waiting for transfers between devices  79.5 us (56%)
  Pallas kernels  29.2 us (21%)
  starting transfers between devices  13 us (9%)
  local copies, waits for them, and re-layouts  12.4 us (9%)
  other arithmetic  4.6 us (3%)
    ppermute x8, waiting for transfers between devices, shift(): lax.ppermute(block, axis, [(i, (i + distance) % size) for i in range(size)])  76.9 us
    pallas_call x2, Pallas kernels, attention(): pl.pallas_call(attention_kernel, grid=(groups,), in_specs=[pl.BlockSpec((...  29.2 us
    ppermute x8, starting transfers between devices, shift(): lax.ppermute(block, axis, [(i, (i + distance) % size) for i in range(size)])  11.9 us
    unnamed x35, local copies, waits for them, and re-layouts  7.43 us
    reshape x1, local copies, waits for them, and re-layouts, staged(): g2 = grad_out.reshape(row_count, -1)  3.36 us
    select_n x2, other arithmetic, forward_exchange(): jnp.where(is_odd, jnp.concatenate([back2, back4], 1), jnp.concatenate([ow...  3.03 us
  transfers between devices with their start and end apart: 12, of which 9 were waited for; matrix products, arithmetic and copies ran while one was open for 8% of the time, Pallas kernels for 21%

profile of v9, /device:TPU:100, one launch (start us, length us, event | category | flops | bytes accessed | tf_op | source)
XLA Modules:
  0.0 139.6 jit_solution(12433225872836525060)
XLA Ops:
  0.6 1.2 copy.25
  2.1 3.2 %collective-permute-start.3 = (bf16[2,256,512]{2,1,0:T(8,128)(2,1)S(1)}, bf16[2,256,512]{2,1,0:T(8,128)(2,1)S(1)}, u32[]{:S(2)}, u32[]{:S(2)}) collective-permute-start(bf16[2,256,512]{2,1,0:T(8,128)(2,1)S(1)} %pad_maximum_fusion.1.p0_ref), channel_id=1, source_target_pairs={{0,2},{1,3},{2,4},{3,5},{4,6},{5,7},{6,8},{7,9},{8,10},{9,11},{10,... | collective-permute-start | bytes 1572872 | tf_op jit(solution)/shard_map/ppermute | solution.py:21
  5.4 0.8 copy-done.5
  6.2 1.0 collective-permute-start
  7.2 10.4 %collective-permute-done.3.p2_ref = bf16[2,256,512]{2,1,0:T(8,128)(2,1)S(1)} collective-permute-done((bf16[2,256,512]{2,1,0:T(8,128)(2,1)S(1)}, bf16[2,256,512]{2,1,0:T(8,128)(2,1)S(1)}, u32[]{:S(2)}, u32[]{:S(2)}) %collective-permute-start.3) | collective-permute-done | bytes 524320 | tf_op jit(solution)/shard_map/ppermute | solution.py:21
  17.6 3.7 %collective-permute-start.4 = (bf16[2,256,512]{2,1,0:T(8,128)(2,1)S(1)}, bf16[2,256,512]{2,1,0:T(8,128)(2,1)}, u32[]{:S(2)}, u32[]{:S(2)}) collective-permute-start(bf16[2,256,512]{2,1,0:T(8,128)(2,1)S(1)} %collective-permute-done.3.p2_ref), channel_id=1, source_target_pairs={{0,2},{1,3},{2,4},{3,5},{4,6},{5,7},{6,8},{7,9},{8,10},{9,11},{10,... | collective-permute-start | bytes 1572872 | tf_op jit(solution)/shard_map/ppermute | solution.py:21
  21.3 7.5 %collective-permute-done.p2_ref = bf16[2,256,512]{2,1,0:T(8,128)(2,1)S(1)} collective-permute-done((bf16[2,256,512]{2,1,0:T(8,128)(2,1)S(1)}, bf16[2,256,512]{2,1,0:T(8,128)(2,1)S(1)}, u32[]{:S(2)}, u32[]{:S(2)}) %collective-permute-start) | collective-permute-done | bytes 524320 | tf_op jit(solution)/shard_map/ppermute | solution.py:21
  28.9 3.7 %collective-permute-start.1 = (bf16[2,256,512]{2,1,0:T(8,128)(2,1)S(1)}, bf16[2,256,512]{2,1,0:T(8,128)(2,1)}, u32[]{:S(2)}, u32[]{:S(2)}) collective-permute-start(bf16[2,256,512]{2,1,0:T(8,128)(2,1)S(1)} %collective-permute-done.p2_ref), channel_id=1, source_target_pairs={{0,2},{1,3},{2,4},{3,5},{4,6},{5,7},{6,8},{7,9},{8,10},{9,11},{10,... | collective-permute-start | bytes 1572872 | tf_op jit(solution)/shard_map/ppermute | solution.py:21
  32.6 7.5 %collective-permute-done.4.p4_ref = bf16[2,256,512]{2,1,0:T(8,128)(2,1)} collective-permute-done((bf16[2,256,512]{2,1,0:T(8,128)(2,1)S(1)}, bf16[2,256,512]{2,1,0:T(8,128)(2,1)}, u32[]{:S(2)}, u32[]{:S(2)}) %collective-permute-start.4) | collective-permute-done | bytes 524320 | tf_op jit(solution)/shard_map/ppermute | solution.py:21
  40.1 1.4 maximum_select_fusion.1
  41.6 8.6 %collective-permute-done.1.p4_ref = bf16[2,256,512]{2,1,0:T(8,128)(2,1)} collective-permute-done((bf16[2,256,512]{2,1,0:T(8,128)(2,1)S(1)}, bf16[2,256,512]{2,1,0:T(8,128)(2,1)}, u32[]{:S(2)}, u32[]{:S(2)}) %collective-permute-start.1) | collective-permute-done | bytes 524320 | tf_op jit(solution)/shard_map/ppermute | solution.py:21
  50.2 1.6 %maximum_select_fusion = bf16[2,512,512]{2,1,0:T(8,128)(2,1)S(1)} fusion(bf16[2,256,512]{2,1,0:T(8,128)(2,1)} %collective-permute-done.1.p4_ref, bf16[2,256,512]{2,1,0:T(8,128)(2,1)} %copy-done.9, bf16[1,256,512]{2,1,0:T(8,128)(2,1)S(1)} %get-tuple-element.33, bf16[1,256,512]{2,1,0:T(8,128)(2,1)S(1)} %get-tuple-element.34, pred[]{:T(512)S(6)} %eq.5), kind=kLoop, calls=%fused_computation.7 | loop fusion | flops 5767168 | bytes 2621441 | tf_op jit(solution)/shard_map/jit(_where)/select_n | solution.py:115
  52.0 0.8 copy.12.qd_ref
  52.9 0.6 reshape.39.kd_ref
  53.5 3.4 %copy_bitcast_fusion = (bf16[256,2048]{1,0:T(8,128)(2,1)}, bf16[256,2048]{1,0:T(8,128)(2,1)}) fusion(bf16[32,8,16,128]{3,2,1,0:T(8,128)(2,1)} %bitcast.41, bf16[32,8,16,128]{3,2,1,0:T(8,128)(2,1)} %bitcast.42), kind=kLoop, calls=%fused_computation.5 | loop fusion | bytes 4194304 | tf_op jit(solution)/shard_map/reshape | solution.py:146
  56.9 14.6 %shard_map.84 = (bf16[256,2048]{1,0:T(8,128)(2,1)}, bf16[256,2048]{1,0:T(8,128)(2,1)}, bf16[2,512,512]{2,1,0:T(8,128)(2,1)}, bf16[2,256,512]{2,1,0:T(8,128)(2,1)...) custom-call(s32[256,1]{1,0:T(8,128)} %copy.12.qd_ref, s32[1,1280]{1,0:T(1,128)} %reshape.39.kd_ref, ...), custom_call_target="tpu_custom_call" | custom-call | flops 4026531840 | bytes 7340032 | tf_op jit(solution)/shard_map/pallas_call | solution.py:80
  71.5 0.7 collective-permute-start.6
  72.2 14.6 %shard_map.85 = (bf16[256,2048]{1,0:T(8,128)(2,1)}, bf16[256,2048]{1,0:T(8,128)(2,1)}, bf16[2,512,512]{2,1,0:T(8,128)(2,1)}, bf16[2,256,512]{2,1,0:T(8,128)(2,1)...) custom-call(s32[256,1]{1,0:T(8,128)} %copy.12.qd_ref, ...), custom_call_target="tpu_custom_call", output_to_operand_aliasing={{0}: (9, {}), {1}: (10, {})} | custom-call | flops 4026531840 | bytes 7340032 | tf_op jit(solution)/shard_map/pallas_call | solution.py:80
  87.3 2.6 %collective-permute-done.9 = bf16[2,512,512]{2,1,0:T(8,128)(2,1)S(1)} collective-permute-done((bf16[2,512,512]{2,1,0:T(8,128)(2,1)}, bf16[2,512,512]{2,1,0:T(8,128)(2,1)S(1)}, u32[]{:S(2)}, u32[]{:S(2)}) %collective-permute-start.9) | collective-permute-done | bytes 1048608 | tf_op jit(solution)/shard_map/ppermute | solution.py:25
  90.1 13.8 %collective-permute-done.7 = bf16[2,256,512]{2,1,0:T(8,128)(2,1)S(1)} collective-permute-done((bf16[2,256,512]{2,1,0:T(8,128)(2,1)S(1)}, bf16[2,256,512]{2,1,0:T(8,128)(2,1)S(1)}, u32[]{:S(2)}, u32[]{:S(2)}) %collective-permute-start.7) | collective-permute-done | bytes 524320 | tf_op jit(solution)/shard_map/ppermute | solution.py:21
  103.8 0.3 add_convert_fusion.1
  104.2 10.9 %collective-permute-done.10 = bf16[2,256,512]{2,1,0:T(8,128)(2,1)S(1)} collective-permute-done((bf16[2,256,512]{2,1,0:T(8,128)(2,1)S(1)}, bf16[2,256,512]{2,1,0:T(8,128)(2,1)S(1)}, u32[]{:S(2)}, u32[]{:S(2)}) %collective-permute-start.10) | collective-permute-done | bytes 524320 | tf_op jit(solution)/shard_map/ppermute | solution.py:21
  115.1 0.3 add_convert_fusion
  115.4 0.9 copy-done
  116.3 1.2 copy.17
  117.7 1.2 copy.18
  118.9 7.4 %collective-permute-done.8 = bf16[2,256,512]{2,1,0:T(8,128)(2,1)S(1)} collective-permute-done((bf16[2,256,512]{2,1,0:T(8,128)(2,1)S(1)}, bf16[2,256,512]{2,1,0:T(8,128)(2,1)S(1)}, u32[]{:S(2)}, u32[]{:S(2)}) %collective-permute-start.8) | collective-permute-done | bytes 524320 | tf_op jit(solution)/shard_map/ppermute | solution.py:21
  126.3 0.2 select_add_fusion.1
  126.5 10.8 %collective-permute-done.11 = bf16[2,256,512]{2,1,0:T(8,128)(2,1)S(1)} collective-permute-done((bf16[2,256,512]{2,1,0:T(8,128)(2,1)S(1)}, bf16[2,256,512]{2,1,0:T(8,128)(2,1)S(1)}, u32[]{:S(2)}, u32[]{:S(2)}) %collective-permute-start.11) | collective-permute-done | bytes 524320 | tf_op jit(solution)/shard_map/ppermute | solution.py:21
  137.3 0.2 select_add_fusion
  137.8 0.9 copy.19
  138.7 0.9 copy.20
  (46 shorter events, 1.9 us)
Async XLA Ops:
  0.6 1.2 copy-start.4
  2.1 26.8 %copy-start.6 = (bf16[2,256,512]{2,1,0:T(8,128)(2,1)}, bf16[2,256,512]{2,1,0:T(8,128)(2,1)S(1)}, u32[]{:S(2)}) copy-start(bf16[2,256,512]{2,1,0:T(8,128)(2,1)S(1)} %pad_maximum_fusion.1.p0_ref) | copy-start | bytes 1572868
  2.1 15.5 %collective-permute-start.3 = (bf16[2,256,512]{2,1,0:T(8,128)(2,1)S(1)}, bf16[2,256,512]{2,1,0:T(8,128)(2,1)S(1)}, u32[]{:S(2)}, u32[]{:S(2)}) collective-permute-start(bf16[2,256,512]{2,1,0:T(8,128)(2,1)S(1)} %pad_maximum_fusion.1.p0_ref), channel_id=1, source_target_pairs={{0,2},{1,3},{2,4},{3,5},{4,6},{5,7},{6,8},{7,9},{8,10},{9,11},{10,... | collective-permute-start | bytes 1572872 | tf_op jit(solution)/shard_map/ppermute | solution.py:21
  5.4 0.8 copy-start.5
  6.2 22.7 %collective-permute-start = (bf16[2,256,512]{2,1,0:T(8,128)(2,1)S(1)}, bf16[2,256,512]{2,1,0:T(8,128)(2,1)S(1)}, u32[]{:S(2)}, u32[]{:S(2)}) collective-permute-start(bf16[2,256,512]{2,1,0:T(8,128)(2,1)S(1)} %pad_maximum_fusion.p0_ref), channel_id=1, source_target_pairs={{0,2},{1,3},{2,4},{3,5},{4,6},{5,7},{6,8},{7,9},{8,10},{9,11},{10,... | collective-permute-start | bytes 1572872 | tf_op jit(solution)/shard_map/ppermute | solution.py:21
  17.6 23.9 %copy-start.10 = (bf16[2,256,512]{2,1,0:T(8,128)(2,1)}, bf16[2,256,512]{2,1,0:T(8,128)(2,1)S(1)}, u32[]{:S(2)}) copy-start(bf16[2,256,512]{2,1,0:T(8,128)(2,1)S(1)} %collective-permute-done.3.p2_ref) | copy-start | bytes 1572868
  17.6 22.5 %collective-permute-start.4 = (bf16[2,256,512]{2,1,0:T(8,128)(2,1)S(1)}, bf16[2,256,512]{2,1,0:T(8,128)(2,1)}, u32[]{:S(2)}, u32[]{:S(2)}) collective-permute-start(bf16[2,256,512]{2,1,0:T(8,128)(2,1)S(1)} %collective-permute-done.3.p2_ref), channel_id=1, source_target_pairs={{0,2},{1,3},{2,4},{3,5},{4,6},{5,7},{6,8},{7,9},{8,10},{9,11},{10,... | collective-permute-start | bytes 1572872 | tf_op jit(solution)/shard_map/ppermute | solution.py:21
  28.9 12.6 %copy-start.9 = (bf16[2,256,512]{2,1,0:T(8,128)(2,1)}, bf16[2,256,512]{2,1,0:T(8,128)(2,1)S(1)}, u32[]{:S(2)}) copy-start(bf16[2,256,512]{2,1,0:T(8,128)(2,1)S(1)} %collective-permute-done.p2_ref) | copy-start | bytes 1572868
  28.9 21.3 %collective-permute-start.1 = (bf16[2,256,512]{2,1,0:T(8,128)(2,1)S(1)}, bf16[2,256,512]{2,1,0:T(8,128)(2,1)}, u32[]{:S(2)}, u32[]{:S(2)}) collective-permute-start(bf16[2,256,512]{2,1,0:T(8,128)(2,1)S(1)} %collective-permute-done.p2_ref), channel_id=1, source_target_pairs={{0,2},{1,3},{2,4},{3,5},{4,6},{5,7},{6,8},{7,9},{8,10},{9,11},{10,... | collective-permute-start | bytes 1572872 | tf_op jit(solution)/shard_map/ppermute | solution.py:21
  41.5 10.4 %copy-start.13 = (s32[4096]{0:T(1024)S(1)}, s32[4096]{0:T(1024)}, u32[]{:S(2)}) copy-start(s32[4096]{0:T(1024)} %param.9) | copy-start | bytes 49156
  41.5 15.4 %collective-permute-start.5 = (bf16[2,512,512]{2,1,0:T(8,128)(2,1)S(1)}, bf16[2,512,512]{2,1,0:T(8,128)(2,1)}, u32[]{:S(2)}, u32[]{:S(2)}) collective-permute-start(bf16[2,512,512]{2,1,0:T(8,128)(2,1)S(1)} %maximum_select_fusion.1), channel_id=1, source_target_pairs={{0,1},{1,0},{2,3},{3,2},{4,5},{5,4},{6,7},{7,6},{8,9},{9,8},{10,11... | collective-permute-start | bytes 3145736 | tf_op jit(solution)/shard_map/ppermute | solution.py:25
  51.9 20.4 %collective-permute-start.2 = (bf16[2,512,512]{2,1,0:T(8,128)(2,1)S(1)}, bf16[2,512,512]{2,1,0:T(8,128)(2,1)}, u32[]{:S(2)}, u32[]{:S(2)}) collective-permute-start(bf16[2,512,512]{2,1,0:T(8,128)(2,1)S(1)} %maximum_select_fusion), channel_id=1, source_target_pairs={{0,1},{1,0},{2,3},{3,2},{4,5},{5,4},{6,7},{7,6},{8,9},{9,8},{10,11... | collective-permute-start | bytes 3145736 | tf_op jit(solution)/shard_map/ppermute | solution.py:25
  71.5 15.5 %collective-permute-start.6 = (bf16[2,512,512]{2,1,0:T(8,128)(2,1)}, bf16[2,512,512]{2,1,0:T(8,128)(2,1)S(1)}, u32[]{:S(2)}, u32[]{:S(2)}) collective-permute-start(bf16[2,512,512]{2,1,0:T(8,128)(2,1)} %get-tuple-element.21), channel_id=1, source_target_pairs={{0,1},{1,0},{2,3},{3,2},{4,5},{5,4},{6,7},{7,6},{8,9},{9,8},{10,11... | collective-permute-start | bytes 3145736 | tf_op jit(solution)/shard_map/ppermute | solution.py:25
  72.2 14.8 %copy-start.7 = (bf16[2,256,512]{2,1,0:T(8,128)(2,1)S(1)}, bf16[2,256,512]{2,1,0:T(8,128)(2,1)}, u32[]{:S(2)}) copy-start(bf16[2,256,512]{2,1,0:T(8,128)(2,1)} %get-tuple-element.20) | copy-start | bytes 1572868
  86.9 3.0 %copy-start.8 = (bf16[2,256,512]{2,1,0:T(8,128)(2,1)S(1)}, bf16[2,256,512]{2,1,0:T(8,128)(2,1)}, u32[]{:S(2)}) copy-start(bf16[2,256,512]{2,1,0:T(8,128)(2,1)} %get-tuple-element.24) | copy-start | bytes 1572868
  86.9 3.0 %collective-permute-start.9 = (bf16[2,512,512]{2,1,0:T(8,128)(2,1)}, bf16[2,512,512]{2,1,0:T(8,128)(2,1)S(1)}, u32[]{:S(2)}, u32[]{:S(2)}) collective-permute-start(bf16[2,512,512]{2,1,0:T(8,128)(2,1)} %get-tuple-element.25), channel_id=1, source_target_pairs={{0,1},{1,0},{2,3},{3,2},{4,5},{5,4},{6,7},{7,6},{8,9},{9,8},{10,11... | collective-permute-start | bytes 3145736 | tf_op jit(solution)/shard_map/ppermute | solution.py:25
  87.2 16.7 %copy-start.11 = (bf16[2,256,512]{2,1,0:T(8,128)(2,1)S(1)}, bf16[2,256,512]{2,1,0:T(8,128)(2,1)}, u32[]{:S(2)}) copy-start(bf16[2,256,512]{2,1,0:T(8,128)(2,1)} %get-tuple-element.22) | copy-start | bytes 1572868
  87.2 16.7 %collective-permute-start.7 = (bf16[2,256,512]{2,1,0:T(8,128)(2,1)S(1)}, bf16[2,256,512]{2,1,0:T(8,128)(2,1)S(1)}, u32[]{:S(2)}, u32[]{:S(2)}) collective-permute-start(bf16[2,256,512]{2,1,0:T(8,128)(2,1)S(1)} %fusion), channel_id=1, source_target_pairs={{0,14},{1,15},{2,0},{3,1},{4,2},{5,3},{6,4},{7,5},{8,6},{9,7},{10,... | collective-permute-start | bytes 1572872 | tf_op jit(solution)/shard_map/ppermute | solution.py:21
  90.0 25.1 %collective-permute-start.10 = (bf16[2,256,512]{2,1,0:T(8,128)(2,1)S(1)}, bf16[2,256,512]{2,1,0:T(8,128)(2,1)S(1)}, u32[]{:S(2)}, u32[]{:S(2)}) collective-permute-start(bf16[2,256,512]{2,1,0:T(8,128)(2,1)S(1)} %fusion.1), channel_id=1, source_target_pairs={{0,14},{1,15},{2,0},{3,1},{4,2},{5,3},{6,4},{7,5},{8,6},{9,7},{10,... | collective-permute-start | bytes 1572872 | tf_op jit(solution)/shard_map/ppermute | solution.py:21
  103.8 11.2 %copy-start.12 = (bf16[2,256,512]{2,1,0:T(8,128)(2,1)S(1)}, bf16[2,256,512]{2,1,0:T(8,128)(2,1)}, u32[]{:S(2)}) copy-start(bf16[2,256,512]{2,1,0:T(8,128)(2,1)} %get-tuple-element.26) | copy-start | bytes 1572868
  104.1 22.2 %collective-permute-start.8 = (bf16[2,256,512]{2,1,0:T(8,128)(2,1)S(1)}, bf16[2,256,512]{2,1,0:T(8,128)(2,1)S(1)}, u32[]{:S(2)}, u32[]{:S(2)}) collective-permute-start(bf16[2,256,512]{2,1,0:T(8,128)(2,1)S(1)} %add_convert_fusion.1), channel_id=1, source_target_pairs={{0,14},{1,15},{2,0},{3,1},{4,2},{5,3},{6,4},{7,5},{8,6},{9,7},{10,... | collective-permute-start | bytes 1572872 | tf_op jit(solution)/shard_map/ppermute | solution.py:21
  115.1 1.2 copy-start
  115.4 22.0 %collective-permute-start.11 = (bf16[2,256,512]{2,1,0:T(8,128)(2,1)S(1)}, bf16[2,256,512]{2,1,0:T(8,128)(2,1)S(1)}, u32[]{:S(2)}, u32[]{:S(2)}) collective-permute-start(bf16[2,256,512]{2,1,0:T(8,128)(2,1)S(1)} %add_convert_fusion), channel_id=1, source_target_pairs={{0,14},{1,15},{2,0},{3,1},{4,2},{5,3},{6,4},{7,5},{8,6},{9,7},{10,... | collective-permute-start | bytes 1572872 | tf_op jit(solution)/shard_map/ppermute | solution.py:21
  116.3 1.4 copy-start.1
  117.7 8.6 %copy-start.2 = (bf16[2,256,512]{2,1,0:T(8,128)(2,1)S(1)}, bf16[2,256,512]{2,1,0:T(8,128)(2,1)}, u32[]{:S(2)}) copy-start(bf16[2,256,512]{2,1,0:T(8,128)(2,1)} %get-tuple-element.23) | copy-start | bytes 1572868
  126.3 11.0 %copy-start.3 = (bf16[2,256,512]{2,1,0:T(8,128)(2,1)S(1)}, bf16[2,256,512]{2,1,0:T(8,128)(2,1)}, u32[]{:S(2)}) copy-start(bf16[2,256,512]{2,1,0:T(8,128)(2,1)} %get-tuple-element.27) | copy-start | bytes 1572868
